TPU v7x, 512 devices: a whole 4x8x8 slice. The times are simulated.
512 devices in a mesh: src: 32 (over y, x_lo, core), rcv: 8 (over z), int: 2 (over x_hi).
Axes of the slice: x: 4 (x_hi: 2, x_lo: 2; x = x_hi * 2 + x_lo), y: 8, z: 8, core: 2. Of those that a mesh axis runs over, the one named last changes fastest.
Arguments:
- traces: float32 [2, 1, 4096, 4096], P(None, None, 'src', 'rcv'), may hold values from -6 to 6
- missing: int32 [32, 32], P('src', 'rcv'), may hold values from 0 to 1, as said below
- aperture: int32 [32, 24], P('src'), may hold values from 0 to 32, as said below
- wavelet: float32 [2, 1], replicated, may hold values from -0.06 to 0.06
Outputs:
- primaries: float32 [2, 1, 4096, 4096], P(None, None, 'src', ('rcv', 'int'))
Inputs may be any that keep to these rules, and one draw needn't show every extreme that they name: `missing`: A tile is marked only where its receiver block lies above its source block, so the mirrored tile is always recorded; some tile is marked. `aperture`: in each row the listed blocks come first and are distinct; the remaining entries are the padding value 32. Each row lists 24 // 2 to 24 blocks; some row lists exactly 24 and some row exactly 12.
All inputs are finite; a program needn't handle non-finite values.
Results may differ from a plain program's by a relative error of at most 0.00005.
Values sent between devices are 32-bit elements; how exact they have to be, the bound alone decides.
No kernel may reach another device: no remote copies, remote signals or barrier semaphores. Data moves between devices by JAX's collectives and lax.ppermute only.
A program may use at most 64 MiB of HBM per device.

v0:
```python
import jax
import jax.numpy as jnp
from jax import lax
from jax.sharding import PartitionSpec as P

TILE = 128


def from_everyone(x, axis):
    copies = jnp.broadcast_to(x, (lax.axis_size(axis), *x.shape))
    return lax.all_to_all(copies, axis, split_axis=0, concat_axis=0, tiled=True)


def joined_along(pieces, dim):
    pieces = jnp.moveaxis(pieces, 0, dim)
    lengths = pieces.shape
    return pieces.reshape(*lengths[:dim], lengths[dim] * lengths[dim + 1], *lengths[dim + 2 :])


def collect(x, axis, dim):
    pieces = from_everyone(x, axis)
    return joined_along(pieces, dim)


def in_blocks(x, dim, count):
    before, after = (x.shape[:dim], x.shape[dim + 1 :])
    return jnp.moveaxis(x.reshape(*before, count, -1, *after), dim, 0)


def sent_and_summed(x, axis, dim):
    pieces = in_blocks(x, dim, lax.axis_size(axis))
    arrived = lax.all_to_all(pieces, axis, split_axis=0, concat_axis=0, tiled=True)
    return arrived.sum(axis=0)


def complex_prod(left_side, right_side):
    return jnp.einsum("fik,fkj->fij", left_side, right_side, precision=lax.Precision.HIGHEST)


def per_device(traces, missing, aperture, wavelet):
    half_count = lax.axis_size("int")
    my_half = lax.axis_index("int")
    rcv_count = lax.axis_size("rcv")
    comp_count, freq_count, local_rows, local_cols = traces.shape
    regrouped = lax.all_to_all(traces, "rcv", split_axis=2, concat_axis=3, tiled=True)
    sectioned = regrouped.reshape(
        comp_count, freq_count, 1, local_rows // rcv_count, local_cols * rcv_count
    )
    arrived = lax.all_to_all(
        lax.all_to_all(sectioned, "src", split_axis=4, concat_axis=2, tiled=True),
        "rcv",
        split_axis=2,
        concat_axis=3,
        tiled=True,
    )
    mirrored = jnp.swapaxes(arrived.reshape(comp_count, freq_count, local_cols, local_rows), 2, 3)
    row_tiles = local_rows // TILE
    col_tiles = local_cols // TILE
    tile_mask = jnp.broadcast_to(
        missing[:, None, :, None] > 0, (row_tiles, TILE, col_tiles, TILE)
    ).reshape(local_rows, local_cols)
    filled = jnp.where(tile_mask[None, None], mirrored, traces)
    half_tile = TILE // half_count
    left_half = filled.reshape(comp_count, freq_count, local_rows, col_tiles, half_count, half_tile)
    left_half = lax.dynamic_index_in_dim(left_half, my_half, 4, keepdims=False)
    left_half = left_half.reshape(comp_count, freq_count, local_rows, col_tiles * half_tile)
    right_half = filled.reshape(
        comp_count, freq_count, row_tiles, half_count, half_tile, local_cols
    )
    right_half = lax.dynamic_index_in_dim(right_half, my_half, 3, keepdims=False)
    right_half = right_half.reshape(comp_count, freq_count, row_tiles * half_tile, local_cols)
    gathered = collect(left_half, "rcv", 3)
    block_count = gathered.shape[3] // half_tile
    chosen = (
        (aperture[:, :, None] == jnp.arange(block_count, dtype=jnp.int32)[None, None, :])
        .astype(jnp.float32)
        .sum(axis=1)
    )
    weighted = gathered.reshape(comp_count, freq_count, row_tiles, TILE, block_count, half_tile)
    weighted = (weighted * chosen[None, None, :, None, :, None]).reshape(
        comp_count, freq_count, local_rows, block_count * half_tile
    )
    slab_piece = lax.all_gather(right_half, "src", axis=2, tiled=True)
    real_part = complex_prod(weighted[0], slab_piece[0]) - complex_prod(weighted[1], slab_piece[1])
    imag_part = complex_prod(weighted[0], slab_piece[1]) + complex_prod(weighted[1], slab_piece[0])
    partial_sum = jnp.stack([real_part, imag_part])
    out_cols = local_cols // half_count
    my_share = sent_and_summed(partial_sum, "int", 3)
    kept_data = filled.reshape(comp_count, freq_count, local_rows, half_count, out_cols)
    kept_data = lax.dynamic_index_in_dim(kept_data, my_half, 3, keepdims=False)
    w_real = wavelet[0][:, None, None]
    w_imag = wavelet[1][:, None, None]
    out_real = kept_data[0] - (w_real * my_share[0] - w_imag * my_share[1])
    out_imag = kept_data[1] - (w_real * my_share[1] + w_imag * my_share[0])
    return jnp.stack([out_real, out_imag])


def solution(mesh):
    placed = (P(None, None, "src", "rcv"), P("src", "rcv"), P("src", None), P())
    return jax.shard_map(
        per_device,
        mesh=mesh,
        in_specs=placed,
        out_specs=P(None, None, "src", ("rcv", "int")),
        check_vma=False,
    )
```

profile of v0, /device:TPU:1, one launch (start us, length us, event | category | flops | bytes accessed | tf_op | source)
XLA Modules:
  0.0 221.6 jit_solution(6146417646936769049)
XLA Ops:
  6.5 1.4 copy.59
  8.0 26.7 %all_to_all.58 = f32[2,1,128,512]{3,0,1,2:T(2,128)S(1)} all-to-all(f32[2,1,128,512]{3,0,1,2:T(2,128)S(1)} %copy.59), channel_id=1, replica_groups=mesh['src'=32,'rcv'=8,'int'=2] {'rcv'}, dimensions={2} | all-to-all | bytes 1048576 | tf_op jit(solution)/shard_map/all_to_all | solution.py:45
  34.6 0.1 copy.60
  34.7 4.3 %copy.73 = f32[2,1,16,8,512]{2,0,4,3,1:T(2,128)} copy(f32[2,1,16,8,512]{4,2,3,0,1:T(8,128)S(1)} %bitcast.68) | data formatting | bytes 1048576 | tf_op jit(solution)/shard_map/reshape | solution.py:46
  39.0 7.3 %reshape.263 = f32[32,1,4096]{2,1,0:T(1,128)S(1)} reshape(f32[4096,1,1,2,16]{4,3,2,1,0:T(2,128)} %bitcast.59) | data formatting | bytes 1048576
  46.4 27.2 %all_to_all.59 = f32[32,1,4096]{2,1,0:T(1,128)S(1)} all-to-all(f32[32,1,4096]{2,1,0:T(1,128)S(1)} %reshape.263), channel_id=1, replica_groups=mesh['src'=32,'rcv'=8,'int'=2] {'src'}, dimensions={0} | all-to-all | bytes 1048576 | tf_op jit(solution)/shard_map/all_to_all | solution.py:50
  73.5 0.5 broadcast.100
  74.0 1.9 reduce.2
  75.9 0.0 copy-start
  75.9 6.9 %reshape.264 = f32[4096,1,1,2,16]{4,3,2,1,0:T(2,128)} reshape(f32[32,4096]{1,0:T(8,128)S(1)} %reduce.2) | data formatting | bytes 1048576
  82.9 0.0 copy-start.2
  82.9 5.9 %copy.63 = f32[2,1,1,16,32,128]{5,3,0,4,2,1:T(8,128)} copy(f32[2,1,1,16,32,128]{3,0,5,4,2,1:T(2,128)} %bitcast.60) | data formatting | bytes 1048576 | tf_op jit(solution)/shard_map/all_to_all | solution.py:50
  88.7 3.5 %all-to-all-start.2 = ((f32[2,1,32,16,128]{4,3,0,1,2:T(8,128)}), f32[2,1,32,16,128]{4,3,0,1,2:T(8,128)S(1)}, u32[]{:S(2)}, u32[]{:S(2)}) async-start(f32[2,1,32,16,128]{4,3,0,1,2:T(8,128)} %bitcast.7), calls=%async_computation.2 | async-start | bytes 1048576 | tf_op jit(solution)/shard_map/all_to_all | solution.py:49
  92.2 0.0 all-gather.3.cloned.1.call-start
  92.3 0.0 copy-done
  92.3 0.2 copy.66
  92.5 0.0 copy-done.2
  92.5 0.1 broadcast_bitcast_fusion
  92.6 15.9 %all-to-all-done.2 = f32[2,1,32,16,128]{4,3,0,1,2:T(8,128)S(1)} async-done(((f32[2,1,32,16,128]{4,3,0,1,2:T(8,128)}), f32[2,1,32,16,128]{4,3,0,1,2:T(8,128)S(1)}, u32[]{:S(2)}, u32[]{:S(2)}) %all-to-all-start.2) | async-done | bytes 524320 | tf_op jit(solution)/shard_map/all_to_all | solution.py:49
  108.6 0.1 bitcast_select_fusion
  108.7 0.2 copy.69
  108.9 0.0 copy-start.3
  108.9 0.7 constant_dynamic-slice_fusion.1
  109.7 0.0 all-gather.3.cloned.1.call-update
  109.7 1.6 broadcast_in_dim.25
  111.3 3.8 %all-to-all-start.3 = ((f32[8,2,1,128,256]{3,4,1,2,0:T(8,128)}), f32[8,2,1,128,256]{3,4,1,2,0:T(8,128)S(1)}, u32[]{:S(2)}, u32[]{:S(2)}) async-start(f32[8,2,1,128,256]{3,4,1,2,0:T(8,128)} %broadcast_in_dim.25), calls=%async_computation.3 | async-start | bytes 4194304 | tf_op jit(solution)/shard_map/all_to_all | solution.py:11
  115.1 0.0 copy-done.3
  115.1 0.1 convert_reduce_fusion
  115.2 48.5 %all-to-all-done.3 = f32[8,2,1,128,256]{3,4,1,2,0:T(8,128)S(1)} async-done(((f32[8,2,1,128,256]{3,4,1,2,0:T(8,128)}), f32[8,2,1,128,256]{3,4,1,2,0:T(8,128)S(1)}, u32[]{:S(2)}, u32[]{:S(2)}) %all-to-all-start.3) | async-done | bytes 2097184 | tf_op jit(solution)/shard_map/all_to_all | solution.py:11
  163.7 0.2 copy.68
  163.9 0.2 broadcast_multiply_fusion
  164.1 0.2 fusion.6
  164.3 14.9 %all-gather.3.cloned.1.call-done = f32[2,1,1,1,2048,512]{5,4,3,0,2,1:T(8,128)} async-done(((f32[2,1,1,1,64,512]{5,4,3,0,2,1:T(8,128)}), f32[2,1,1,1,2048,512]{5,4,3,0,2,1:T(8,128)}) %all-gather.3.cloned.1.call-update) | async-done | bytes 8388624 | tf_op jit(solution)/shard_map/all_gather | solution.py:83
  179.2 4.8 %fusion = f32[128,512]{1,0:T(8,128)S(1)} fusion(f32[128,2048]{0,1:T(8,128)S(1)} %bitcast.61, f32[2,1,1,1,2048,512]{5,4,3,0,2,1:T(8,128)} %all-gather.3.cloned.1.call-done), kind=kOutput, calls=%fused_computation.2 | convolution fusion | flops 1610612736 | bytes 5505024 | tf_op jit(solution)/shard_map/fik,fkj->fij/dot_general | solution.py:37
  184.0 4.8 %fusion.5 = f32[128,512]{1,0:T(8,128)S(1)} fusion(f32[128,512]{1,0:T(8,128)S(1)} %fusion, f32[128,2048]{0,1:T(8,128)S(1)} %bitcast.63, f32[2,1,1,1,2048,512]{5,4,3,0,2,1:T(8,128)} %all-gather.3.cloned.1.call-done), kind=kOutput, calls=%fused_computation.7 | convolution fusion | flops 1610678272 | bytes 5767168 | tf_op jit(solution)/shard_map/fik,fkj->fij/dot_general | solution.py:37
  188.8 0.2 stack.15
  189.0 4.8 %fusion.1 = f32[128,512]{1,0:T(8,128)S(1)} fusion(f32[128,2048]{0,1:T(8,128)S(1)} %bitcast.64, f32[2,1,1,1,2048,512]{5,4,3,0,2,1:T(8,128)} %all-gather.3.cloned.1.call-done), kind=kOutput, calls=%fused_computation.3 | convolution fusion | flops 1610612736 | bytes 5505024 | tf_op jit(solution)/shard_map/fik,fkj->fij/dot_general | solution.py:37
  193.8 0.0 copy-start.1
  193.8 4.8 %fusion.4 = f32[128,512]{1,0:T(8,128)S(1)} fusion(f32[128,512]{1,0:T(8,128)S(1)} %fusion.1, f32[128,2048]{0,1:T(8,128)S(1)} %bitcast.62, f32[2,1,1,1,2048,512]{5,4,3,0,2,1:T(8,128)} %all-gather.3.cloned.1.call-done), kind=kOutput, calls=%fused_computation.6 | convolution fusion | flops 1610678272 | bytes 5767168 | tf_op jit(solution)/shard_map/fik,fkj->fij/dot_general | solution.py:37
  198.6 0.2 stack.14
  198.8 0.8 maximum_bitcast_fusion
  199.6 4.0 %all-to-all-start.4 = ((f32[2,2,1,128,256]{4,3,2,1,0:T(8,128)}), f32[2,2,1,128,256]{4,3,2,1,0:T(8,128)S(1)}, u32[]{:S(2)}, u32[]{:S(2)}) async-start(f32[2,2,1,128,256]{4,3,2,1,0:T(8,128)} %maximum_bitcast_fusion), calls=%async_computation.4 | async-start | bytes 1048576 | tf_op jit(solution)/shard_map/all_to_all | solution.py:32
  203.6 0.0 copy-done.1
  203.6 0.6 fusion.7
  204.3 0.1 copy.77
  204.4 0.1 copy.80
  204.5 8.2 %all-to-all-done.4 = f32[2,2,1,128,256]{4,3,2,1,0:T(8,128)S(1)} async-done(((f32[2,2,1,128,256]{4,3,2,1,0:T(8,128)}), f32[2,2,1,128,256]{4,3,2,1,0:T(8,128)S(1)}, u32[]{:S(2)}, u32[]{:S(2)}) %all-to-all-start.4) | async-done | bytes 524320 | tf_op jit(solution)/shard_map/all_to_all | solution.py:32
  212.7 1.3 bitcast_subtract_fusion.1
  214.0 0.7 pad_maximum_fusion
  (8 shorter events, 0.2 us)
Async XLA Ops:
  75.9 16.3 %copy-start = (f32[2,1,128,512]{3,2,1,0:T(8,128)S(1)}, f32[2,1,128,512]{3,2,1,0:T(8,128)}, u32[]{:S(2)}) copy-start(f32[2,1,128,512]{3,2,1,0:T(8,128)} %param.4) | copy-start | bytes 1572868
  82.9 9.6 %copy-start.2 = (s32[1,4]{1,0:T(1,128)S(1)}, s32[1,4]{1,0:T(1,128)}, u32[]{:S(2)}) copy-start(s32[1,4]{1,0:T(1,128)} %param.5) | copy-start | bytes 52
  88.7 19.8 %all-to-all-start.2 = ((f32[2,1,32,16,128]{4,3,0,1,2:T(8,128)}), f32[2,1,32,16,128]{4,3,0,1,2:T(8,128)S(1)}, u32[]{:S(2)}, u32[]{:S(2)}) async-start(f32[2,1,32,16,128]{4,3,0,1,2:T(8,128)} %bitcast.7), calls=%async_computation.2 | async-start | bytes 1048576 | tf_op jit(solution)/shard_map/all_to_all | solution.py:49
  92.2 87.0 %all-gather.3.cloned.1.call-start = ((), (), s32[]{:S(2)}) async-start(), calls=%async_computation.5 | async-start | bytes 8650752 | tf_op jit(solution)/shard_map/all_gather | solution.py:83
  108.9 6.2 %copy-start.3 = (s32[1,24]{1,0:T(1,128)S(1)}, s32[1,24]{1,0:T(1,128)}, u32[]{:S(2)}) copy-start(s32[1,24]{1,0:T(1,128)} %param.6) | copy-start | bytes 292
  111.3 52.4 %all-to-all-start.3 = ((f32[8,2,1,128,256]{3,4,1,2,0:T(8,128)}), f32[8,2,1,128,256]{3,4,1,2,0:T(8,128)S(1)}, u32[]{:S(2)}, u32[]{:S(2)}) async-start(f32[8,2,1,128,256]{3,4,1,2,0:T(8,128)} %broadcast_in_dim.25), calls=%async_computation.3 | async-start | bytes 4194304 | tf_op jit(solution)/shard_map/all_to_all | solution.py:11
  193.8 9.8 %copy-start.1 = (f32[2,1]{0,1:T(1,128)S(1)}, f32[2,1]{0,1:T(1,128)}, u32[]{:S(2)}) copy-start(f32[2,1]{0,1:T(1,128)} %param.7) | copy-start | bytes 28
  199.6 13.0 %all-to-all-start.4 = ((f32[2,2,1,128,256]{4,3,2,1,0:T(8,128)}), f32[2,2,1,128,256]{4,3,2,1,0:T(8,128)S(1)}, u32[]{:S(2)}, u32[]{:S(2)}) async-start(f32[2,2,1,128,256]{4,3,2,1,0:T(8,128)} %maximum_bitcast_fusion), calls=%async_computation.4 | async-start | bytes 1048576 | tf_op jit(solution)/shard_map/all_to_all | solution.py:32
Sparse Core Ops, SparseCore 0:
  109.8 69.3 all-gather.2
where the time goes:
time: 222 us
  waiting for transfers between devices  87.5 us (39%)
  blocking collectives  53.8 us (24%)
  local copies, waits for them, and re-layouts  30.9 us (14%)
  matrix products  19.2 us (9%)
  between operations  13.7 us (6%)
  starting transfers between devices  11.3 us (5%)
  other arithmetic  5.23 us (2%)
    all_to_all x1, waiting for transfers between devices, from_everyone(): return lax.all_to_all(copies, axis, split_axis=0, concat_axis=0, tiled=True)  48.5 us
    all_to_all x1, blocking collectives, per_device(): lax.all_to_all(sectioned, 'src', split_axis=4, concat_axis=2, tiled=True)  27.2 us
    all_to_all x1, blocking collectives, per_device(): lax.all_to_all(traces, 'rcv', split_axis=2, concat_axis=3, tiled=True)  26.7 us
    dot_general x4, matrix products, complex_prod(): jnp.einsum('fik,fkj->fij', left_side, right_side, precision=lax.Precision...  19.2 us
    unnamed x14, local copies, waits for them, and re-layouts  16.1 us
    all_to_all x1, waiting for transfers between devices, per_device(): lax.all_to_all(lax.all_to_all(sectioned, 'src', split_axis=4, concat_axis...  15.9 us
    all_gather x1, waiting for transfers between devices, per_device(): slab_piece = lax.all_gather(right_half, 'src', axis=2, tiled=True)  14.9 us
    all_to_all x1, waiting for transfers between devices, sent_and_summed(): lax.all_to_all(pieces, axis, split_axis=0, concat_axis=0, tiled=True)  8.19 us
  transfers between devices with their start and end apart: 4, of which 4 were waited for; matrix products, arithmetic and copies ran while one was open for 2% of the time, Pallas kernels for 0%

commit v1 on v0

v1 whole, which is shorter than its diff:
```python
import jax
import jax.numpy as jnp
import numpy as np
from jax import lax
from jax.sharding import Mesh
from jax.sharding import PartitionSpec as P

TILE = 128
SRC = ("y", "xl", "c")
FILL = ("y", "xl", "c", "z")


def mirror_pairs(n_src, n_rcv, per_rcv, step):
    pairs = []
    for s in range(n_src):
        for r in range(n_rcv):
            t = (s % per_rcv + step) % per_rcv
            dest_s = per_rcv * r + t
            if s > dest_s:
                pairs.append((s * n_rcv + r, dest_s * n_rcv + s // per_rcv))
    return pairs


def per_device(traces, missing, aperture, wavelet):
    n_src = lax.axis_size(SRC)
    n_rcv = lax.axis_size("z")
    n_half = lax.axis_size("xh")
    n_core = lax.axis_size("c")
    me_src = lax.axis_index(SRC)
    me_rcv = lax.axis_index("z")
    my_half = lax.axis_index("xh")
    comp_count, freq_count, local_rows, local_cols = traces.shape
    assert local_rows == TILE
    per_rcv = local_cols // TILE
    tiles = traces.reshape(comp_count, freq_count, TILE, per_rcv, TILE)

    arrived = []
    for step in range(per_rcv):
        pick = (me_src % per_rcv + step) % per_rcv
        sent = lax.dynamic_index_in_dim(tiles, pick, 3, keepdims=False)
        got = lax.ppermute(sent, FILL, mirror_pairs(n_src, n_rcv, per_rcv, step))
        arrived.append(jnp.swapaxes(got, 2, 3))
    arrived = jnp.stack(arrived, axis=3)
    order = (me_src % per_rcv - jnp.arange(per_rcv)) % per_rcv
    mirrored = jnp.take(arrived, order, axis=3)
    marks = (missing[0] > 0)[None, None, None, :, None]
    filled = jnp.where(marks, mirrored, tiles)

    first = me_rcv * per_rcv
    local_blocks = first + jnp.arange(per_rcv, dtype=jnp.int32)
    chosen = (aperture[0][:, None] == local_blocks[None, :]).astype(jnp.float32).sum(axis=0)

    half = TILE // n_half
    left = filled.reshape(comp_count, freq_count, TILE, per_rcv, n_half, half)
    left = lax.dynamic_index_in_dim(left, my_half, 4, keepdims=False)
    left = left * chosen[None, None, None, :, None]
    left = left.reshape(comp_count, freq_count, TILE, per_rcv * half)
    left = lax.all_gather(left, "z", axis=3, tiled=True)
    n_pair = n_src // n_core
    left = left.reshape(comp_count, freq_count, TILE, n_pair, n_core, half)
    left = jnp.transpose(left, (1, 0, 2, 4, 3, 5))
    left = left.reshape(freq_count, comp_count * TILE, n_src * half)

    right = filled.reshape(comp_count, freq_count, n_half, half, local_cols)
    right = lax.dynamic_index_in_dim(right, my_half, 2, keepdims=False)
    right = jnp.transpose(right, (1, 2, 0, 3))
    right = lax.all_gather(right, ("y", "xl"), axis=1, tiled=True)
    right = lax.all_gather(right, "c", axis=1, tiled=False)
    right = right.reshape(freq_count, n_src * half, comp_count * local_cols)

    prod = jnp.einsum("fak,fkb->fab", left, right, precision=lax.Precision.HIGHEST)
    prod = prod.reshape(freq_count, comp_count, TILE, comp_count, local_cols)
    real_part = prod[:, 0, :, 0] - prod[:, 1, :, 1]
    imag_part = prod[:, 0, :, 1] + prod[:, 1, :, 0]
    partial_sum = jnp.stack([real_part, imag_part])
    my_share = lax.psum_scatter(partial_sum, "xh", scatter_dimension=3, tiled=True)

    out_cols = local_cols // n_half
    kept = filled.reshape(comp_count, freq_count, TILE, local_cols)
    kept = lax.dynamic_slice_in_dim(kept, my_half * out_cols, out_cols, axis=3)
    w_real = wavelet[0][:, None, None]
    w_imag = wavelet[1][:, None, None]
    out_real = kept[0] - (w_real * my_share[0] - w_imag * my_share[1])
    out_imag = kept[1] - (w_real * my_share[1] + w_imag * my_share[0])
    return jnp.stack([out_real, out_imag])


def solution(mesh):
    n_src, n_rcv, n_int = (mesh.shape[a] for a in ("src", "rcv", "int"))
    fine = Mesh(
        np.asarray(mesh.devices).reshape(n_src // 4, 2, 2, n_rcv, n_int),
        ("y", "xl", "c", "z", "xh"),
    )
    placed = (P(None, None, SRC, "z"), P(SRC, "z"), P(SRC, None), P())
    return jax.shard_map(
        per_device,
        mesh=fine,
        in_specs=placed,
        out_specs=P(None, None, SRC, ("z", "xh")),
        check_vma=False,
    )
```

time: 222 us -> 326 us (1.47)
  waiting for transfers between devices: 87.5 us -> 241 us
  blocking collectives: 53.8 us -> 0 us
  local copies, waits for them, and re-layouts: 30.9 us -> 35.6 us
  matrix products: 19.2 us -> 15.8 us
    all_gather x1 -> x3, waiting for transfers between devices: 14.9 us -> 214 us  [the longest x1 139 us: per_device(): right = lax.all_gather(right, ('y', 'xl'), axis=1, tiled=True)]
    all_to_all x3 -> x0, waiting for transfers between devices: 72.6 us -> none  [the longest x1 48.5 us: from_everyone(): return lax.all_to_all(copies, axis, split_axis=0, concat_axis=0, tiled=True)]
    all_to_all x2 -> x0, blocking collectives: 53.8 us -> none  [the longest x1 27.2 us: per_device(): lax.all_to_all(sectioned, 'src', split_axis=4, concat_axis=2, tiled=True)]
    reduce_scatter x0 -> x1, waiting for transfers between devices: none -> 22.8 us  [per_device(): lax.psum_scatter(partial_sum, 'xh', scatter_dimension=3, tiled=True)]
    all_gather x0 -> x1, local copies, waits for them, and re-layouts: none -> 14.4 us  [per_device(): right = lax.all_gather(right, 'c', axis=1, tiled=False)]
    ppermute x0 -> x4, starting transfers between devices: none -> 11.4 us  [per_device(): got = lax.ppermute(sent, FILL, mirror_pairs(n_src, n_rcv, per_rcv, step))]
    all_to_all x3 -> x0, starting transfers between devices: 11.3 us -> none  [the longest x1 3.98 us: sent_and_summed(): lax.all_to_all(pieces, axis, split_axis=0, concat_axis=0, tiled=True)]
    unnamed x14 -> x12, local copies, waits for them, and re-layouts: 16.1 us -> 5.9 us
  transfers between devices with their start and end apart: 4 -> 8, of which waited for: 4 -> 5; matrix products, arithmetic and copies ran while one was open for 2% -> 2% of each run, Pallas kernels for 0% -> 0%
where the time goes in v1:
time: 326 us; the launch traced here: 325 us
  waiting for transfers between devices  241 us (74%)
  local copies, waits for them, and re-layouts  35.6 us (11%)
  matrix products  15.8 us (5%)
  between operations  13.4 us (4%)
  starting transfers between devices  11.7 us (4%)
  other arithmetic  7.52 us (2%)
    all_gather x1, waiting for transfers between devices, per_device(): right = lax.all_gather(right, ('y', 'xl'), axis=1, tiled=True)  139 us
    all_gather x1, waiting for transfers between devices, per_device(): left = lax.all_gather(left, 'z', axis=3, tiled=True)  43.9 us
    all_gather x1, waiting for transfers between devices, per_device(): right = lax.all_gather(right, 'c', axis=1, tiled=False)  32 us
    reduce_scatter x1, waiting for transfers between devices, per_device(): lax.psum_scatter(partial_sum, 'xh', scatter_dimension=3, tiled=True)  22.8 us
    dot_general x1, matrix products, per_device(): jnp.einsum('fak,fkb->fab', left, right, precision=lax.Precision.HIGHEST)  15.8 us
    all_gather x1, local copies, waits for them, and re-layouts, per_device(): right = lax.all_gather(right, 'c', axis=1, tiled=False)  14.4 us
    ppermute x4, starting transfers between devices, per_device(): got = lax.ppermute(sent, FILL, mirror_pairs(n_src, n_rcv, per_rcv, step))  11.4 us
    dot_general x1, local copies, waits for them, and re-layouts, per_device(): jnp.einsum('fak,fkb->fab', left, right, precision=lax.Precision.HIGHEST)  9.22 us
  transfers between devices with their start and end apart: 8, of which 5 were waited for; matrix products, arithmetic and copies ran while one was open for 2% of the time, Pallas kernels for 0%

profile of v1, /device:TPU:1, one launch (start us, length us, event | category | flops | bytes accessed | tf_op | source)
XLA Modules:
  0.0 325.5 jit_solution(12362574936343730955)
XLA Ops:
  6.5 0.0 copy-start
  6.5 0.0 copy-start.2
  6.5 0.0 all-gather.7.cloned.1.call-start
  6.5 1.3 reshape.249
  7.8 0.5 constant_dynamic-slice_fusion.3
  8.3 0.1 copy.56
  8.4 8.8 %collective-permute-start.3 = (f32[2,1,128,128]{2,3,0,1:T(8,128)S(1)}, f32[2,1,128,128]{2,3,0,1:T(8,128)S(1)}, u32[]{:S(2)}, u32[]{:S(2)}) collective-permute-start(f32[2,1,128,128]{2,3,0,1:T(8,128)S(1)} %bitcast.75), channel_id=1, source_target_pairs={{16,0},{32,16},{48,32},{64,50},{80,2},{82,66},{96,18},{98,82},{112... | collective-permute-start | bytes 393224 | tf_op jit(solution)/shard_map/ppermute | solution.py:41
  17.2 0.1 copy.54
  17.3 0.7 collective-permute-start.1
  18.0 0.1 copy.55
  18.1 1.3 collective-permute-start.2
  19.4 0.1 copy.53
  19.5 0.7 collective-permute-start
  20.2 0.7 compare_bitcast_fusion
  20.8 0.1 broadcast_bitcast_fusion
  21.0 0.0 collective-permute-done.3
  21.0 0.0 collective-permute-done.1
  21.0 4.1 %collective-permute-done.2 = f32[2,1,128,128]{2,3,0,1:T(8,128)S(1)} collective-permute-done((f32[2,1,128,128]{2,3,0,1:T(8,128)S(1)}, f32[2,1,128,128]{2,3,0,1:T(8,128)S(1)}, u32[]{:S(2)}, u32[]{:S(2)}) %collective-permute-start.2) | collective-permute-done | bytes 131104 | tf_op jit(solution)/shard_map/ppermute | solution.py:41
  25.1 0.0 collective-permute-done
  25.1 0.6 gather_fusion
  25.7 0.3 copy.42
  26.1 0.2 gather.13
  26.3 1.7 fusion.2
  28.0 0.0 all-gather.7.cloned.1.call-update
  28.0 0.0 all-gather.5.cloned.1.call-start
  28.1 0.0 copy-done
  28.1 0.2 copy.44
  28.3 0.0 copy-done.2
  28.3 0.2 convert_reduce_fusion
  28.5 0.1 mul.83
  28.6 0.1 mul.84
  28.7 0.2 copy.43
  28.9 0.1 dynamic-slice_select_fusion.2
  29.0 0.8 bitcast_multiply_fusion
  29.8 0.0 all-gather.5.cloned.1.call-update
  29.8 0.0 all-gather.9.cloned.1.call-start
  29.8 138.6 %all-gather.7.cloned.1.call-done = f32[1,1024,2,512]{3,1,2,0:T(8,128)} async-done(((f32[1,64,2,512]{3,1,2,0:T(8,128)}), f32[1,1024,2,512]{3,1,2,0:T(8,128)}) %all-gather.7.cloned.1.call-update) | async-done | bytes 4194320 | tf_op jit(solution)/shard_map/all_gather | solution.py:67
  168.4 0.0 all-gather.9.cloned.1.call-update
  168.5 0.2 reduce-scatter.2.cloned.1.call-start
  168.7 43.9 %all-gather.5.cloned.1.call-done = f32[2,1,128,2048]{2,3,0,1:T(8,128)} async-done(((f32[2,1,128,256]{2,3,0,1:T(8,128)}), f32[2,1,128,2048]{2,3,0,1:T(8,128)}) %all-gather.5.cloned.1.call-update) | async-done | bytes 2097168 | tf_op jit(solution)/shard_map/all_gather | solution.py:58
  212.6 1.7 copy.45
  214.3 32.0 %all-gather.9.cloned.1.call-done = f32[2,1024,2,512]{3,1,2,0:T(8,128)} async-done(((f32[1,1024,2,512]{3,1,2,0:T(8,128)}), f32[2,1024,2,512]{3,1,2,0:T(8,128)}) %all-gather.9.cloned.1.call-update) | async-done | bytes 8388624 | tf_op jit(solution)/shard_map/all_gather | solution.py:68
  246.3 14.4 %copy.47 = f32[2,1024,2,512]{3,2,1,0:T(2,128)S(1)} copy(f32[2,1024,2,512]{3,1,2,0:T(8,128)} %all-gather.9.cloned.1.call-done) | data formatting | bytes 16777216 | tf_op jit(solution)/shard_map/all_gather | solution.py:68
  260.7 5.3 %copy.57 = f32[256,8,2,512]{3,1,2,0:T(8,128)} copy(f32[256,8,2,512]{3,2,1,0:T(2,128)S(1)} %bitcast.66) | data formatting | bytes 16777216
  266.0 9.2 %copy.48 = f32[1024,2048]{1,0:T(8,128)} copy(f32[1024,2048]{0,1:T(8,128)} %bitcast.67) | data formatting | bytes 16777216 | tf_op jit(solution)/shard_map/fak,fkb->fab/dot_general | solution.py:71
  275.3 0.0 copy-start.1
  275.3 15.8 %convolution_bitcast_fusion = f32[1,2,128,2,512]{4,2,3,1,0:T(8,128)S(1)} fusion(f32[2,128,2048,1]{1,2,3,0:T(8,128)S(1)} %bitcast.68, f32[2,512,2048,1]{2,1,0,3:T(8,128)} %bitcast.65), kind=kOutput, calls=%fused_computation.1 | convolution fusion | flops 6442450944 | bytes 11534336 | tf_op jit(solution)/shard_map/fak,fkb->fab/dot_general | solution.py:71
  291.1 0.1 fusion.1
  291.2 0.8 pad_maximum_fusion
  292.0 0.0 reduce-scatter.2.cloned.1.call-update
  292.0 0.1 dynamic-slice
  292.1 0.1 dynamic-slice.1
  292.2 0.0 copy-done.1
  292.2 0.6 fusion.6
  292.8 0.2 gather.11
  293.0 0.1 dynamic-slice_select_fusion.4
  293.1 22.8 %reduce-scatter.2.cloned.1.call-done = f32[2,1,128,256]{3,2,1,0:T(8,128)} async-done(((f32[2,1,128,512]{3,2,1,0:T(8,128)}), f32[2,1,128,256]{3,2,1,0:T(8,128)}) %reduce-scatter.2.cloned.1.call-update) | async-done | bytes 262160 | tf_op jit(solution)/shard_map/reduce_scatter | solution.py:76
  315.9 2.3 slice_subtract_fusion.2
  318.2 0.7 pad_maximum_fusion.1
  (5 shorter events, 0.1 us)
Async XLA Ops:
  6.5 21.5 %copy-start = (f32[2,1,128,512]{3,2,1,0:T(8,128)S(1)}, f32[2,1,128,512]{3,2,1,0:T(8,128)}, u32[]{:S(2)}) copy-start(f32[2,1,128,512]{3,2,1,0:T(8,128)} %param.4) | copy-start | bytes 1572868
  6.5 21.8 %copy-start.2 = (s32[1,24]{1,0:T(1,128)S(1)}, s32[1,24]{1,0:T(1,128)}, u32[]{:S(2)}) copy-start(s32[1,24]{1,0:T(1,128)} %param.6) | copy-start | bytes 292
  6.5 161.9 %all-gather.7.cloned.1.call-start = ((), (), s32[]{:S(2)}) async-start(), calls=%async_computation.2 | async-start | bytes 4456448 | tf_op jit(solution)/shard_map/all_gather | solution.py:67
  8.4 12.5 %collective-permute-start.3 = (f32[2,1,128,128]{2,3,0,1:T(8,128)S(1)}, f32[2,1,128,128]{2,3,0,1:T(8,128)S(1)}, u32[]{:S(2)}, u32[]{:S(2)}) collective-permute-start(f32[2,1,128,128]{2,3,0,1:T(8,128)S(1)} %bitcast.75), channel_id=1, source_target_pairs={{16,0},{32,16},{48,32},{64,50},{80,2},{82,66},{96,18},{98,82},{112... | collective-permute-start | bytes 393224 | tf_op jit(solution)/shard_map/ppermute | solution.py:41
  17.3 3.7 %collective-permute-start.1 = (f32[2,1,128,128]{2,3,0,1:T(8,128)S(1)}, f32[2,1,128,128]{2,3,0,1:T(8,128)S(1)}, u32[]{:S(2)}, u32[]{:S(2)}) collective-permute-start(f32[2,1,128,128]{2,3,0,1:T(8,128)S(1)} %bitcast.76), channel_id=1, source_target_pairs={{48,0},{64,18},{80,34},{96,50},{112,2},{114,66},{128,20},{130,84},... | collective-permute-start | bytes 393224 | tf_op jit(solution)/shard_map/ppermute | solution.py:41
  18.1 7.0 %collective-permute-start.2 = (f32[2,1,128,128]{2,3,0,1:T(8,128)S(1)}, f32[2,1,128,128]{2,3,0,1:T(8,128)S(1)}, u32[]{:S(2)}, u32[]{:S(2)}) collective-permute-start(f32[2,1,128,128]{2,3,0,1:T(8,128)S(1)} %bitcast.77), channel_id=1, source_target_pairs={{32,0},{48,16},{64,34},{80,50},{96,2},{98,66},{112,18},{114,82},{1... | collective-permute-start | bytes 393224 | tf_op jit(solution)/shard_map/ppermute | solution.py:41
  19.5 5.6 %collective-permute-start = (f32[2,1,128,128]{2,3,0,1:T(8,128)S(1)}, f32[2,1,128,128]{2,3,0,1:T(8,128)S(1)}, u32[]{:S(2)}, u32[]{:S(2)}) collective-permute-start(f32[2,1,128,128]{2,3,0,1:T(8,128)S(1)} %bitcast.78), channel_id=1, source_target_pairs={{64,2},{80,18},{96,34},{112,50},{128,4},{130,68},{144,20},{146,84}... | collective-permute-start | bytes 393224 | tf_op jit(solution)/shard_map/ppermute | solution.py:41
  28.0 184.5 %all-gather.5.cloned.1.call-start = ((), (), s32[]{:S(2)}) async-start(), calls=%async_computation.1 | async-start | bytes 2359296 | tf_op jit(solution)/shard_map/all_gather | solution.py:58
  29.8 216.5 %all-gather.9.cloned.1.call-start = ((), (), s32[]{:S(2)}) async-start(), calls=%async_computation.4 | async-start | bytes 12582912 | tf_op jit(solution)/shard_map/all_gather | solution.py:68
  168.5 147.5 %reduce-scatter.2.cloned.1.call-start = ((), (), s32[]{:S(2)}) async-start(), calls=%async_computation.3 | async-start | bytes 786432 | tf_op jit(solution)/shard_map/reduce_scatter | solution.py:76
  275.3 16.9 %copy-start.1 = (f32[2,1]{0,1:T(1,128)S(1)}, f32[2,1]{0,1:T(1,128)}, u32[]{:S(2)}) copy-start(f32[2,1]{0,1:T(1,128)} %param.7) | copy-start | bytes 28
Sparse Core Ops, SparseCore 0:
  28.2 140.2 all-gather.6
  170.5 42.0 all-gather.4
  214.7 31.5 all-gather.8
  292.1 23.7 reduce-scatter.1

commit v2 on v1

--- a/solution.py
+++ b/solution.py
@@ -55,15 +55,15 @@
     left = lax.dynamic_index_in_dim(left, my_half, 4, keepdims=False)
     left = left * chosen[None, None, None, :, None]
     left = left.reshape(comp_count, freq_count, TILE, per_rcv * half)
-    left = lax.all_gather(left, "z", axis=3, tiled=True)
+    left = lax.all_gather(left, "z", axis=0, tiled=False)
     n_pair = n_src // n_core
-    left = left.reshape(comp_count, freq_count, TILE, n_pair, n_core, half)
-    left = jnp.transpose(left, (1, 0, 2, 4, 3, 5))
+    left = left.reshape(n_rcv, comp_count, freq_count, TILE, per_rcv // n_core, n_core, half)
+    left = jnp.transpose(left, (2, 1, 3, 5, 0, 4, 6))
     left = left.reshape(freq_count, comp_count * TILE, n_src * half)
 
     right = filled.reshape(comp_count, freq_count, n_half, half, local_cols)
     right = lax.dynamic_index_in_dim(right, my_half, 2, keepdims=False)
-    right = jnp.transpose(right, (1, 2, 0, 3))
+    right = jnp.transpose(right, (1, 2, 0, 3)).reshape(freq_count, half, comp_count * local_cols)
     right = lax.all_gather(right, ("y", "xl"), axis=1, tiled=True)
     right = lax.all_gather(right, "c", axis=1, tiled=False)
     right = right.reshape(freq_count, n_src * half, comp_count * local_cols)

time: 326 us -> 305 us (0.936)
  local copies, waits for them, and re-layouts: 35.6 us -> 19 us
    all_gather x1, local copies, waits for them, and re-layouts: 14.4 us -> 1.91 us  [per_device(): left = lax.all_gather(left, 'z', axis=0, tiled=False)]
    another operation x0 -> x1, local copies, waits for them, and re-layouts: none -> 9.27 us
    dot_general x1 -> x0, local copies, waits for them, and re-layouts: 9.22 us -> none  [per_device(): jnp.einsum('fak,fkb->fab', left, right, precision=lax.Precision.HIGHEST)]
    unnamed x12 -> x13, local copies, waits for them, and re-layouts: 5.9 us -> 0.59 us
where the time goes in v2:
time: 305 us
  waiting for transfers between devices  240 us (79%)
  local copies, waits for them, and re-layouts  19 us (6%)
  matrix products  15.8 us (5%)
  between operations  13.4 us (4%)
  starting transfers between devices  11.5 us (4%)
  other arithmetic  5.09 us (2%)
    all_gather x1, waiting for transfers between devices, per_device(): right = lax.all_gather(right, ('y', 'xl'), axis=1, tiled=True)  139 us
    all_gather x1, waiting for transfers between devices, per_device(): left = lax.all_gather(left, 'z', axis=0, tiled=False)  44.1 us
    all_gather x1, waiting for transfers between devices, per_device(): right = lax.all_gather(right, 'c', axis=1, tiled=False)  30.3 us
    reduce_scatter x1, waiting for transfers between devices, per_device(): lax.psum_scatter(partial_sum, 'xh', scatter_dimension=3, tiled=True)  22.9 us
    dot_general x1, matrix products, per_device(): jnp.einsum('fak,fkb->fab', left, right, precision=lax.Precision.HIGHEST)  15.8 us
    ppermute x4, starting transfers between devices, per_device(): got = lax.ppermute(sent, FILL, mirror_pairs(n_src, n_rcv, per_rcv, step))  11.4 us
    another operation x1, local copies, waits for them, and re-layouts  9.27 us
  transfers between devices with their start and end apart: 8, of which 5 were waited for; matrix products, arithmetic and copies ran while one was open for 2% of the time, Pallas kernels for 0%

profile of v2, /device:TPU:1, one launch (start us, length us, event | category | flops | bytes accessed | tf_op | source)
XLA Modules:
  0.0 304.8 jit_solution(9181908193627222289)
XLA Ops:
  6.5 0.0 copy-start.1
  6.5 0.0 all-gather.7.cloned.1.call-start
  6.5 1.3 reshape.251
  7.8 0.5 constant_dynamic-slice_fusion.3
  8.3 0.0 copy-start.3
  8.3 0.1 copy.60
  8.4 8.8 %collective-permute-start.3 = (f32[2,1,128,128]{2,3,0,1:T(8,128)S(1)}, f32[2,1,128,128]{2,3,0,1:T(8,128)S(1)}, u32[]{:S(2)}, u32[]{:S(2)}) collective-permute-start(f32[2,1,128,128]{2,3,0,1:T(8,128)S(1)} %bitcast.75), channel_id=1, source_target_pairs={{16,0},{32,16},{48,32},{64,50},{80,2},{82,66},{96,18},{98,82},{112... | collective-permute-start | bytes 393224 | tf_op jit(solution)/shard_map/ppermute | solution.py:41
  17.2 0.1 copy.58
  17.3 0.7 collective-permute-start.1
  18.0 0.1 copy.59
  18.1 1.3 collective-permute-start.2
  19.4 0.1 copy.57
  19.5 0.7 collective-permute-start
  20.2 0.7 compare_bitcast_fusion
  20.9 0.1 broadcast_bitcast_fusion
  21.0 0.0 collective-permute-done.3
  21.0 0.0 collective-permute-done.1
  21.0 4.1 %collective-permute-done.2 = f32[2,1,128,128]{2,3,0,1:T(8,128)S(1)} collective-permute-done((f32[2,1,128,128]{2,3,0,1:T(8,128)S(1)}, f32[2,1,128,128]{2,3,0,1:T(8,128)S(1)}, u32[]{:S(2)}, u32[]{:S(2)}) %collective-permute-start.2) | collective-permute-done | bytes 131104 | tf_op jit(solution)/shard_map/ppermute | solution.py:41
  25.1 0.0 collective-permute-done
  25.2 0.6 gather_fusion
  25.7 0.3 copy.44
  26.1 0.2 gather.13
  26.3 0.0 copy-done.1
  26.4 0.7 copy.61
  27.1 0.0 all-gather.7.cloned.1.call-update
  27.1 0.0 all-gather.5.cloned.1.call-start
  27.2 0.2 copy.46
  27.4 0.0 copy-done.3
  27.4 0.2 convert_reduce_fusion
  27.6 0.1 mul.83
  27.6 0.1 mul.84
  27.7 0.2 copy.45
  27.9 0.1 dynamic-slice_select_fusion.2
  28.0 0.1 broadcast_multiply_fusion
  28.1 0.8 copy.47
  29.0 0.0 all-gather.5.cloned.1.call-update
  29.0 0.0 all-gather.9.cloned.1.call-start
  29.1 138.5 %all-gather.7.cloned.1.call-done = f32[1,1024,1024]{2,1,0:T(8,128)} async-done(((f32[1,64,1024]{2,1,0:T(8,128)}), f32[1,1024,1024]{2,1,0:T(8,128)}) %all-gather.7.cloned.1.call-update) | async-done | bytes 4194320 | tf_op jit(solution)/shard_map/all_gather | solution.py:67
  167.6 0.0 all-gather.9.cloned.1.call-update
  167.6 0.0 reduce-scatter.2.cloned.1.call-start
  167.6 44.1 %all-gather.5.cloned.1.call-done = f32[8,2,1,128,256]{4,3,2,1,0:T(8,128)} async-done(((f32[1,2,1,128,256]{4,3,2,1,0:T(8,128)}), f32[8,2,1,128,256]{4,3,2,1,0:T(8,128)}) %all-gather.5.cloned.1.call-update) | async-done | bytes 2097168 | tf_op jit(solution)/shard_map/all_gather | solution.py:58
  211.7 1.9 copy.48
  213.6 1.5 copy.49
  215.1 30.3 %all-gather.9.cloned.1.call-done = f32[2,1024,1024]{2,1,0:T(8,128)} async-done(((f32[1,1024,1024]{2,1,0:T(8,128)}), f32[2,1024,1024]{2,1,0:T(8,128)}) %all-gather.9.cloned.1.call-update) | async-done | bytes 8388624 | tf_op jit(solution)/shard_map/all_gather | solution.py:68
  245.4 0.0 copy-start
  245.4 9.3 %copy.52 = f32[2048,1024]{0,1:T(8,128)} copy(f32[2048,1024]{1,0:T(8,128)} %bitcast.65) | data formatting | bytes 16777216 | tf_op jit(solution)/shard_map/reshape.5
  254.7 0.0 copy-done
  254.7 0.0 copy-start.2
  254.7 15.8 %convolution_bitcast_fusion = f32[1,2,128,2,512]{4,2,3,1,0:T(8,128)S(1)} fusion(f32[2,128,2048,1]{1,2,3,0:T(8,128)S(1)} %bitcast.67, f32[2,512,2048,1]{2,1,0,3:T(8,128)} %bitcast.64), kind=kOutput, calls=%fused_computation.1 | convolution fusion | flops 6442450944 | bytes 11534336 | tf_op jit(solution)/shard_map/fak,fkb->fab/dot_general | solution.py:71
  270.5 0.1 fusion.1
  270.6 0.8 pad_maximum_fusion
  271.4 0.0 reduce-scatter.2.cloned.1.call-update
  271.4 0.1 dynamic-slice
  271.5 0.1 dynamic-slice.1
  271.6 0.0 copy-done.2
  271.6 0.6 fusion.6
  272.1 0.2 gather.11
  272.4 0.1 dynamic-slice_select_fusion.4
  272.4 22.9 %reduce-scatter.2.cloned.1.call-done = f32[2,1,128,256]{3,2,1,0:T(8,128)} async-done(((f32[2,1,128,512]{3,2,1,0:T(8,128)}), f32[2,1,128,256]{3,2,1,0:T(8,128)}) %reduce-scatter.2.cloned.1.call-update) | async-done | bytes 262160 | tf_op jit(solution)/shard_map/reduce_scatter | solution.py:76
  295.3 2.2 slice_subtract_fusion.2
  297.6 0.7 pad_maximum_fusion.1
  (6 shorter events, 0.1 us)
Async XLA Ops:
  6.5 19.8 %copy-start.1 = (f32[2,1,128,512]{3,2,1,0:T(8,128)S(1)}, f32[2,1,128,512]{3,2,1,0:T(8,128)}, u32[]{:S(2)}) copy-start(f32[2,1,128,512]{3,2,1,0:T(8,128)} %param.4) | copy-start | bytes 1572868
  6.5 161.0 %all-gather.7.cloned.1.call-start = ((), (), s32[]{:S(2)}) async-start(), calls=%async_computation.2 | async-start | bytes 4456448 | tf_op jit(solution)/shard_map/all_gather | solution.py:67
  8.3 19.1 %copy-start.3 = (s32[1,24]{1,0:T(1,128)S(1)}, s32[1,24]{1,0:T(1,128)}, u32[]{:S(2)}) copy-start(s32[1,24]{1,0:T(1,128)} %param.6) | copy-start | bytes 292
  8.4 12.5 %collective-permute-start.3 = (f32[2,1,128,128]{2,3,0,1:T(8,128)S(1)}, f32[2,1,128,128]{2,3,0,1:T(8,128)S(1)}, u32[]{:S(2)}, u32[]{:S(2)}) collective-permute-start(f32[2,1,128,128]{2,3,0,1:T(8,128)S(1)} %bitcast.75), channel_id=1, source_target_pairs={{16,0},{32,16},{48,32},{64,50},{80,2},{82,66},{96,18},{98,82},{112... | collective-permute-start | bytes 393224 | tf_op jit(solution)/shard_map/ppermute | solution.py:41
  17.3 3.7 %collective-permute-start.1 = (f32[2,1,128,128]{2,3,0,1:T(8,128)S(1)}, f32[2,1,128,128]{2,3,0,1:T(8,128)S(1)}, u32[]{:S(2)}, u32[]{:S(2)}) collective-permute-start(f32[2,1,128,128]{2,3,0,1:T(8,128)S(1)} %bitcast.76), channel_id=1, source_target_pairs={{48,0},{64,18},{80,34},{96,50},{112,2},{114,66},{128,20},{130,84},... | collective-permute-start | bytes 393224 | tf_op jit(solution)/shard_map/ppermute | solution.py:41
  18.1 7.0 %collective-permute-start.2 = (f32[2,1,128,128]{2,3,0,1:T(8,128)S(1)}, f32[2,1,128,128]{2,3,0,1:T(8,128)S(1)}, u32[]{:S(2)}, u32[]{:S(2)}) collective-permute-start(f32[2,1,128,128]{2,3,0,1:T(8,128)S(1)} %bitcast.77), channel_id=1, source_target_pairs={{32,0},{48,16},{64,34},{80,50},{96,2},{98,66},{112,18},{114,82},{1... | collective-permute-start | bytes 393224 | tf_op jit(solution)/shard_map/ppermute | solution.py:41
  19.5 5.6 %collective-permute-start = (f32[2,1,128,128]{2,3,0,1:T(8,128)S(1)}, f32[2,1,128,128]{2,3,0,1:T(8,128)S(1)}, u32[]{:S(2)}, u32[]{:S(2)}) collective-permute-start(f32[2,1,128,128]{2,3,0,1:T(8,128)S(1)} %bitcast.78), channel_id=1, source_target_pairs={{64,2},{80,18},{96,34},{112,50},{128,4},{130,68},{144,20},{146,84}... | collective-permute-start | bytes 393224 | tf_op jit(solution)/shard_map/ppermute | solution.py:41
  27.1 184.6 %all-gather.5.cloned.1.call-start = ((), (), s32[]{:S(2)}) async-start(), calls=%async_computation.1 | async-start | bytes 2359296 | tf_op jit(solution)/shard_map/all_gather | solution.py:58
  29.0 216.4 %all-gather.9.cloned.1.call-start = ((), (), s32[]{:S(2)}) async-start(), calls=%async_computation.4 | async-start | bytes 12582912 | tf_op jit(solution)/shard_map/all_gather | solution.py:68
  167.6 127.8 %reduce-scatter.2.cloned.1.call-start = ((), (), s32[]{:S(2)}) async-start(), calls=%async_computation.3 | async-start | bytes 786432 | tf_op jit(solution)/shard_map/reduce_scatter | solution.py:76
  245.4 9.3 %copy-start = (f32[1,2,128,2,8,2,64]{2,6,5,4,3,1,0:T(8,128)S(1)}, f32[1,2,128,2,8,2,64]{2,6,5,4,3,1,0:T(8,128)}, u32[]{:S(2)}) copy-start(f32[1,2,128,2,8,2,64]{2,6,5,4,3,1,0:T(8,128)} %copy.49) | copy-start | bytes 6291460
  254.7 16.9 %copy-start.2 = (f32[2,1]{0,1:T(1,128)S(1)}, f32[2,1]{0,1:T(1,128)}, u32[]{:S(2)}) copy-start(f32[2,1]{0,1:T(1,128)} %param.7) | copy-start | bytes 28
Sparse Core Ops, SparseCore 0:
  27.2 140.2 all-gather.6
  169.6 42.0 all-gather.4
  213.8 31.5 all-gather.8
  271.5 23.7 reduce-scatter.1

commit v3 on v0

--- a/solution.py
+++ b/solution.py
@@ -33,6 +33,17 @@
     return arrived.sum(axis=0)
 
 
+def mirror_pairs(n_src, n_rcv, per_rcv, step):
+    pairs = []
+    for s in range(n_src):
+        for r in range(n_rcv):
+            t = (s % per_rcv + step) % per_rcv
+            dest_s = per_rcv * r + t
+            if s > dest_s:
+                pairs.append((s * n_rcv + r, dest_s * n_rcv + s // per_rcv))
+    return pairs
+
+
 def complex_prod(left_side, right_side):
     return jnp.einsum("fik,fkj->fij", left_side, right_side, precision=lax.Precision.HIGHEST)
 
@@ -42,24 +53,23 @@
     my_half = lax.axis_index("int")
     rcv_count = lax.axis_size("rcv")
     comp_count, freq_count, local_rows, local_cols = traces.shape
-    regrouped = lax.all_to_all(traces, "rcv", split_axis=2, concat_axis=3, tiled=True)
-    sectioned = regrouped.reshape(
-        comp_count, freq_count, 1, local_rows // rcv_count, local_cols * rcv_count
-    )
-    arrived = lax.all_to_all(
-        lax.all_to_all(sectioned, "src", split_axis=4, concat_axis=2, tiled=True),
-        "rcv",
-        split_axis=2,
-        concat_axis=3,
-        tiled=True,
-    )
-    mirrored = jnp.swapaxes(arrived.reshape(comp_count, freq_count, local_cols, local_rows), 2, 3)
+    per_rcv = local_cols // TILE
+    src_count = lax.axis_size("src")
+    me_src = lax.axis_index("src")
+    tiles = traces.reshape(comp_count, freq_count, TILE, per_rcv, TILE)
+    arrived = []
+    for step in range(per_rcv):
+        pick = (me_src % per_rcv + step) % per_rcv
+        sent = lax.dynamic_index_in_dim(tiles, pick, 3, keepdims=False)
+        got = lax.ppermute(sent, ("src", "rcv"), mirror_pairs(src_count, rcv_count, per_rcv, step))
+        arrived.append(jnp.swapaxes(got, 2, 3))
+    arrived = jnp.stack(arrived, axis=3)
+    order = (me_src % per_rcv - jnp.arange(per_rcv)) % per_rcv
+    mirrored = jnp.take(arrived, order, axis=3)
+    marks = (missing[0] > 0)[None, None, None, :, None]
+    filled = jnp.where(marks, mirrored, tiles).reshape(traces.shape)
     row_tiles = local_rows // TILE
     col_tiles = local_cols // TILE
-    tile_mask = jnp.broadcast_to(
-        missing[:, None, :, None] > 0, (row_tiles, TILE, col_tiles, TILE)
-    ).reshape(local_rows, local_cols)
-    filled = jnp.where(tile_mask[None, None], mirrored, traces)
     half_tile = TILE // half_count
     left_half = filled.reshape(comp_count, freq_count, local_rows, col_tiles, half_count, half_tile)
     left_half = lax.dynamic_index_in_dim(left_half, my_half, 4, keepdims=False)

time: 222 us -> 187 us (0.84)
  blocking collectives: 53.8 us -> 0 us
  starting transfers between devices: 11.3 us -> 63.1 us
  local copies, waits for them, and re-layouts: 30.9 us -> 8.86 us
  waiting for transfers between devices: 87.5 us -> 76.7 us
    all_to_all x2 -> x0, blocking collectives: 53.8 us -> none  [the longest x1 27.2 us: per_device(): lax.all_to_all(sectioned, 'src', split_axis=4, concat_axis=2, tiled=True)]
    all_to_all x1, starting transfers between devices: 3.78 us -> 47.4 us  [from_everyone(): return lax.all_to_all(copies, axis, split_axis=0, concat_axis=0, tiled=True)]
    all_to_all x1 -> x0, waiting for transfers between devices: 15.9 us -> none  [per_device(): lax.all_to_all(lax.all_to_all(sectioned, 'src', split_axis=4, concat_axis...]
    unnamed x14 -> x17, local copies, waits for them, and re-layouts: 16.1 us -> 1.01 us
    ppermute x0 -> x4, starting transfers between devices: none -> 11.4 us  [per_device(): lax.ppermute(sent, ('src', 'rcv'), mirror_pairs(src_count, rcv_count, per...]
    all_to_all x5 -> x0, local copies, waits for them, and re-layouts: 6.54 us -> none  [the longest x2 6.36 us: per_device(): lax.all_to_all(sectioned, 'src', split_axis=4, concat_axis=2, tiled=True)]
    all_to_all x1 -> x0, starting transfers between devices: 3.49 us -> none  [per_device(): lax.all_to_all(lax.all_to_all(sectioned, 'src', split_axis=4, concat_axis...]
    ppermute x0 -> x4, waiting for transfers between devices: none -> 3.43 us  [per_device(): lax.ppermute(sent, ('src', 'rcv'), mirror_pairs(src_count, rcv_count, per...]
  transfers between devices with their start and end apart: 4 -> 7, of which waited for: 4 -> 4; matrix products, arithmetic and copies ran while one was open for 2% -> 3% of each run, Pallas kernels for 0% -> 0%
where the time goes in v3:
time: 187 us; the launch traced here: 186 us
  waiting for transfers between devices  76.7 us (41%)
  starting transfers between devices  63.1 us (34%)
  matrix products  19.2 us (10%)
  between operations  13.7 us (7%)
  local copies, waits for them, and re-layouts  8.86 us (5%)
  other arithmetic  4.76 us (3%)
    all_to_all x1, waiting for transfers between devices, from_everyone(): return lax.all_to_all(copies, axis, split_axis=0, concat_axis=0, tiled=True)  50.3 us
    all_to_all x1, starting transfers between devices, from_everyone(): return lax.all_to_all(copies, axis, split_axis=0, concat_axis=0, tiled=True)  47.4 us
    dot_general x4, matrix products, complex_prod(): jnp.einsum('fik,fkj->fij', left_side, right_side, precision=lax.Precision...  19.2 us
    all_gather x1, waiting for transfers between devices, per_device(): slab_piece = lax.all_gather(right_half, 'src', axis=2, tiled=True)  14.3 us
    ppermute x4, starting transfers between devices, per_device(): lax.ppermute(sent, ('src', 'rcv'), mirror_pairs(src_count, rcv_count, per...  11.4 us
    all_to_all x1, waiting for transfers between devices, sent_and_summed(): lax.all_to_all(pieces, axis, split_axis=0, concat_axis=0, tiled=True)  8.69 us
    all_to_all x1, starting transfers between devices, sent_and_summed(): lax.all_to_all(pieces, axis, split_axis=0, concat_axis=0, tiled=True)  4.31 us
  transfers between devices with their start and end apart: 7, of which 4 were waited for; matrix products, arithmetic and copies ran while one was open for 3% of the time, Pallas kernels for 0%

profile of v3, /device:TPU:1, one launch (start us, length us, event | category | flops | bytes accessed | tf_op | source)
XLA Modules:
  0.0 186.3 jit_solution(3559364013275598438)
XLA Ops:
  6.5 0.0 copy-start
  6.5 0.0 all-gather.3.cloned.1.call-start
  6.5 1.3 reshape.367
  7.8 0.5 constant_dynamic-slice_fusion.7
  8.3 0.1 copy.61
  8.4 8.8 %collective-permute-start.3 = (f32[2,1,128,128]{2,3,0,1:T(8,128)S(1)}, f32[2,1,128,128]{2,3,0,1:T(8,128)S(1)}, u32[]{:S(2)}, u32[]{:S(2)}) collective-permute-start(f32[2,1,128,128]{2,3,0,1:T(8,128)S(1)} %bitcast.96), channel_id=1, source_target_pairs={{16,0},{32,16},{48,32},{64,50},{80,2},{82,66},{96,18},{98,82},{112... | collective-permute-start | bytes 393224 | tf_op jit(solution)/shard_map/ppermute | solution.py:64
  17.2 0.1 copy.60
  17.3 1.3 collective-permute-start.2
  18.6 0.1 copy.59
  18.7 0.7 collective-permute-start.1
  19.4 0.1 copy.58
  19.5 0.7 collective-permute-start
  20.2 0.7 compare_bitcast_fusion
  20.9 0.1 broadcast_bitcast_fusion.2
  21.0 0.0 collective-permute-done.3
  21.0 3.4 %collective-permute-done.2 = f32[2,1,128,128]{2,3,0,1:T(8,128)S(1)} collective-permute-done((f32[2,1,128,128]{2,3,0,1:T(8,128)S(1)}, f32[2,1,128,128]{2,3,0,1:T(8,128)S(1)}, u32[]{:S(2)}, u32[]{:S(2)}) %collective-permute-start.2) | collective-permute-done | bytes 131104 | tf_op jit(solution)/shard_map/ppermute | solution.py:64
  24.4 0.0 collective-permute-done.1
  24.4 0.0 collective-permute-done
  24.5 0.6 gather_fusion
  25.0 0.3 copy.53
  25.4 0.2 gather.13
  25.6 0.0 copy-done
  25.6 0.7 dynamic-slice_select_fusion
  26.4 0.0 all-gather.3.cloned.1.call-update
  26.4 0.2 copy.48
  26.6 0.0 copy-start.1
  26.6 0.0 copy-start.2
  26.6 0.2 copy.46
  26.8 0.1 dynamic-slice_select_fusion.2
  26.9 1.6 broadcast_in_dim.63
  28.5 47.4 %all-to-all-start = ((f32[8,2,1,128,256]{3,4,1,2,0:T(8,128)}), f32[8,2,1,128,256]{3,4,1,2,0:T(8,128)S(1)}, u32[]{:S(2)}, u32[]{:S(2)}) async-start(f32[8,2,1,128,256]{3,4,1,2,0:T(8,128)} %broadcast_in_dim.63), calls=%async_computation | async-start | bytes 4194304 | tf_op jit(solution)/shard_map/all_to_all | solution.py:11
  75.9 0.1 gt.15
  75.9 0.1 broadcast_bitcast_fusion.1
  76.0 0.1 broadcast_bitcast_fusion
  76.1 0.0 copy-done.1
  76.2 0.6 fusion.13
  76.8 0.0 copy-done.2
  76.8 0.1 convert_reduce_fusion
  76.8 50.3 %all-to-all-done = f32[8,2,1,128,256]{3,4,1,2,0:T(8,128)S(1)} async-done(((f32[8,2,1,128,256]{3,4,1,2,0:T(8,128)}), f32[8,2,1,128,256]{3,4,1,2,0:T(8,128)S(1)}, u32[]{:S(2)}, u32[]{:S(2)}) %all-to-all-start) | async-done | bytes 2097184 | tf_op jit(solution)/shard_map/all_to_all | solution.py:11
  127.2 0.2 copy.52
  127.3 0.2 broadcast_multiply_fusion
  127.5 0.2 fusion.12
  127.8 14.3 %all-gather.3.cloned.1.call-done = f32[2,1,1,1,2048,512]{5,4,3,0,2,1:T(8,128)} async-done(((f32[2,1,1,1,64,512]{5,4,3,0,2,1:T(8,128)}), f32[2,1,1,1,2048,512]{5,4,3,0,2,1:T(8,128)}) %all-gather.3.cloned.1.call-update) | async-done | bytes 8388624 | tf_op jit(solution)/shard_map/all_gather | solution.py:93
  142.1 4.8 %fusion = f32[128,512]{1,0:T(8,128)S(1)} fusion(f32[128,2048]{0,1:T(8,128)S(1)} %bitcast.83, f32[2,1,1,1,2048,512]{5,4,3,0,2,1:T(8,128)} %all-gather.3.cloned.1.call-done), kind=kOutput, calls=%fused_computation.3 | convolution fusion | flops 1610612736 | bytes 5505024 | tf_op jit(solution)/shard_map/fik,fkj->fij/dot_general | solution.py:48
  146.9 4.8 %fusion.5 = f32[128,512]{1,0:T(8,128)S(1)} fusion(f32[128,512]{1,0:T(8,128)S(1)} %fusion, f32[128,2048]{0,1:T(8,128)S(1)} %bitcast.85, f32[2,1,1,1,2048,512]{5,4,3,0,2,1:T(8,128)} %all-gather.3.cloned.1.call-done), kind=kOutput, calls=%fused_computation.8 | convolution fusion | flops 1610678272 | bytes 5767168 | tf_op jit(solution)/shard_map/fik,fkj->fij/dot_general | solution.py:48
  151.7 0.9 stack.35
  152.5 1.0 copy.55
  153.5 4.8 %fusion.1 = f32[128,512]{1,0:T(8,128)S(1)} fusion(f32[128,2048]{0,1:T(8,128)S(1)} %bitcast.86, f32[2,1,1,1,2048,512]{5,4,3,0,2,1:T(8,128)} %all-gather.3.cloned.1.call-done), kind=kOutput, calls=%fused_computation.4 | convolution fusion | flops 1610612736 | bytes 5505024 | tf_op jit(solution)/shard_map/fik,fkj->fij/dot_general | solution.py:48
  158.3 4.8 %fusion.4 = f32[128,512]{1,0:T(8,128)S(1)} fusion(f32[128,512]{1,0:T(8,128)S(1)} %fusion.1, f32[128,2048]{0,1:T(8,128)S(1)} %bitcast.84, f32[2,1,1,1,2048,512]{5,4,3,0,2,1:T(8,128)} %all-gather.3.cloned.1.call-done), kind=kOutput, calls=%fused_computation.7 | convolution fusion | flops 1610678272 | bytes 5767168 | tf_op jit(solution)/shard_map/fik,fkj->fij/dot_general | solution.py:48
  163.1 0.2 stack.34
  163.3 0.8 maximum_bitcast_fusion.1
  164.1 4.3 %all-to-all-start.1 = ((f32[2,2,1,128,256]{4,3,2,1,0:T(8,128)}), f32[2,2,1,128,256]{4,3,2,1,0:T(8,128)S(1)}, u32[]{:S(2)}, u32[]{:S(2)}) async-start(f32[2,2,1,128,256]{4,3,2,1,0:T(8,128)} %maximum_bitcast_fusion.1), calls=%async_computation.1 | async-start | bytes 1048576 | tf_op jit(solution)/shard_map/all_to_all | solution.py:32
  168.5 0.1 copy.65
  168.6 0.1 copy.64
  168.8 8.7 %all-to-all-done.1 = f32[2,2,1,128,256]{4,3,2,1,0:T(8,128)S(1)} async-done(((f32[2,2,1,128,256]{4,3,2,1,0:T(8,128)}), f32[2,2,1,128,256]{4,3,2,1,0:T(8,128)S(1)}, u32[]{:S(2)}, u32[]{:S(2)}) %all-to-all-start.1) | async-done | bytes 524320 | tf_op jit(solution)/shard_map/all_to_all | solution.py:32
  177.5 1.2 fusion.7
  178.7 0.7 pad_maximum_fusion
  (12 shorter events, 0.2 us)
Async XLA Ops:
  6.5 19.1 %copy-start = (f32[2,1,128,512]{3,2,1,0:T(8,128)S(1)}, f32[2,1,128,512]{3,2,1,0:T(8,128)}, u32[]{:S(2)}) copy-start(f32[2,1,128,512]{3,2,1,0:T(8,128)} %param.4) | copy-start | bytes 1572868
  6.5 135.5 %all-gather.3.cloned.1.call-start = ((), (), s32[]{:S(2)}) async-start(), calls=%async_computation.2 | async-start | bytes 8650752 | tf_op jit(solution)/shard_map/all_gather | solution.py:93
  8.4 12.6 %collective-permute-start.3 = (f32[2,1,128,128]{2,3,0,1:T(8,128)S(1)}, f32[2,1,128,128]{2,3,0,1:T(8,128)S(1)}, u32[]{:S(2)}, u32[]{:S(2)}) collective-permute-start(f32[2,1,128,128]{2,3,0,1:T(8,128)S(1)} %bitcast.96), channel_id=1, source_target_pairs={{16,0},{32,16},{48,32},{64,50},{80,2},{82,66},{96,18},{98,82},{112... | collective-permute-start | bytes 393224 | tf_op jit(solution)/shard_map/ppermute | solution.py:64
  17.3 7.1 %collective-permute-start.2 = (f32[2,1,128,128]{2,3,0,1:T(8,128)S(1)}, f32[2,1,128,128]{2,3,0,1:T(8,128)S(1)}, u32[]{:S(2)}, u32[]{:S(2)}) collective-permute-start(f32[2,1,128,128]{2,3,0,1:T(8,128)S(1)} %bitcast.97), channel_id=1, source_target_pairs={{32,0},{48,16},{64,34},{80,50},{96,2},{98,66},{112,18},{114,82},{1... | collective-permute-start | bytes 393224 | tf_op jit(solution)/shard_map/ppermute | solution.py:64
  18.7 5.7 %collective-permute-start.1 = (f32[2,1,128,128]{2,3,0,1:T(8,128)S(1)}, f32[2,1,128,128]{2,3,0,1:T(8,128)S(1)}, u32[]{:S(2)}, u32[]{:S(2)}) collective-permute-start(f32[2,1,128,128]{2,3,0,1:T(8,128)S(1)} %bitcast.98), channel_id=1, source_target_pairs={{48,0},{64,18},{80,34},{96,50},{112,2},{114,66},{128,20},{130,84},... | collective-permute-start | bytes 393224 | tf_op jit(solution)/shard_map/ppermute | solution.py:64
  19.5 4.9 %collective-permute-start = (f32[2,1,128,128]{2,3,0,1:T(8,128)S(1)}, f32[2,1,128,128]{2,3,0,1:T(8,128)S(1)}, u32[]{:S(2)}, u32[]{:S(2)}) collective-permute-start(f32[2,1,128,128]{2,3,0,1:T(8,128)S(1)} %bitcast.99), channel_id=1, source_target_pairs={{64,2},{80,18},{96,34},{112,50},{128,4},{130,68},{144,20},{146,84}... | collective-permute-start | bytes 393224 | tf_op jit(solution)/shard_map/ppermute | solution.py:64
  26.6 49.6 %copy-start.1 = (f32[2,1]{0,1:T(1,128)S(1)}, f32[2,1]{0,1:T(1,128)}, u32[]{:S(2)}) copy-start(f32[2,1]{0,1:T(1,128)} %param.7) | copy-start | bytes 28
  26.6 50.2 %copy-start.2 = (s32[1,24]{1,0:T(1,128)S(1)}, s32[1,24]{1,0:T(1,128)}, u32[]{:S(2)}) copy-start(s32[1,24]{1,0:T(1,128)} %param.6) | copy-start | bytes 292
  28.5 98.7 %all-to-all-start = ((f32[8,2,1,128,256]{3,4,1,2,0:T(8,128)}), f32[8,2,1,128,256]{3,4,1,2,0:T(8,128)S(1)}, u32[]{:S(2)}, u32[]{:S(2)}) async-start(f32[8,2,1,128,256]{3,4,1,2,0:T(8,128)} %broadcast_in_dim.63), calls=%async_computation | async-start | bytes 4194304 | tf_op jit(solution)/shard_map/all_to_all | solution.py:11
  164.1 13.4 %all-to-all-start.1 = ((f32[2,2,1,128,256]{4,3,2,1,0:T(8,128)}), f32[2,2,1,128,256]{4,3,2,1,0:T(8,128)S(1)}, u32[]{:S(2)}, u32[]{:S(2)}) async-start(f32[2,2,1,128,256]{4,3,2,1,0:T(8,128)} %maximum_bitcast_fusion.1), calls=%async_computation.1 | async-start | bytes 1048576 | tf_op jit(solution)/shard_map/all_to_all | solution.py:32
Sparse Core Ops, SparseCore 0:
  26.5 115.5 all-gather.2

commit v4 on v3

--- a/solution.py
+++ b/solution.py
@@ -91,11 +91,19 @@
         comp_count, freq_count, local_rows, block_count * half_tile
     )
     slab_piece = lax.all_gather(right_half, "src", axis=2, tiled=True)
-    real_part = complex_prod(weighted[0], slab_piece[0]) - complex_prod(weighted[1], slab_piece[1])
-    imag_part = complex_prod(weighted[0], slab_piece[1]) + complex_prod(weighted[1], slab_piece[0])
-    partial_sum = jnp.stack([real_part, imag_part])
     out_cols = local_cols // half_count
-    my_share = sent_and_summed(partial_sum, "int", 3)
+    assert half_count == 2
+
+    def half_product(which):
+        cols = slab_piece.reshape(comp_count, freq_count, -1, half_count, out_cols)
+        cols = lax.dynamic_index_in_dim(cols, which, 3, keepdims=False)
+        real_part = complex_prod(weighted[0], cols[0]) - complex_prod(weighted[1], cols[1])
+        imag_part = complex_prod(weighted[0], cols[1]) + complex_prod(weighted[1], cols[0])
+        return jnp.stack([real_part, imag_part])
+
+    sent = half_product(1 - my_half)
+    got = lax.ppermute(sent, "int", [(0, 1), (1, 0)])
+    my_share = half_product(my_half) + got
     kept_data = filled.reshape(comp_count, freq_count, local_rows, half_count, out_cols)
     kept_data = lax.dynamic_index_in_dim(kept_data, my_half, 3, keepdims=False)
     w_real = wavelet[0][:, None, None]

time: 187 us -> 197 us (1.053)
  local copies, waits for them, and re-layouts: 8.86 us -> 31 us
  waiting for transfers between devices: 76.7 us -> 69.7 us
  matrix products: 19.2 us -> 14.9 us
    slice x1 -> x2, local copies, waits for them, and re-layouts: 0.24 us -> 12.3 us  [the longest x1 12.1 us: half_product(): cols[0]]
    reshape x0 -> x1, local copies, waits for them, and re-layouts: none -> 10.5 us  [half_product(): cols = slab_piece.reshape(comp_count, freq_count, -1, half_count, out_cols)]
    all_to_all x1 -> x0, waiting for transfers between devices: 8.69 us -> none  [sent_and_summed(): lax.all_to_all(pieces, axis, split_axis=0, concat_axis=0, tiled=True)]
    all_to_all x1, waiting for transfers between devices: 50.3 us -> 45.4 us  [from_everyone(): return lax.all_to_all(copies, axis, split_axis=0, concat_axis=0, tiled=True)]
    ppermute x0 -> x1, starting transfers between devices: none -> 4.82 us  [per_device(): got = lax.ppermute(sent, 'int', [(0, 1), (1, 0)])]
    all_to_all x1 -> x0, starting transfers between devices: 4.31 us -> none  [sent_and_summed(): lax.all_to_all(pieces, axis, split_axis=0, concat_axis=0, tiled=True)]
    dot_general x4 -> x8, matrix products: 19.2 us -> 14.9 us  [complex_prod(): jnp.einsum('fik,fkj->fij', left_side, right_side, precision=lax.Precision...]
    ppermute x0 -> x1, waiting for transfers between devices: none -> 2.48 us  [per_device(): got = lax.ppermute(sent, 'int', [(0, 1), (1, 0)])]
  transfers between devices with their start and end apart: 7 -> 7, of which waited for: 4 -> 4; matrix products, arithmetic and copies ran while one was open for 3% -> 5% of each run, Pallas kernels for 0% -> 0%
where the time goes in v4:
time: 197 us
  waiting for transfers between devices  69.7 us (35%)
  starting transfers between devices  64.1 us (33%)
  local copies, waits for them, and re-layouts  31 us (16%)
  matrix products  14.9 us (8%)
  between operations  13.8 us (7%)
  other arithmetic  3.33 us (2%)
    all_to_all x1, starting transfers between devices, from_everyone(): return lax.all_to_all(copies, axis, split_axis=0, concat_axis=0, tiled=True)  47.8 us
    all_to_all x1, waiting for transfers between devices, from_everyone(): return lax.all_to_all(copies, axis, split_axis=0, concat_axis=0, tiled=True)  45.4 us
    all_gather x1, waiting for transfers between devices, per_device(): slab_piece = lax.all_gather(right_half, 'src', axis=2, tiled=True)  16.3 us
    dot_general x8, matrix products, complex_prod(): jnp.einsum('fik,fkj->fij', left_side, right_side, precision=lax.Precision...  14.9 us
    slice x1, local copies, waits for them, and re-layouts, half_product(): cols[0]  12.1 us
    ppermute x4, starting transfers between devices, per_device(): lax.ppermute(sent, ('src', 'rcv'), mirror_pairs(src_count, rcv_count, per...  11.4 us
    reshape x1, local copies, waits for them, and re-layouts, half_product(): cols = slab_piece.reshape(comp_count, freq_count, -1, half_count, out_cols)  10.5 us
    ppermute x4, waiting for transfers between devices, per_device(): lax.ppermute(sent, ('src', 'rcv'), mirror_pairs(src_count, rcv_count, per...  5.54 us
  transfers between devices with their start and end apart: 7, of which 4 were waited for; matrix products, arithmetic and copies ran while one was open for 5% of the time, Pallas kernels for 0%

profile of v4, /device:TPU:1, one launch (start us, length us, event | category | flops | bytes accessed | tf_op | source)
XLA Modules:
  0.0 196.7 jit_solution(8965229386990329958)
XLA Ops:
  6.5 0.0 copy-start.2
  6.5 0.0 all-gather.3.cloned.1.call-start
  6.5 1.2 reshape.329
  7.8 0.5 constant_dynamic-slice_fusion.11
  8.2 0.1 copy.58
  8.4 8.8 %collective-permute-start.3 = (f32[2,1,128,128]{2,3,0,1:T(8,128)S(1)}, f32[2,1,128,128]{2,3,0,1:T(8,128)S(1)}, u32[]{:S(2)}, u32[]{:S(2)}) collective-permute-start(f32[2,1,128,128]{2,3,0,1:T(8,128)S(1)} %bitcast.134), channel_id=1, source_target_pairs={{16,0},{32,16},{48,32},{64,50},{80,2},{82,66},{96,18},{98,82},{112... | collective-permute-start | bytes 393224 | tf_op jit(solution)/shard_map/ppermute | solution.py:64
  17.1 0.1 copy.55
  17.2 0.7 collective-permute-start
  17.9 0.1 copy.56
  18.0 0.7 collective-permute-start.1
  18.7 0.1 copy.57
  18.8 1.3 collective-permute-start.2
  20.1 0.0 copy-done.2
  20.2 0.1 broadcast_bitcast_fusion.2
  20.3 0.0 collective-permute-done.3
  20.3 0.0 collective-permute-done
  20.3 0.0 collective-permute-done.1
  20.3 5.5 %collective-permute-done.2 = f32[2,1,128,128]{2,3,0,1:T(8,128)S(1)} collective-permute-done((f32[2,1,128,128]{2,3,0,1:T(8,128)S(1)}, f32[2,1,128,128]{2,3,0,1:T(8,128)S(1)}, u32[]{:S(2)}, u32[]{:S(2)}) %collective-permute-start.2) | collective-permute-done | bytes 131104 | tf_op jit(solution)/shard_map/ppermute | solution.py:64
  25.8 0.0 copy-start
  25.9 0.6 gather_fusion
  26.5 0.3 copy.50
  26.8 0.2 gather.13
  27.0 0.0 copy-done
  27.0 0.8 dynamic-slice_select_fusion
  27.8 0.0 all-gather.3.cloned.1.call-update
  27.8 0.2 copy.45
  28.0 0.2 copy.43
  28.2 0.1 dynamic-slice_select_fusion.2
  28.3 1.6 broadcast_in_dim.63
  29.9 0.0 copy-start.1
  29.9 0.0 copy-start.3
  29.9 47.8 %all-to-all-start = ((f32[8,2,1,128,256]{3,4,1,2,0:T(8,128)}), f32[8,2,1,128,256]{3,4,1,2,0:T(8,128)S(1)}, u32[]{:S(2)}, u32[]{:S(2)}) async-start(f32[8,2,1,128,256]{3,4,1,2,0:T(8,128)} %broadcast_in_dim.63), calls=%async_computation | async-start | bytes 4194304 | tf_op jit(solution)/shard_map/all_to_all | solution.py:11
  77.8 0.1 broadcast_bitcast_fusion
  77.9 0.1 gt.15
  78.0 0.1 broadcast_bitcast_fusion.1
  78.1 0.0 copy-done.1
  78.1 0.6 fusion.55
  78.6 0.0 copy-done.3
  78.6 0.1 convert_reduce_fusion
  78.7 0.7 constant_dynamic-slice_fusion.3
  79.5 1.1 copy.59
  80.6 0.1 copy.60
  80.7 45.4 %all-to-all-done = f32[8,2,1,128,256]{3,4,1,2,0:T(8,128)S(1)} async-done(((f32[8,2,1,128,256]{3,4,1,2,0:T(8,128)}), f32[8,2,1,128,256]{3,4,1,2,0:T(8,128)S(1)}, u32[]{:S(2)}, u32[]{:S(2)}) %all-to-all-start) | async-done | bytes 2097184 | tf_op jit(solution)/shard_map/all_to_all | solution.py:11
  126.1 0.2 copy.49
  126.3 0.2 broadcast_multiply_fusion
  126.5 0.2 fusion.54
  126.7 16.3 %all-gather.3.cloned.1.call-done = f32[2,1,1,1,2048,512]{5,4,3,0,2,1:T(8,128)} async-done(((f32[2,1,1,1,64,512]{5,4,3,0,2,1:T(8,128)}), f32[2,1,1,1,2048,512]{5,4,3,0,2,1:T(8,128)}) %all-gather.3.cloned.1.call-update) | async-done | bytes 8388624 | tf_op jit(solution)/shard_map/all_gather | solution.py:93
  143.0 10.5 %reshape.336 = f32[2,1,2048,2,256]{4,3,2,0,1:T(2,128)} reshape(f32[2,1,1,1,2048,512]{5,4,3,0,2,1:T(8,128)} %all-gather.3.cloned.1.call-done) | data formatting | bytes 16777216 | tf_op jit(solution)/shard_map/reshape | solution.py:98
  153.5 12.1 %constant_dynamic-slice_fusion = (f32[1,1,2048,1,256]{4,3,2,0,1:T(1,128)S(1)}, f32[1,1,2048,1,256]{4,3,2,0,1:T(1,128)S(1)}, f32[1,1,2048,1,256]{4,3,2,0,1:T(1,128)S(1)}, f32[1,1,2048,1,256]{4,3,2,0,1:T(1,128)S(1)}) fusion(f32[2,1,2048,2,256]{4,3,2,0,1:T(2,128)} %reshape.336, s32[]{:T(128)S(6)} %select_n.173, s32[]{:T(128)S(6)} %select_n.180, s32[]{:T(128)S(6)} %add.138), kind=kLoop, calls=%fused_computation.50 | loop fusion | bytes 16777228 | tf_op jit(solution)/shard_map/slice | solution.py:100
  165.6 1.9 fusion.10
  167.5 1.9 fusion.8
  169.3 1.9 fusion.2
  171.2 1.9 fusion
  173.1 1.9 fusion.39
  174.9 1.9 fusion.45
  176.8 4.8 %collective-permute-start.4 = (f32[2,1,128,256]{3,2,1,0:T(8,128)S(1)}, f32[2,1,128,256]{3,2,1,0:T(8,128)S(1)}, u32[]{:S(2)}, u32[]{:S(2)}) collective-permute-start(f32[2,1,128,256]{3,2,1,0:T(8,128)S(1)} %pad_maximum_fusion), channel_id=1, source_target_pairs={{0,1},{1,0},{2,3},{3,2},{4,5},{5,4},{6,7},{7,6},{8,9},{9,8},{10,11... | collective-permute-start | bytes 786440 | tf_op jit(solution)/shard_map/ppermute | solution.py:105
  181.7 1.9 fusion.27
  183.5 1.9 fusion.33
  185.4 2.5 %collective-permute-done.4 = f32[2,1,128,256]{3,2,1,0:T(8,128)S(1)} collective-permute-done((f32[2,1,128,256]{3,2,1,0:T(8,128)S(1)}, f32[2,1,128,256]{3,2,1,0:T(8,128)S(1)}, u32[]{:S(2)}, u32[]{:S(2)}) %collective-permute-start.4) | collective-permute-done | bytes 262176 | tf_op jit(solution)/shard_map/ppermute | solution.py:105
  187.9 1.3 fusion.49
  189.2 0.7 pad_maximum_fusion.1
  (12 shorter events, 0.2 us)
Async XLA Ops:
  6.5 13.6 %copy-start.2 = (s32[1,4]{1,0:T(1,128)S(1)}, s32[1,4]{1,0:T(1,128)}, u32[]{:S(2)}) copy-start(s32[1,4]{1,0:T(1,128)} %param.5) | copy-start | bytes 52
  6.5 136.5 %all-gather.3.cloned.1.call-start = ((), (), s32[]{:S(2)}) async-start(), calls=%async_computation.1 | async-start | bytes 8650752 | tf_op jit(solution)/shard_map/all_gather | solution.py:93
  8.4 11.9 %collective-permute-start.3 = (f32[2,1,128,128]{2,3,0,1:T(8,128)S(1)}, f32[2,1,128,128]{2,3,0,1:T(8,128)S(1)}, u32[]{:S(2)}, u32[]{:S(2)}) collective-permute-start(f32[2,1,128,128]{2,3,0,1:T(8,128)S(1)} %bitcast.134), channel_id=1, source_target_pairs={{16,0},{32,16},{48,32},{64,50},{80,2},{82,66},{96,18},{98,82},{112... | collective-permute-start | bytes 393224 | tf_op jit(solution)/shard_map/ppermute | solution.py:64
  17.2 3.0 %collective-permute-start = (f32[2,1,128,128]{2,3,0,1:T(8,128)S(1)}, f32[2,1,128,128]{2,3,0,1:T(8,128)S(1)}, u32[]{:S(2)}, u32[]{:S(2)}) collective-permute-start(f32[2,1,128,128]{2,3,0,1:T(8,128)S(1)} %bitcast.135), channel_id=1, source_target_pairs={{64,2},{80,18},{96,34},{112,50},{128,4},{130,68},{144,20},{146,84}... | collective-permute-start | bytes 393224 | tf_op jit(solution)/shard_map/ppermute | solution.py:64
  18.0 2.3 %collective-permute-start.1 = (f32[2,1,128,128]{2,3,0,1:T(8,128)S(1)}, f32[2,1,128,128]{2,3,0,1:T(8,128)S(1)}, u32[]{:S(2)}, u32[]{:S(2)}) collective-permute-start(f32[2,1,128,128]{2,3,0,1:T(8,128)S(1)} %bitcast.136), channel_id=1, source_target_pairs={{48,0},{64,18},{80,34},{96,50},{112,2},{114,66},{128,20},{130,84},... | collective-permute-start | bytes 393224 | tf_op jit(solution)/shard_map/ppermute | solution.py:64
  18.8 7.0 %collective-permute-start.2 = (f32[2,1,128,128]{2,3,0,1:T(8,128)S(1)}, f32[2,1,128,128]{2,3,0,1:T(8,128)S(1)}, u32[]{:S(2)}, u32[]{:S(2)}) collective-permute-start(f32[2,1,128,128]{2,3,0,1:T(8,128)S(1)} %bitcast.137), channel_id=1, source_target_pairs={{32,0},{48,16},{64,34},{80,50},{96,2},{98,66},{112,18},{114,82},{1... | collective-permute-start | bytes 393224 | tf_op jit(solution)/shard_map/ppermute | solution.py:64
  25.8 1.2 copy-start
  29.9 48.1 %copy-start.1 = (f32[2,1]{0,1:T(1,128)S(1)}, f32[2,1]{0,1:T(1,128)}, u32[]{:S(2)}) copy-start(f32[2,1]{0,1:T(1,128)} %param.7) | copy-start | bytes 28
  29.9 48.7 %copy-start.3 = (s32[1,24]{1,0:T(1,128)S(1)}, s32[1,24]{1,0:T(1,128)}, u32[]{:S(2)}) copy-start(s32[1,24]{1,0:T(1,128)} %param.6) | copy-start | bytes 292
  29.9 96.2 %all-to-all-start = ((f32[8,2,1,128,256]{3,4,1,2,0:T(8,128)}), f32[8,2,1,128,256]{3,4,1,2,0:T(8,128)S(1)}, u32[]{:S(2)}, u32[]{:S(2)}) async-start(f32[8,2,1,128,256]{3,4,1,2,0:T(8,128)} %broadcast_in_dim.63), calls=%async_computation | async-start | bytes 4194304 | tf_op jit(solution)/shard_map/all_to_all | solution.py:11
  176.8 11.0 %collective-permute-start.4 = (f32[2,1,128,256]{3,2,1,0:T(8,128)S(1)}, f32[2,1,128,256]{3,2,1,0:T(8,128)S(1)}, u32[]{:S(2)}, u32[]{:S(2)}) collective-permute-start(f32[2,1,128,256]{3,2,1,0:T(8,128)S(1)} %pad_maximum_fusion), channel_id=1, source_target_pairs={{0,1},{1,0},{2,3},{3,2},{4,5},{5,4},{6,7},{7,6},{8,9},{9,8},{10,11... | collective-permute-start | bytes 786440 | tf_op jit(solution)/shard_map/ppermute | solution.py:105
Sparse Core Ops, SparseCore 0:
  27.9 115.0 all-gather.2

commit v5 on v4

--- a/solution.py
+++ b/solution.py
@@ -74,11 +74,11 @@
     left_half = filled.reshape(comp_count, freq_count, local_rows, col_tiles, half_count, half_tile)
     left_half = lax.dynamic_index_in_dim(left_half, my_half, 4, keepdims=False)
     left_half = left_half.reshape(comp_count, freq_count, local_rows, col_tiles * half_tile)
-    right_half = filled.reshape(
-        comp_count, freq_count, row_tiles, half_count, half_tile, local_cols
-    )
+    out_cols = local_cols // half_count
+    right_half = filled.reshape(comp_count, freq_count, row_tiles, half_count, half_tile, half_count, out_cols)
     right_half = lax.dynamic_index_in_dim(right_half, my_half, 3, keepdims=False)
-    right_half = right_half.reshape(comp_count, freq_count, row_tiles * half_tile, local_cols)
+    right_half = jnp.transpose(right_half, (4, 0, 1, 2, 3, 5))
+    right_half = right_half.reshape(half_count, comp_count, freq_count, row_tiles * half_tile, out_cols)
     gathered = collect(left_half, "rcv", 3)
     block_count = gathered.shape[3] // half_tile
     chosen = (
@@ -90,13 +90,11 @@
     weighted = (weighted * chosen[None, None, :, None, :, None]).reshape(
         comp_count, freq_count, local_rows, block_count * half_tile
     )
-    slab_piece = lax.all_gather(right_half, "src", axis=2, tiled=True)
-    out_cols = local_cols // half_count
     assert half_count == 2
 
     def half_product(which):
-        cols = slab_piece.reshape(comp_count, freq_count, -1, half_count, out_cols)
-        cols = lax.dynamic_index_in_dim(cols, which, 3, keepdims=False)
+        piece = lax.dynamic_index_in_dim(right_half, which, 0, keepdims=False)
+        cols = lax.all_gather(piece, "src", axis=2, tiled=True)
         real_part = complex_prod(weighted[0], cols[0]) - complex_prod(weighted[1], cols[1])
         imag_part = complex_prod(weighted[0], cols[1]) + complex_prod(weighted[1], cols[0])
         return jnp.stack([real_part, imag_part])

time: 197 us -> 242 us (1.23)
  waiting for transfers between devices: 69.7 us -> 126 us
  local copies, waits for them, and re-layouts: 31 us -> 20.5 us
    all_gather x1 -> x2, waiting for transfers between devices: 16.3 us -> 70.3 us  [half_product(): cols = lax.all_gather(piece, 'src', axis=2, tiled=True)]
    reshape x1 -> x0, local copies, waits for them, and re-layouts: 10.5 us -> none  [half_product(): cols = slab_piece.reshape(comp_count, freq_count, -1, half_count, out_cols)]
    all_to_all x1, waiting for transfers between devices: 45.4 us -> 48.6 us  [from_everyone(): return lax.all_to_all(copies, axis, split_axis=0, concat_axis=0, tiled=True)]
    slice x1 -> x2, local copies, waits for them, and re-layouts: 12.1 us -> 10.5 us  [half_product(): cols[0]]
  transfers between devices with their start and end apart: 7 -> 8, of which waited for: 4 -> 5; matrix products, arithmetic and copies ran while one was open for 5% -> 8% of each run, Pallas kernels for 0% -> 0%
where the time goes in v5:
time: 242 us
  waiting for transfers between devices  126 us (52%)
  starting transfers between devices  63.3 us (26%)
  local copies, waits for them, and re-layouts  20.5 us (8%)
  matrix products  15.1 us (6%)
  between operations  13.8 us (6%)
  other arithmetic  2.92 us (1%)
    all_gather x2, waiting for transfers between devices, half_product(): cols = lax.all_gather(piece, 'src', axis=2, tiled=True)  70.3 us
    all_to_all x1, waiting for transfers between devices, from_everyone(): return lax.all_to_all(copies, axis, split_axis=0, concat_axis=0, tiled=True)  48.6 us
    all_to_all x1, starting transfers between devices, from_everyone(): return lax.all_to_all(copies, axis, split_axis=0, concat_axis=0, tiled=True)  47.5 us
    dot_general x8, matrix products, complex_prod(): jnp.einsum('fik,fkj->fij', left_side, right_side, precision=lax.Precision...  15.1 us
    ppermute x4, starting transfers between devices, per_device(): lax.ppermute(sent, ('src', 'rcv'), mirror_pairs(src_count, rcv_count, per...  11.4 us
    slice x2, local copies, waits for them, and re-layouts, half_product(): cols[0]  10.5 us
  transfers between devices with their start and end apart: 8, of which 5 were waited for; matrix products, arithmetic and copies ran while one was open for 8% of the time, Pallas kernels for 0%

profile of v5, /device:TPU:1, one launch (start us, length us, event | category | flops | bytes accessed | tf_op | source)
XLA Modules:
  0.0 241.7 jit_solution(11651914283931169607)
XLA Ops:
  6.5 0.0 copy-start.1
  6.5 0.0 all-gather.7.cloned.1.call-start
  6.5 1.3 reshape.331
  7.8 0.5 constant_dynamic-slice_fusion.9
  8.3 0.1 copy.58
  8.4 8.8 %collective-permute-start.3 = (f32[2,1,128,128]{2,3,0,1:T(8,128)S(1)}, f32[2,1,128,128]{2,3,0,1:T(8,128)S(1)}, u32[]{:S(2)}, u32[]{:S(2)}) collective-permute-start(f32[2,1,128,128]{2,3,0,1:T(8,128)S(1)} %bitcast.126), channel_id=1, source_target_pairs={{16,0},{32,16},{48,32},{64,50},{80,2},{82,66},{96,18},{98,82},{112... | collective-permute-start | bytes 393224 | tf_op jit(solution)/shard_map/ppermute | solution.py:64
  17.2 0.1 copy.57
  17.3 1.3 collective-permute-start.2
  18.6 0.1 copy.56
  18.7 0.7 collective-permute-start.1
  19.4 0.1 copy.55
  19.5 0.7 collective-permute-start
  20.2 0.0 copy-done.3
  20.2 0.1 gt.15
  20.3 0.1 broadcast_bitcast_fusion.1
  20.4 0.1 broadcast_bitcast_fusion
  20.5 0.0 copy-done.1
  20.5 0.3 reshape.336
  20.9 0.0 collective-permute-done.3
  20.9 3.5 %collective-permute-done.2 = f32[2,1,128,128]{2,3,0,1:T(8,128)S(1)} collective-permute-done((f32[2,1,128,128]{2,3,0,1:T(8,128)S(1)}, f32[2,1,128,128]{2,3,0,1:T(8,128)S(1)}, u32[]{:S(2)}, u32[]{:S(2)}) %collective-permute-start.2) | collective-permute-done | bytes 131104 | tf_op jit(solution)/shard_map/ppermute | solution.py:64
  24.4 0.0 collective-permute-done.1
  24.4 0.0 collective-permute-done
  24.5 0.6 gather_fusion
  25.0 0.3 copy.50
  25.4 0.5 gather.13
  25.8 0.3 select_select_fusion
  26.2 1.0 constant_dynamic-slice_fusion.4
  27.1 0.0 all-gather.7.cloned.1.call-update
  27.2 0.0 all-gather.5.cloned.1.call-start
  27.2 0.7 all-gather.5.cloned.1.call-update
  27.9 0.2 copy.45
  28.1 0.2 copy.43
  28.3 0.1 dynamic-slice_select_fusion
  28.5 1.6 broadcast_in_dim.55
  30.1 47.5 %all-to-all-start = ((f32[8,2,1,128,256]{3,4,1,2,0:T(8,128)}), f32[8,2,1,128,256]{3,4,1,2,0:T(8,128)S(1)}, u32[]{:S(2)}, u32[]{:S(2)}) async-start(f32[8,2,1,128,256]{3,4,1,2,0:T(8,128)} %broadcast_in_dim.55), calls=%async_computation | async-start | bytes 4194304 | tf_op jit(solution)/shard_map/all_to_all | solution.py:11
  77.6 0.0 copy-done.2
  77.6 0.6 fusion.57
  78.2 0.0 copy-done.4
  78.2 0.1 convert_reduce_fusion
  78.3 0.7 constant_dynamic-slice_fusion.1
  79.0 1.1 copy.60
  80.1 0.1 copy.59
  80.3 48.6 %all-to-all-done = f32[8,2,1,128,256]{3,4,1,2,0:T(8,128)S(1)} async-done(((f32[8,2,1,128,256]{3,4,1,2,0:T(8,128)}), f32[8,2,1,128,256]{3,4,1,2,0:T(8,128)S(1)}, u32[]{:S(2)}, u32[]{:S(2)}) %all-to-all-start) | async-done | bytes 2097184 | tf_op jit(solution)/shard_map/all_to_all | solution.py:11
  128.9 0.2 copy.49
  129.0 0.2 broadcast_multiply_fusion
  129.2 0.2 fusion.56
  129.5 8.0 %all-gather.7.cloned.1.call-done = f32[2,1,1,1,2048,1,256]{6,5,4,3,0,2,1:T(1,128)} async-done(((f32[2,1,1,1,64,1,256]{6,5,4,3,0,2,1:T(1,128)}), f32[2,1,1,1,2048,1,256]{6,5,4,3,0,2,1:T(1,128)}) %all-gather.7.cloned.1.call-update) | async-done | bytes 4194320 | tf_op jit(solution)/shard_map/all_gather | solution.py:97
  137.5 5.7 %fusion.55 = (f32[1,1,1,1,2048,1,256]{6,5,4,3,0,2,1:T(1,128)}, f32[1,1,1,1,2048,1,256]{6,5,4,3,0,2,1:T(1,128)S(1)}) fusion(f32[2,1,1,1,2048,1,256]{6,5,4,3,0,2,1:T(1,128)} %all-gather.7.cloned.1.call-done), kind=kLoop, calls=%fused_computation.84 | loop fusion | bytes 8388608 | tf_op jit(solution)/shard_map/slice | solution.py:98
  143.2 1.9 fusion
  145.1 1.9 fusion.2
  147.0 62.3 %all-gather.5.cloned.1.call-done = f32[2,1,1,1,2048,1,256]{6,5,4,3,0,2,1:T(1,128)} async-done(((f32[2,1,1,1,64,1,256]{6,5,4,3,0,2,1:T(1,128)}), f32[2,1,1,1,2048,1,256]{6,5,4,3,0,2,1:T(1,128)}) %all-gather.5.cloned.1.call-update) | async-done | bytes 4194320 | tf_op jit(solution)/shard_map/all_gather | solution.py:97
  209.2 4.9 %fusion.54 = (f32[1,1,1,1,2048,1,256]{6,5,4,3,0,2,1:T(1,128)S(1)}, f32[1,1,1,1,2048,1,256]{6,5,4,3,0,2,1:T(1,128)S(1)}) fusion(f32[2,1,1,1,2048,1,256]{6,5,4,3,0,2,1:T(1,128)} %all-gather.5.cloned.1.call-done), kind=kLoop, calls=%fused_computation.83 | loop fusion | bytes 8388608 | tf_op jit(solution)/shard_map/slice | solution.py:98
  214.1 1.9 fusion.8
  216.0 0.0 copy-start
  216.0 1.9 fusion.10
  217.9 0.0 copy-done
  217.9 1.9 fusion.45
  219.8 1.9 fusion.39
  221.7 4.4 %collective-permute-start.4 = (f32[2,1,128,256]{3,2,1,0:T(8,128)S(1)}, f32[2,1,128,256]{3,2,1,0:T(8,128)S(1)}, u32[]{:S(2)}, u32[]{:S(2)}) collective-permute-start(f32[2,1,128,256]{3,2,1,0:T(8,128)S(1)} %pad_maximum_fusion), channel_id=1, source_target_pairs={{0,1},{1,0},{2,3},{3,2},{4,5},{5,4},{6,7},{7,6},{8,9},{9,8},{10,11... | collective-permute-start | bytes 786440 | tf_op jit(solution)/shard_map/ppermute | solution.py:103
  226.1 1.9 fusion.33
  228.0 1.9 fusion.27
  229.9 2.9 %collective-permute-done.4 = f32[2,1,128,256]{3,2,1,0:T(8,128)S(1)} collective-permute-done((f32[2,1,128,256]{3,2,1,0:T(8,128)S(1)}, f32[2,1,128,256]{3,2,1,0:T(8,128)S(1)}, u32[]{:S(2)}, u32[]{:S(2)}) %collective-permute-start.4) | collective-permute-done | bytes 262176 | tf_op jit(solution)/shard_map/ppermute | solution.py:103
  232.8 1.3 fusion.49
  234.1 0.7 pad_maximum_fusion.1
  (15 shorter events, 0.2 us)
Async XLA Ops:
  6.5 13.9 %copy-start.1 = (f32[2,1,128,512]{3,2,1,0:T(8,128)S(1)}, f32[2,1,128,512]{3,2,1,0:T(8,128)}, u32[]{:S(2)}) copy-start(f32[2,1,128,512]{3,2,1,0:T(8,128)} %param.4) | copy-start | bytes 1572868
  6.5 13.7 %copy-start.3 = (s32[1,4]{1,0:T(1,128)S(1)}, s32[1,4]{1,0:T(1,128)}, u32[]{:S(2)}) copy-start(s32[1,4]{1,0:T(1,128)} %param.5) | copy-start | bytes 52
  6.5 131.0 %all-gather.7.cloned.1.call-start = ((), (), s32[]{:S(2)}) async-start(), calls=%async_computation.2 | async-start | bytes 4325376 | tf_op jit(solution)/shard_map/all_gather | solution.py:97
  8.4 12.5 %collective-permute-start.3 = (f32[2,1,128,128]{2,3,0,1:T(8,128)S(1)}, f32[2,1,128,128]{2,3,0,1:T(8,128)S(1)}, u32[]{:S(2)}, u32[]{:S(2)}) collective-permute-start(f32[2,1,128,128]{2,3,0,1:T(8,128)S(1)} %bitcast.126), channel_id=1, source_target_pairs={{16,0},{32,16},{48,32},{64,50},{80,2},{82,66},{96,18},{98,82},{112... | collective-permute-start | bytes 393224 | tf_op jit(solution)/shard_map/ppermute | solution.py:64
  17.3 7.1 %collective-permute-start.2 = (f32[2,1,128,128]{2,3,0,1:T(8,128)S(1)}, f32[2,1,128,128]{2,3,0,1:T(8,128)S(1)}, u32[]{:S(2)}, u32[]{:S(2)}) collective-permute-start(f32[2,1,128,128]{2,3,0,1:T(8,128)S(1)} %bitcast.127), channel_id=1, source_target_pairs={{32,0},{48,16},{64,34},{80,50},{96,2},{98,66},{112,18},{114,82},{1... | collective-permute-start | bytes 393224 | tf_op jit(solution)/shard_map/ppermute | solution.py:64
  18.7 5.7 %collective-permute-start.1 = (f32[2,1,128,128]{2,3,0,1:T(8,128)S(1)}, f32[2,1,128,128]{2,3,0,1:T(8,128)S(1)}, u32[]{:S(2)}, u32[]{:S(2)}) collective-permute-start(f32[2,1,128,128]{2,3,0,1:T(8,128)S(1)} %bitcast.128), channel_id=1, source_target_pairs={{48,0},{64,18},{80,34},{96,50},{112,2},{114,66},{128,20},{130,84},... | collective-permute-start | bytes 393224 | tf_op jit(solution)/shard_map/ppermute | solution.py:64
  19.5 4.9 %collective-permute-start = (f32[2,1,128,128]{2,3,0,1:T(8,128)S(1)}, f32[2,1,128,128]{2,3,0,1:T(8,128)S(1)}, u32[]{:S(2)}, u32[]{:S(2)}) collective-permute-start(f32[2,1,128,128]{2,3,0,1:T(8,128)S(1)} %bitcast.129), channel_id=1, source_target_pairs={{64,2},{80,18},{96,34},{112,50},{128,4},{130,68},{144,20},{146,84}... | collective-permute-start | bytes 393224 | tf_op jit(solution)/shard_map/ppermute | solution.py:64
  27.2 182.1 %all-gather.5.cloned.1.call-start = ((), (), s32[]{:S(2)}) async-start(), calls=%async_computation.1 | async-start | bytes 4325376 | tf_op jit(solution)/shard_map/all_gather | solution.py:97
  30.1 47.5 %copy-start.2 = (f32[2,1]{0,1:T(1,128)S(1)}, f32[2,1]{0,1:T(1,128)}, u32[]{:S(2)}) copy-start(f32[2,1]{0,1:T(1,128)} %param.7) | copy-start | bytes 28
  30.1 48.1 %copy-start.4 = (s32[1,24]{1,0:T(1,128)S(1)}, s32[1,24]{1,0:T(1,128)}, u32[]{:S(2)}) copy-start(s32[1,24]{1,0:T(1,128)} %param.6) | copy-start | bytes 292
  30.1 98.8 %all-to-all-start = ((f32[8,2,1,128,256]{3,4,1,2,0:T(8,128)}), f32[8,2,1,128,256]{3,4,1,2,0:T(8,128)S(1)}, u32[]{:S(2)}, u32[]{:S(2)}) async-start(f32[8,2,1,128,256]{3,4,1,2,0:T(8,128)} %broadcast_in_dim.55), calls=%async_computation | async-start | bytes 4194304 | tf_op jit(solution)/shard_map/all_to_all | solution.py:11
  216.0 1.9 copy-start
  221.7 11.0 %collective-permute-start.4 = (f32[2,1,128,256]{3,2,1,0:T(8,128)S(1)}, f32[2,1,128,256]{3,2,1,0:T(8,128)S(1)}, u32[]{:S(2)}, u32[]{:S(2)}) collective-permute-start(f32[2,1,128,256]{3,2,1,0:T(8,128)S(1)} %pad_maximum_fusion), channel_id=1, source_target_pairs={{0,1},{1,0},{2,3},{3,2},{4,5},{5,4},{6,7},{7,6},{8,9},{9,8},{10,11... | collective-permute-start | bytes 786440 | tf_op jit(solution)/shard_map/ppermute | solution.py:103
Sparse Core Ops, SparseCore 0:
  27.3 110.1 all-gather.6
  139.7 69.5 all-gather.4

commit v6 on v3

--- a/solution.py
+++ b/solution.py
@@ -45,7 +45,7 @@
 
 
 def complex_prod(left_side, right_side):
-    return jnp.einsum("fik,fkj->fij", left_side, right_side, precision=lax.Precision.HIGHEST)
+    return jnp.einsum("fik,fkj->fij", left_side, right_side, precision=lax.Precision.HIGH)
 
 
 def per_device(traces, missing, aperture, wavelet):

time: 187 us -> 182 us (0.973)
  matrix products: 19.2 us -> 14 us
    dot_general x4, matrix products: 19.2 us -> 14 us  [complex_prod(): jnp.einsum('fik,fkj->fij', left_side, right_side, precision=lax.Precision...]
where the time goes in v6:
time: 182 us; the launch traced here: 181 us
  waiting for transfers between devices  76.7 us (42%)
  starting transfers between devices  63.1 us (35%)
  matrix products  14 us (8%)
  between operations  13.7 us (8%)
  local copies, waits for them, and re-layouts  8.86 us (5%)
  other arithmetic  4.76 us (3%)
    all_to_all x1, waiting for transfers between devices, from_everyone(): return lax.all_to_all(copies, axis, split_axis=0, concat_axis=0, tiled=True)  50.3 us
    all_to_all x1, starting transfers between devices, from_everyone(): return lax.all_to_all(copies, axis, split_axis=0, concat_axis=0, tiled=True)  47.4 us
    all_gather x1, waiting for transfers between devices, per_device(): slab_piece = lax.all_gather(right_half, 'src', axis=2, tiled=True)  14.3 us
    dot_general x4, matrix products, complex_prod(): jnp.einsum('fik,fkj->fij', left_side, right_side, precision=lax.Precision...  14 us
    ppermute x4, starting transfers between devices, per_device(): lax.ppermute(sent, ('src', 'rcv'), mirror_pairs(src_count, rcv_count, per...  11.4 us
    all_to_all x1, waiting for transfers between devices, sent_and_summed(): lax.all_to_all(pieces, axis, split_axis=0, concat_axis=0, tiled=True)  8.68 us
    all_to_all x1, starting transfers between devices, sent_and_summed(): lax.all_to_all(pieces, axis, split_axis=0, concat_axis=0, tiled=True)  4.31 us
  transfers between devices with their start and end apart: 7, of which 4 were waited for; matrix products, arithmetic and copies ran while one was open for 3% of the time, Pallas kernels for 0%

profile of v6, /device:TPU:1, one launch (start us, length us, event | category | flops | bytes accessed | tf_op | source)
XLA Modules:
  0.0 181.1 jit_solution(6529939517453105577)
XLA Ops:
  6.5 0.0 copy-start
  6.5 0.0 all-gather.3.cloned.1.call-start
  6.5 1.3 reshape.367
  7.8 0.5 constant_dynamic-slice_fusion.7
  8.3 0.1 copy.61
  8.4 8.8 %collective-permute-start.3 = (f32[2,1,128,128]{2,3,0,1:T(8,128)S(1)}, f32[2,1,128,128]{2,3,0,1:T(8,128)S(1)}, u32[]{:S(2)}, u32[]{:S(2)}) collective-permute-start(f32[2,1,128,128]{2,3,0,1:T(8,128)S(1)} %bitcast.96), channel_id=1, source_target_pairs={{16,0},{32,16},{48,32},{64,50},{80,2},{82,66},{96,18},{98,82},{112... | collective-permute-start | bytes 393224 | tf_op jit(solution)/shard_map/ppermute | solution.py:64
  17.2 0.1 copy.60
  17.3 1.3 collective-permute-start.2
  18.6 0.1 copy.59
  18.7 0.7 collective-permute-start.1
  19.4 0.1 copy.58
  19.5 0.7 collective-permute-start
  20.2 0.7 compare_bitcast_fusion
  20.9 0.1 broadcast_bitcast_fusion.2
  21.0 0.0 collective-permute-done.3
  21.0 3.4 %collective-permute-done.2 = f32[2,1,128,128]{2,3,0,1:T(8,128)S(1)} collective-permute-done((f32[2,1,128,128]{2,3,0,1:T(8,128)S(1)}, f32[2,1,128,128]{2,3,0,1:T(8,128)S(1)}, u32[]{:S(2)}, u32[]{:S(2)}) %collective-permute-start.2) | collective-permute-done | bytes 131104 | tf_op jit(solution)/shard_map/ppermute | solution.py:64
  24.4 0.0 collective-permute-done.1
  24.4 0.0 collective-permute-done
  24.5 0.6 gather_fusion
  25.0 0.3 copy.53
  25.4 0.2 gather.13
  25.6 0.0 copy-done
  25.6 0.7 dynamic-slice_select_fusion
  26.4 0.0 all-gather.3.cloned.1.call-update
  26.4 0.2 copy.48
  26.6 0.0 copy-start.1
  26.6 0.0 copy-start.2
  26.6 0.2 copy.46
  26.8 0.1 dynamic-slice_select_fusion.2
  26.9 1.6 broadcast_in_dim.63
  28.5 47.4 %all-to-all-start = ((f32[8,2,1,128,256]{3,4,1,2,0:T(8,128)}), f32[8,2,1,128,256]{3,4,1,2,0:T(8,128)S(1)}, u32[]{:S(2)}, u32[]{:S(2)}) async-start(f32[8,2,1,128,256]{3,4,1,2,0:T(8,128)} %broadcast_in_dim.63), calls=%async_computation | async-start | bytes 4194304 | tf_op jit(solution)/shard_map/all_to_all | solution.py:11
  75.9 0.1 gt.15
  75.9 0.1 broadcast_bitcast_fusion.1
  76.0 0.1 broadcast_bitcast_fusion
  76.1 0.0 copy-done.1
  76.2 0.6 fusion.13
  76.8 0.0 copy-done.2
  76.8 0.1 convert_reduce_fusion
  76.8 50.3 %all-to-all-done = f32[8,2,1,128,256]{3,4,1,2,0:T(8,128)S(1)} async-done(((f32[8,2,1,128,256]{3,4,1,2,0:T(8,128)}), f32[8,2,1,128,256]{3,4,1,2,0:T(8,128)S(1)}, u32[]{:S(2)}, u32[]{:S(2)}) %all-to-all-start) | async-done | bytes 2097184 | tf_op jit(solution)/shard_map/all_to_all | solution.py:11
  127.2 0.2 copy.52
  127.3 0.2 broadcast_multiply_fusion
  127.5 0.2 fusion.12
  127.8 14.3 %all-gather.3.cloned.1.call-done = f32[2,1,1,1,2048,512]{5,4,3,0,2,1:T(8,128)} async-done(((f32[2,1,1,1,64,512]{5,4,3,0,2,1:T(8,128)}), f32[2,1,1,1,2048,512]{5,4,3,0,2,1:T(8,128)}) %all-gather.3.cloned.1.call-update) | async-done | bytes 8388624 | tf_op jit(solution)/shard_map/all_gather | solution.py:93
  142.1 3.5 %fusion = f32[128,512]{1,0:T(8,128)S(1)} fusion(f32[128,2048]{0,1:T(8,128)S(1)} %bitcast.83, f32[2,1,1,1,2048,512]{5,4,3,0,2,1:T(8,128)} %all-gather.3.cloned.1.call-done), kind=kOutput, calls=%fused_computation.3 | convolution fusion | flops 805306368 | bytes 5505024 | tf_op jit(solution)/shard_map/fik,fkj->fij/dot_general | solution.py:48
  145.6 3.5 %fusion.5 = f32[128,512]{1,0:T(8,128)S(1)} fusion(f32[128,512]{1,0:T(8,128)S(1)} %fusion, f32[128,2048]{0,1:T(8,128)S(1)} %bitcast.85, f32[2,1,1,1,2048,512]{5,4,3,0,2,1:T(8,128)} %all-gather.3.cloned.1.call-done), kind=kOutput, calls=%fused_computation.8 | convolution fusion | flops 805371904 | bytes 5767168 | tf_op jit(solution)/shard_map/fik,fkj->fij/dot_general | solution.py:48
  149.1 0.9 stack.35
  149.9 1.0 copy.55
  150.9 3.5 %fusion.1 = f32[128,512]{1,0:T(8,128)S(1)} fusion(f32[128,2048]{0,1:T(8,128)S(1)} %bitcast.86, f32[2,1,1,1,2048,512]{5,4,3,0,2,1:T(8,128)} %all-gather.3.cloned.1.call-done), kind=kOutput, calls=%fused_computation.4 | convolution fusion | flops 805306368 | bytes 5505024 | tf_op jit(solution)/shard_map/fik,fkj->fij/dot_general | solution.py:48
  154.4 3.5 %fusion.4 = f32[128,512]{1,0:T(8,128)S(1)} fusion(f32[128,512]{1,0:T(8,128)S(1)} %fusion.1, f32[128,2048]{0,1:T(8,128)S(1)} %bitcast.84, f32[2,1,1,1,2048,512]{5,4,3,0,2,1:T(8,128)} %all-gather.3.cloned.1.call-done), kind=kOutput, calls=%fused_computation.7 | convolution fusion | flops 805371904 | bytes 5767168 | tf_op jit(solution)/shard_map/fik,fkj->fij/dot_general | solution.py:48
  157.9 0.2 stack.34
  158.1 0.8 maximum_bitcast_fusion.1
  158.9 4.3 %all-to-all-start.1 = ((f32[2,2,1,128,256]{4,3,2,1,0:T(8,128)}), f32[2,2,1,128,256]{4,3,2,1,0:T(8,128)S(1)}, u32[]{:S(2)}, u32[]{:S(2)}) async-start(f32[2,2,1,128,256]{4,3,2,1,0:T(8,128)} %maximum_bitcast_fusion.1), calls=%async_computation.1 | async-start | bytes 1048576 | tf_op jit(solution)/shard_map/all_to_all | solution.py:32
  163.3 0.1 copy.65
  163.4 0.1 copy.64
  163.6 8.7 %all-to-all-done.1 = f32[2,2,1,128,256]{4,3,2,1,0:T(8,128)S(1)} async-done(((f32[2,2,1,128,256]{4,3,2,1,0:T(8,128)}), f32[2,2,1,128,256]{4,3,2,1,0:T(8,128)S(1)}, u32[]{:S(2)}, u32[]{:S(2)}) %all-to-all-start.1) | async-done | bytes 524320 | tf_op jit(solution)/shard_map/all_to_all | solution.py:32
  172.3 1.2 fusion.7
  173.5 0.7 pad_maximum_fusion
  (12 shorter events, 0.2 us)
Async XLA Ops:
  6.5 19.1 %copy-start = (f32[2,1,128,512]{3,2,1,0:T(8,128)S(1)}, f32[2,1,128,512]{3,2,1,0:T(8,128)}, u32[]{:S(2)}) copy-start(f32[2,1,128,512]{3,2,1,0:T(8,128)} %param.4) | copy-start | bytes 1572868
  6.5 135.5 %all-gather.3.cloned.1.call-start = ((), (), s32[]{:S(2)}) async-start(), calls=%async_computation.2 | async-start | bytes 8650752 | tf_op jit(solution)/shard_map/all_gather | solution.py:93
  8.4 12.6 %collective-permute-start.3 = (f32[2,1,128,128]{2,3,0,1:T(8,128)S(1)}, f32[2,1,128,128]{2,3,0,1:T(8,128)S(1)}, u32[]{:S(2)}, u32[]{:S(2)}) collective-permute-start(f32[2,1,128,128]{2,3,0,1:T(8,128)S(1)} %bitcast.96), channel_id=1, source_target_pairs={{16,0},{32,16},{48,32},{64,50},{80,2},{82,66},{96,18},{98,82},{112... | collective-permute-start | bytes 393224 | tf_op jit(solution)/shard_map/ppermute | solution.py:64
  17.3 7.1 %collective-permute-start.2 = (f32[2,1,128,128]{2,3,0,1:T(8,128)S(1)}, f32[2,1,128,128]{2,3,0,1:T(8,128)S(1)}, u32[]{:S(2)}, u32[]{:S(2)}) collective-permute-start(f32[2,1,128,128]{2,3,0,1:T(8,128)S(1)} %bitcast.97), channel_id=1, source_target_pairs={{32,0},{48,16},{64,34},{80,50},{96,2},{98,66},{112,18},{114,82},{1... | collective-permute-start | bytes 393224 | tf_op jit(solution)/shard_map/ppermute | solution.py:64
  18.7 5.7 %collective-permute-start.1 = (f32[2,1,128,128]{2,3,0,1:T(8,128)S(1)}, f32[2,1,128,128]{2,3,0,1:T(8,128)S(1)}, u32[]{:S(2)}, u32[]{:S(2)}) collective-permute-start(f32[2,1,128,128]{2,3,0,1:T(8,128)S(1)} %bitcast.98), channel_id=1, source_target_pairs={{48,0},{64,18},{80,34},{96,50},{112,2},{114,66},{128,20},{130,84},... | collective-permute-start | bytes 393224 | tf_op jit(solution)/shard_map/ppermute | solution.py:64
  19.5 4.9 %collective-permute-start = (f32[2,1,128,128]{2,3,0,1:T(8,128)S(1)}, f32[2,1,128,128]{2,3,0,1:T(8,128)S(1)}, u32[]{:S(2)}, u32[]{:S(2)}) collective-permute-start(f32[2,1,128,128]{2,3,0,1:T(8,128)S(1)} %bitcast.99), channel_id=1, source_target_pairs={{64,2},{80,18},{96,34},{112,50},{128,4},{130,68},{144,20},{146,84}... | collective-permute-start | bytes 393224 | tf_op jit(solution)/shard_map/ppermute | solution.py:64
  26.6 49.6 %copy-start.1 = (f32[2,1]{0,1:T(1,128)S(1)}, f32[2,1]{0,1:T(1,128)}, u32[]{:S(2)}) copy-start(f32[2,1]{0,1:T(1,128)} %param.7) | copy-start | bytes 28
  26.6 50.2 %copy-start.2 = (s32[1,24]{1,0:T(1,128)S(1)}, s32[1,24]{1,0:T(1,128)}, u32[]{:S(2)}) copy-start(s32[1,24]{1,0:T(1,128)} %param.6) | copy-start | bytes 292
  28.5 98.7 %all-to-all-start = ((f32[8,2,1,128,256]{3,4,1,2,0:T(8,128)}), f32[8,2,1,128,256]{3,4,1,2,0:T(8,128)S(1)}, u32[]{:S(2)}, u32[]{:S(2)}) async-start(f32[8,2,1,128,256]{3,4,1,2,0:T(8,128)} %broadcast_in_dim.63), calls=%async_computation | async-start | bytes 4194304 | tf_op jit(solution)/shard_map/all_to_all | solution.py:11
  158.9 13.3 %all-to-all-start.1 = ((f32[2,2,1,128,256]{4,3,2,1,0:T(8,128)}), f32[2,2,1,128,256]{4,3,2,1,0:T(8,128)S(1)}, u32[]{:S(2)}, u32[]{:S(2)}) async-start(f32[2,2,1,128,256]{4,3,2,1,0:T(8,128)} %maximum_bitcast_fusion.1), calls=%async_computation.1 | async-start | bytes 1048576 | tf_op jit(solution)/shard_map/all_to_all | solution.py:32
Sparse Core Ops, SparseCore 0:
  26.5 115.5 all-gather.2

commit v7 on v4

--- a/solution.py
+++ b/solution.py
@@ -45,7 +45,7 @@
 
 
 def complex_prod(left_side, right_side):
-    return jnp.einsum("fik,fkj->fij", left_side, right_side, precision=lax.Precision.HIGHEST)
+    return jnp.einsum("fik,fkj->fij", left_side, right_side, precision=lax.Precision.HIGH)
 
 
 def per_device(traces, missing, aperture, wavelet):
@@ -95,8 +95,7 @@
     assert half_count == 2
 
     def half_product(which):
-        cols = slab_piece.reshape(comp_count, freq_count, -1, half_count, out_cols)
-        cols = lax.dynamic_index_in_dim(cols, which, 3, keepdims=False)
+        cols = lax.dynamic_slice_in_dim(slab_piece, which * out_cols, out_cols, axis=3)
         real_part = complex_prod(weighted[0], cols[0]) - complex_prod(weighted[1], cols[1])
         imag_part = complex_prod(weighted[0], cols[1]) + complex_prod(weighted[1], cols[0])
         return jnp.stack([real_part, imag_part])

time: 197 us -> 172 us (0.87)
  local copies, waits for them, and re-layouts: 31 us -> 8.47 us
    slice x2 -> x1, local copies, waits for them, and re-layouts: 12.3 us -> 0.24 us  [half_product(): weighted[0]]
    reshape x1 -> x0, local copies, waits for them, and re-layouts: 10.5 us -> none  [half_product(): cols = slab_piece.reshape(comp_count, freq_count, -1, half_count, out_cols)]
    all_to_all x1, waiting for transfers between devices: 45.4 us -> 48.3 us  [from_everyone(): return lax.all_to_all(copies, axis, split_axis=0, concat_axis=0, tiled=True)]
    all_gather x1, waiting for transfers between devices: 16.3 us -> 14.2 us  [per_device(): slab_piece = lax.all_gather(right_half, 'src', axis=2, tiled=True)]
  transfers between devices with their start and end apart: 7 -> 7, of which waited for: 4 -> 4; matrix products, arithmetic and copies ran while one was open for 5% -> 6% of each run, Pallas kernels for 0% -> 0%
where the time goes in v7:
time: 172 us
  waiting for transfers between devices  68.3 us (40%)
  starting transfers between devices  63.9 us (37%)
  matrix products  13.8 us (8%)
  between operations  13.7 us (8%)
  local copies, waits for them, and re-layouts  8.47 us (5%)
  other arithmetic  3.4 us (2%)
    all_to_all x1, waiting for transfers between devices, from_everyone(): return lax.all_to_all(copies, axis, split_axis=0, concat_axis=0, tiled=True)  48.3 us
    all_to_all x1, starting transfers between devices, from_everyone(): return lax.all_to_all(copies, axis, split_axis=0, concat_axis=0, tiled=True)  47.5 us
    all_gather x1, waiting for transfers between devices, per_device(): slab_piece = lax.all_gather(right_half, 'src', axis=2, tiled=True)  14.2 us
    dot_general x8, matrix products, complex_prod(): jnp.einsum('fik,fkj->fij', left_side, right_side, precision=lax.Precision...  13.8 us
    ppermute x4, starting transfers between devices, per_device(): lax.ppermute(sent, ('src', 'rcv'), mirror_pairs(src_count, rcv_count, per...  11.4 us
    ppermute x1, starting transfers between devices, per_device(): got = lax.ppermute(sent, 'int', [(0, 1), (1, 0)])  4.95 us
    ppermute x4, waiting for transfers between devices, per_device(): lax.ppermute(sent, ('src', 'rcv'), mirror_pairs(src_count, rcv_count, per...  4.08 us
  transfers between devices with their start and end apart: 7, of which 4 were waited for; matrix products, arithmetic and copies ran while one was open for 6% of the time, Pallas kernels for 0%

profile of v7, /device:TPU:1, one launch (start us, length us, event | category | flops | bytes accessed | tf_op | source)
XLA Modules:
  0.0 171.6 jit_solution(10306422470728002496)
XLA Ops:
  6.5 0.0 copy-start.3
  6.5 0.0 all-gather.3.cloned.1.call-start
  6.5 1.2 reshape.317
  7.8 0.5 constant_dynamic-slice_fusion.7
  8.2 0.1 copy.54
  8.4 8.8 %collective-permute-start.3 = (f32[2,1,128,128]{2,3,0,1:T(8,128)S(1)}, f32[2,1,128,128]{2,3,0,1:T(8,128)S(1)}, u32[]{:S(2)}, u32[]{:S(2)}) collective-permute-start(f32[2,1,128,128]{2,3,0,1:T(8,128)S(1)} %bitcast.126), channel_id=1, source_target_pairs={{16,0},{32,16},{48,32},{64,50},{80,2},{82,66},{96,18},{98,82},{112... | collective-permute-start | bytes 393224 | tf_op jit(solution)/shard_map/ppermute | solution.py:64
  17.1 0.1 copy.53
  17.2 1.3 collective-permute-start.2
  18.6 0.1 copy.52
  18.7 0.7 collective-permute-start.1
  19.3 0.1 copy.51
  19.4 0.7 collective-permute-start
  20.1 0.0 copy-done.3
  20.2 0.1 broadcast_bitcast_fusion.2
  20.3 0.0 collective-permute-done.3
  20.3 4.1 %collective-permute-done.2 = f32[2,1,128,128]{2,3,0,1:T(8,128)S(1)} collective-permute-done((f32[2,1,128,128]{2,3,0,1:T(8,128)S(1)}, f32[2,1,128,128]{2,3,0,1:T(8,128)S(1)}, u32[]{:S(2)}, u32[]{:S(2)}) %collective-permute-start.2) | collective-permute-done | bytes 131104 | tf_op jit(solution)/shard_map/ppermute | solution.py:64
  24.3 0.0 collective-permute-done.1
  24.3 0.0 collective-permute-done
  24.4 0.0 copy-start.1
  24.4 0.6 gather_fusion
  25.0 0.3 copy.50
  25.3 0.2 gather.13
  25.6 0.0 copy-done.1
  25.6 0.8 dynamic-slice_select_fusion
  26.3 0.0 all-gather.3.cloned.1.call-update
  26.4 0.2 copy.45
  26.5 0.2 copy.43
  26.8 0.1 dynamic-slice_select_fusion.2
  26.9 1.6 broadcast_in_dim.63
  28.5 0.0 copy-start.2
  28.5 0.0 copy-start.4
  28.5 47.5 %all-to-all-start = ((f32[8,2,1,128,256]{3,4,1,2,0:T(8,128)}), f32[8,2,1,128,256]{3,4,1,2,0:T(8,128)S(1)}, u32[]{:S(2)}, u32[]{:S(2)}) async-start(f32[8,2,1,128,256]{3,4,1,2,0:T(8,128)} %broadcast_in_dim.63), calls=%async_computation | async-start | bytes 4194304 | tf_op jit(solution)/shard_map/all_to_all | solution.py:11
  75.9 0.1 gt.15
  76.0 0.1 broadcast_bitcast_fusion.1
  76.1 0.1 broadcast_bitcast_fusion
  76.2 0.0 copy-done.2
  76.2 0.6 fusion.31
  76.9 0.0 copy-done.4
  76.9 0.1 convert_reduce_fusion
  77.0 0.7 constant_dynamic-slice_fusion.1
  77.7 1.1 copy.56
  78.8 0.1 copy.55
  79.0 48.3 %all-to-all-done = f32[8,2,1,128,256]{3,4,1,2,0:T(8,128)S(1)} async-done(((f32[8,2,1,128,256]{3,4,1,2,0:T(8,128)}), f32[8,2,1,128,256]{3,4,1,2,0:T(8,128)S(1)}, u32[]{:S(2)}, u32[]{:S(2)}) %all-to-all-start) | async-done | bytes 2097184 | tf_op jit(solution)/shard_map/all_to_all | solution.py:11
  127.2 0.2 copy.49
  127.4 0.2 broadcast_multiply_fusion
  127.6 0.2 fusion.30
  127.9 14.2 %all-gather.3.cloned.1.call-done = f32[2,1,1,1,2048,512]{5,4,3,0,2,1:T(8,128)} async-done(((f32[2,1,1,1,64,512]{5,4,3,0,2,1:T(8,128)}), f32[2,1,1,1,2048,512]{5,4,3,0,2,1:T(8,128)}) %all-gather.3.cloned.1.call-update) | async-done | bytes 8388624 | tf_op jit(solution)/shard_map/all_gather | solution.py:93
  142.0 0.0 copy-start
  142.0 2.7 %fusion.2 = f32[128,256]{1,0:T(8,128)S(1)} fusion(f32[128,2048]{0,1:T(8,128)S(1)} %bitcast.109, f32[2,1,1,1,2048,512]{5,4,3,0,2,1:T(8,128)} %all-gather.3.cloned.1.call-done, s32[]{:T(128)S(6)} %select_n.182), kind=kOutput, calls=%fused_computation.7 | convolution fusion | flops 402653184 | bytes 3276804 | tf_op jit(solution)/shard_map/fik,fkj->fij/dot_general | solution.py:48
  144.8 2.9 %fusion.3 = f32[128,256]{1,0:T(8,128)S(1)} fusion(f32[128,2048]{0,1:T(8,128)S(1)} %bitcast.113, f32[2,1,1,1,2048,512]{5,4,3,0,2,1:T(8,128)} %all-gather.3.cloned.1.call-done, s32[]{:T(128)S(6)} %select_n.182), kind=kOutput, calls=%fused_computation.8 | convolution fusion | flops 402653184 | bytes 3276804 | tf_op jit(solution)/shard_map/fik,fkj->fij/dot_general | solution.py:48
  147.6 2.6 %fusion.11 = f32[1,1,128,256]{3,2,1,0:T(8,128)S(1)} fusion(f32[128,256]{1,0:T(8,128)S(1)} %fusion.2, f32[128,2048]{0,1:T(8,128)S(1)} %bitcast.114, f32[2,1,1,1,2048,512]{5,4,3,0,2,1:T(8,128)} %all-gather.3.cloned.1.call-done, s32[]{:T(128)S(6)} %add.139, s32[]{:T(128)S(6)} %select_n.182), kind=kOutput, calls=%fused_computation.16 | convolution fusion | flops 402685952 | bytes 3407880 | tf_op jit(solution)/shard_map/fik,fkj->fij/dot_general | solution.py:48
  150.2 0.0 copy-done
  150.3 1.1 fusion.9
  151.4 5.0 %collective-permute-start.4 = (f32[2,1,128,256]{3,2,1,0:T(8,128)S(1)}, f32[2,1,128,256]{3,2,1,0:T(8,128)S(1)}, u32[]{:S(2)}, u32[]{:S(2)}) collective-permute-start(f32[2,1,128,256]{3,2,1,0:T(8,128)S(1)} %pad_maximum_fusion), channel_id=1, source_target_pairs={{0,1},{1,0},{2,3},{3,2},{4,5},{5,4},{6,7},{7,6},{8,9},{9,8},{10,11... | collective-permute-start | bytes 786440 | tf_op jit(solution)/shard_map/ppermute | solution.py:104
  156.4 1.1 fusion
  157.5 1.1 fusion.1
  158.6 1.1 fusion.15
  159.8 1.1 fusion.13
  160.9 1.7 %collective-permute-done.4 = f32[2,1,128,256]{3,2,1,0:T(8,128)S(1)} collective-permute-done((f32[2,1,128,256]{3,2,1,0:T(8,128)S(1)}, f32[2,1,128,256]{3,2,1,0:T(8,128)S(1)}, u32[]{:S(2)}, u32[]{:S(2)}) %collective-permute-start.4) | collective-permute-done | bytes 262176 | tf_op jit(solution)/shard_map/ppermute | solution.py:104
  162.7 1.3 fusion.17
  164.0 0.7 pad_maximum_fusion.1
  (12 shorter events, 0.2 us)
Async XLA Ops:
  6.5 13.6 %copy-start.3 = (s32[1,4]{1,0:T(1,128)S(1)}, s32[1,4]{1,0:T(1,128)}, u32[]{:S(2)}) copy-start(s32[1,4]{1,0:T(1,128)} %param.5) | copy-start | bytes 52
  6.5 135.5 %all-gather.3.cloned.1.call-start = ((), (), s32[]{:S(2)}) async-start(), calls=%async_computation.1 | async-start | bytes 8650752 | tf_op jit(solution)/shard_map/all_gather | solution.py:93
  8.4 11.9 %collective-permute-start.3 = (f32[2,1,128,128]{2,3,0,1:T(8,128)S(1)}, f32[2,1,128,128]{2,3,0,1:T(8,128)S(1)}, u32[]{:S(2)}, u32[]{:S(2)}) collective-permute-start(f32[2,1,128,128]{2,3,0,1:T(8,128)S(1)} %bitcast.126), channel_id=1, source_target_pairs={{16,0},{32,16},{48,32},{64,50},{80,2},{82,66},{96,18},{98,82},{112... | collective-permute-start | bytes 393224 | tf_op jit(solution)/shard_map/ppermute | solution.py:64
  17.2 7.1 %collective-permute-start.2 = (f32[2,1,128,128]{2,3,0,1:T(8,128)S(1)}, f32[2,1,128,128]{2,3,0,1:T(8,128)S(1)}, u32[]{:S(2)}, u32[]{:S(2)}) collective-permute-start(f32[2,1,128,128]{2,3,0,1:T(8,128)S(1)} %bitcast.127), channel_id=1, source_target_pairs={{32,0},{48,16},{64,34},{80,50},{96,2},{98,66},{112,18},{114,82},{1... | collective-permute-start | bytes 393224 | tf_op jit(solution)/shard_map/ppermute | solution.py:64
  18.7 5.7 %collective-permute-start.1 = (f32[2,1,128,128]{2,3,0,1:T(8,128)S(1)}, f32[2,1,128,128]{2,3,0,1:T(8,128)S(1)}, u32[]{:S(2)}, u32[]{:S(2)}) collective-permute-start(f32[2,1,128,128]{2,3,0,1:T(8,128)S(1)} %bitcast.128), channel_id=1, source_target_pairs={{48,0},{64,18},{80,34},{96,50},{112,2},{114,66},{128,20},{130,84},... | collective-permute-start | bytes 393224 | tf_op jit(solution)/shard_map/ppermute | solution.py:64
  19.4 4.9 %collective-permute-start = (f32[2,1,128,128]{2,3,0,1:T(8,128)S(1)}, f32[2,1,128,128]{2,3,0,1:T(8,128)S(1)}, u32[]{:S(2)}, u32[]{:S(2)}) collective-permute-start(f32[2,1,128,128]{2,3,0,1:T(8,128)S(1)} %bitcast.129), channel_id=1, source_target_pairs={{64,2},{80,18},{96,34},{112,50},{128,4},{130,68},{144,20},{146,84}... | collective-permute-start | bytes 393224 | tf_op jit(solution)/shard_map/ppermute | solution.py:64
  24.4 1.2 copy-start.1
  28.5 47.8 %copy-start.2 = (f32[2,1]{0,1:T(1,128)S(1)}, f32[2,1]{0,1:T(1,128)}, u32[]{:S(2)}) copy-start(f32[2,1]{0,1:T(1,128)} %param.7) | copy-start | bytes 28
  28.5 48.4 %copy-start.4 = (s32[1,24]{1,0:T(1,128)S(1)}, s32[1,24]{1,0:T(1,128)}, u32[]{:S(2)}) copy-start(s32[1,24]{1,0:T(1,128)} %param.6) | copy-start | bytes 292
  28.5 98.8 %all-to-all-start = ((f32[8,2,1,128,256]{3,4,1,2,0:T(8,128)}), f32[8,2,1,128,256]{3,4,1,2,0:T(8,128)S(1)}, u32[]{:S(2)}, u32[]{:S(2)}) async-start(f32[8,2,1,128,256]{3,4,1,2,0:T(8,128)} %broadcast_in_dim.63), calls=%async_computation | async-start | bytes 4194304 | tf_op jit(solution)/shard_map/all_to_all | solution.py:11
  142.0 8.2 %copy-start = (f32[2,1,1,1,2048,512]{5,4,3,0,2,1:T(8,128)S(1)}, f32[2,1,1,1,2048,512]{5,4,3,0,2,1:T(8,128)}, u32[]{:S(2)}) copy-start(f32[2,1,1,1,2048,512]{5,4,3,0,2,1:T(8,128)} %all-gather.3.cloned.1.call-done) | copy-start | bytes 25165828
  151.4 11.2 %collective-permute-start.4 = (f32[2,1,128,256]{3,2,1,0:T(8,128)S(1)}, f32[2,1,128,256]{3,2,1,0:T(8,128)S(1)}, u32[]{:S(2)}, u32[]{:S(2)}) collective-permute-start(f32[2,1,128,256]{3,2,1,0:T(8,128)S(1)} %pad_maximum_fusion), channel_id=1, source_target_pairs={{0,1},{1,0},{2,3},{3,2},{4,5},{5,4},{6,7},{7,6},{8,9},{9,8},{10,11... | collective-permute-start | bytes 786440 | tf_op jit(solution)/shard_map/ppermute | solution.py:104
Sparse Core Ops, SparseCore 0:
  26.5 115.4 all-gather.2

commit v8 on v7

--- a/solution.py
+++ b/solution.py
@@ -57,13 +57,18 @@
     src_count = lax.axis_size("src")
     me_src = lax.axis_index("src")
     tiles = traces.reshape(comp_count, freq_count, TILE, per_rcv, TILE)
+    assert comp_count == half_count
     arrived = []
     for step in range(per_rcv):
         pick = (me_src % per_rcv + step) % per_rcv
         sent = lax.dynamic_index_in_dim(tiles, pick, 3, keepdims=False)
+        sent = lax.dynamic_index_in_dim(sent, my_half, 0, keepdims=False)
         got = lax.ppermute(sent, ("src", "rcv"), mirror_pairs(src_count, rcv_count, per_rcv, step))
-        arrived.append(jnp.swapaxes(got, 2, 3))
-    arrived = jnp.stack(arrived, axis=3)
+        arrived.append(jnp.swapaxes(got, 1, 2))
+    mine = jnp.stack(arrived, axis=2)
+    theirs = lax.ppermute(mine, "int", [(0, 1), (1, 0)])
+    arrived = jnp.stack([mine, theirs])
+    arrived = jnp.take(arrived, (jnp.arange(comp_count) + my_half) % comp_count, axis=0)
     order = (me_src % per_rcv - jnp.arange(per_rcv)) % per_rcv
     mirrored = jnp.take(arrived, order, axis=3)
     marks = (missing[0] > 0)[None, None, None, :, None]

time: 172 us -> 161 us (0.936)
  starting transfers between devices: 63.9 us -> 45.6 us
  waiting for transfers between devices: 68.3 us -> 76.7 us
  local copies, waits for them, and re-layouts: 8.47 us -> 6.47 us
    all_to_all x1, starting transfers between devices: 47.5 us -> 27.3 us  [from_everyone(): return lax.all_to_all(copies, axis, split_axis=0, concat_axis=0, tiled=True)]
    ppermute x0 -> x1, waiting for transfers between devices: none -> 7.87 us  [per_device(): theirs = lax.ppermute(mine, 'int', [(0, 1), (1, 0)])]
    all_to_all x1, waiting for transfers between devices: 48.3 us -> 50.3 us  [from_everyone(): return lax.all_to_all(copies, axis, split_axis=0, concat_axis=0, tiled=True)]
    ppermute x0 -> x1, starting transfers between devices: none -> 1.92 us  [per_device(): theirs = lax.ppermute(mine, 'int', [(0, 1), (1, 0)])]
    ppermute x4, waiting for transfers between devices: 4.08 us -> 2.22 us  [per_device(): lax.ppermute(sent, ('src', 'rcv'), mirror_pairs(src_count, rcv_count, per...]
  transfers between devices with their start and end apart: 7 -> 8, of which waited for: 4 -> 5; matrix products, arithmetic and copies ran while one was open for 6% -> 6% of each run, Pallas kernels for 0% -> 0%
where the time goes in v8:
time: 161 us
  waiting for transfers between devices  76.7 us (48%)
  starting transfers between devices  45.6 us (28%)
  matrix products  13.8 us (9%)
  between operations  13.8 us (9%)
  local copies, waits for them, and re-layouts  6.47 us (4%)
  other arithmetic  4.25 us (3%)
    all_to_all x1, waiting for transfers between devices, from_everyone(): return lax.all_to_all(copies, axis, split_axis=0, concat_axis=0, tiled=True)  50.3 us
    all_to_all x1, starting transfers between devices, from_everyone(): return lax.all_to_all(copies, axis, split_axis=0, concat_axis=0, tiled=True)  27.3 us
    all_gather x1, waiting for transfers between devices, per_device(): slab_piece = lax.all_gather(right_half, 'src', axis=2, tiled=True)  14.6 us
    dot_general x8, matrix products, complex_prod(): jnp.einsum('fik,fkj->fij', left_side, right_side, precision=lax.Precision...  13.8 us
    ppermute x4, starting transfers between devices, per_device(): lax.ppermute(sent, ('src', 'rcv'), mirror_pairs(src_count, rcv_count, per...  11.4 us
    ppermute x1, waiting for transfers between devices, per_device(): theirs = lax.ppermute(mine, 'int', [(0, 1), (1, 0)])  7.87 us
    ppermute x1, starting transfers between devices, per_device(): got = lax.ppermute(sent, 'int', [(0, 1), (1, 0)])  4.96 us
  transfers between devices with their start and end apart: 8, of which 5 were waited for; matrix products, arithmetic and copies ran while one was open for 6% of the time, Pallas kernels for 0%

profile of v8, /device:TPU:1, one launch (start us, length us, event | category | flops | bytes accessed | tf_op | source)
XLA Modules:
  0.0 160.6 jit_solution(18257886963123302568)
XLA Ops:
  6.5 0.0 all-gather.3.cloned.1.call-start
  6.5 1.2 copy.50
  7.8 8.8 %collective-permute-start.3 = (f32[1,128,128]{1,2,0:T(8,128)S(1)}, f32[1,128,128]{1,2,0:T(8,128)S(1)}, u32[]{:S(2)}, u32[]{:S(2)}) collective-permute-start(f32[1,128,128]{1,2,0:T(8,128)S(1)} %get-tuple-element.10), channel_id=1, source_target_pairs={{16,0},{32,16},{48,32},{64,50},{80,2},{82,66},{96,18},{98,82},{112... | collective-permute-start | bytes 196616 | tf_op jit(solution)/shard_map/ppermute | solution.py:66
  16.6 1.3 collective-permute-start.2
  17.9 0.7 collective-permute-start.1
  18.6 0.7 collective-permute-start
  19.3 0.7 compare_bitcast_fusion
  20.0 0.1 broadcast_bitcast_fusion.3
  20.1 0.0 collective-permute-done.3
  20.1 2.2 %collective-permute-done.2 = f32[1,128,128]{1,2,0:T(8,128)S(1)} collective-permute-done((f32[1,128,128]{1,2,0:T(8,128)S(1)}, f32[1,128,128]{1,2,0:T(8,128)S(1)}, u32[]{:S(2)}, u32[]{:S(2)}) %collective-permute-start.2) | collective-permute-done | bytes 65568 | tf_op jit(solution)/shard_map/ppermute | solution.py:66
  22.3 0.0 collective-permute-done.1
  22.3 0.0 collective-permute-done
  22.4 1.9 %collective-permute-start.4 = (f32[1,128,4,128]{3,1,2,0:T(8,128)S(1)}, f32[1,128,4,128]{3,1,2,0:T(8,128)S(1)}, u32[]{:S(2)}, u32[]{:S(2)}) collective-permute-start(f32[1,128,4,128]{3,1,2,0:T(8,128)S(1)} %get-tuple-element.14), channel_id=1, source_target_pairs={{0,1},{1,0},{2,3},{3,2},{4,5},{5,4},{6,7},{7,6},{8,9},{9,8},{10,11... | collective-permute-start | bytes 786440 | tf_op jit(solution)/shard_map/ppermute | solution.py:69
  24.3 0.1 broadcast_bitcast_fusion.2
  24.4 7.9 %collective-permute-done.4 = f32[1,128,4,128]{3,1,2,0:T(8,128)S(1)} collective-permute-done((f32[1,128,4,128]{3,1,2,0:T(8,128)S(1)}, f32[1,128,4,128]{3,1,2,0:T(8,128)S(1)}, u32[]{:S(2)}, u32[]{:S(2)}) %collective-permute-start.4) | collective-permute-done | bytes 262176 | tf_op jit(solution)/shard_map/ppermute | solution.py:69
  32.3 0.6 gather_fusion
  32.9 0.0 copy-start.1
  32.9 0.1 fusion.16
  33.0 0.6 gather_fusion.1
  33.6 0.3 copy.49
  34.0 0.2 gather.18
  34.2 0.0 copy-done.1
  34.2 0.7 dynamic-slice_select_fusion
  34.9 0.0 all-gather.3.cloned.1.call-update
  35.0 0.2 copy.42
  35.2 0.1 dynamic-slice_select_fusion.2
  35.3 1.6 broadcast_in_dim.75
  36.9 0.0 copy-start.2
  36.9 0.0 copy-start.3
  36.9 27.3 %all-to-all-start = ((f32[8,2,1,128,256]{3,4,1,2,0:T(8,128)}), f32[8,2,1,128,256]{3,4,1,2,0:T(8,128)S(1)}, u32[]{:S(2)}, u32[]{:S(2)}) async-start(f32[8,2,1,128,256]{3,4,1,2,0:T(8,128)} %broadcast_in_dim.75), calls=%async_computation | async-start | bytes 4194304 | tf_op jit(solution)/shard_map/all_to_all | solution.py:11
  64.2 0.1 copy.52
  64.3 0.1 gt.15
  64.4 0.1 broadcast_bitcast_fusion.1
  64.5 0.1 broadcast_bitcast_fusion
  64.6 0.0 copy-done.2
  64.6 0.6 fusion.36
  65.2 0.0 copy-done.3
  65.2 0.1 convert_reduce_fusion
  65.3 0.1 copy.51
  65.5 50.3 %all-to-all-done = f32[8,2,1,128,256]{3,4,1,2,0:T(8,128)S(1)} async-done(((f32[8,2,1,128,256]{3,4,1,2,0:T(8,128)}), f32[8,2,1,128,256]{3,4,1,2,0:T(8,128)S(1)}, u32[]{:S(2)}, u32[]{:S(2)}) %all-to-all-start) | async-done | bytes 2097184 | tf_op jit(solution)/shard_map/all_to_all | solution.py:11
  115.8 0.2 copy.48
  116.0 0.2 broadcast_multiply_fusion
  116.2 0.2 fusion.35
  116.4 14.6 %all-gather.3.cloned.1.call-done = f32[2,1,1,1,2048,512]{5,4,3,0,2,1:T(8,128)} async-done(((f32[2,1,1,1,64,512]{5,4,3,0,2,1:T(8,128)}), f32[2,1,1,1,2048,512]{5,4,3,0,2,1:T(8,128)}) %all-gather.3.cloned.1.call-update) | async-done | bytes 8388624 | tf_op jit(solution)/shard_map/all_gather | solution.py:98
  131.0 0.0 copy-start
  131.0 2.7 %fusion.2 = f32[128,256]{1,0:T(8,128)S(1)} fusion(f32[128,2048]{0,1:T(8,128)S(1)} %bitcast.125, f32[2,1,1,1,2048,512]{5,4,3,0,2,1:T(8,128)} %all-gather.3.cloned.1.call-done, s32[]{:T(128)S(6)} %select_n.252), kind=kOutput, calls=%fused_computation.8 | convolution fusion | flops 402653184 | bytes 3276804 | tf_op jit(solution)/shard_map/fik,fkj->fij/dot_general | solution.py:48
  133.7 2.9 %fusion.3 = f32[128,256]{1,0:T(8,128)S(1)} fusion(f32[128,2048]{0,1:T(8,128)S(1)} %bitcast.129, f32[2,1,1,1,2048,512]{5,4,3,0,2,1:T(8,128)} %all-gather.3.cloned.1.call-done, s32[]{:T(128)S(6)} %select_n.252), kind=kOutput, calls=%fused_computation.9 | convolution fusion | flops 402653184 | bytes 3276804 | tf_op jit(solution)/shard_map/fik,fkj->fij/dot_general | solution.py:48
  136.6 2.6 %fusion.11 = f32[1,1,128,256]{3,2,1,0:T(8,128)S(1)} fusion(f32[128,256]{1,0:T(8,128)S(1)} %fusion.2, f32[128,2048]{0,1:T(8,128)S(1)} %bitcast.130, f32[2,1,1,1,2048,512]{5,4,3,0,2,1:T(8,128)} %all-gather.3.cloned.1.call-done, s32[]{:T(128)S(6)} %add.223, s32[]{:T(128)S(6)} %select_n.252), kind=kOutput, calls=%fused_computation.17 | convolution fusion | flops 402685952 | bytes 3407880 | tf_op jit(solution)/shard_map/fik,fkj->fij/dot_general | solution.py:48
  139.2 0.0 copy-done
  139.2 1.1 fusion.9
  140.4 5.0 %collective-permute-start.5 = (f32[2,1,128,256]{3,2,1,0:T(8,128)S(1)}, f32[2,1,128,256]{3,2,1,0:T(8,128)S(1)}, u32[]{:S(2)}, u32[]{:S(2)}) collective-permute-start(f32[2,1,128,256]{3,2,1,0:T(8,128)S(1)} %pad_maximum_fusion.1), channel_id=1, source_target_pairs={{0,1},{1,0},{2,3},{3,2},{4,5},{5,4},{6,7},{7,6},{8,9},{9,8},{10,11... | collective-permute-start | bytes 786440 | tf_op jit(solution)/shard_map/ppermute | solution.py:109
  145.3 1.1 fusion
  146.5 1.1 fusion.1
  147.6 1.1 fusion.15
  148.7 1.1 fusion.13
  149.9 1.7 %collective-permute-done.5 = f32[2,1,128,256]{3,2,1,0:T(8,128)S(1)} collective-permute-done((f32[2,1,128,256]{3,2,1,0:T(8,128)S(1)}, f32[2,1,128,256]{3,2,1,0:T(8,128)S(1)}, u32[]{:S(2)}, u32[]{:S(2)}) %collective-permute-start.5) | collective-permute-done | bytes 262176 | tf_op jit(solution)/shard_map/ppermute | solution.py:109
  151.7 1.4 fusion.18
  153.0 0.7 pad_maximum_fusion.2
  (18 shorter events, 0.3 us)
Async XLA Ops:
  6.5 124.4 %all-gather.3.cloned.1.call-start = ((), (), s32[]{:S(2)}) async-start(), calls=%async_computation.1 | async-start | bytes 8650752 | tf_op jit(solution)/shard_map/all_gather | solution.py:98
  7.8 12.3 %collective-permute-start.3 = (f32[1,128,128]{1,2,0:T(8,128)S(1)}, f32[1,128,128]{1,2,0:T(8,128)S(1)}, u32[]{:S(2)}, u32[]{:S(2)}) collective-permute-start(f32[1,128,128]{1,2,0:T(8,128)S(1)} %get-tuple-element.10), channel_id=1, source_target_pairs={{16,0},{32,16},{48,32},{64,50},{80,2},{82,66},{96,18},{98,82},{112... | collective-permute-start | bytes 196616 | tf_op jit(solution)/shard_map/ppermute | solution.py:66
  16.6 5.7 %collective-permute-start.2 = (f32[1,128,128]{1,2,0:T(8,128)S(1)}, f32[1,128,128]{1,2,0:T(8,128)S(1)}, u32[]{:S(2)}, u32[]{:S(2)}) collective-permute-start(f32[1,128,128]{1,2,0:T(8,128)S(1)} %get-tuple-element.11), channel_id=1, source_target_pairs={{32,0},{48,16},{64,34},{80,50},{96,2},{98,66},{112,18},{114,82},{1... | collective-permute-start | bytes 196616 | tf_op jit(solution)/shard_map/ppermute | solution.py:66
  17.9 4.4 %collective-permute-start.1 = (f32[1,128,128]{1,2,0:T(8,128)S(1)}, f32[1,128,128]{1,2,0:T(8,128)S(1)}, u32[]{:S(2)}, u32[]{:S(2)}) collective-permute-start(f32[1,128,128]{1,2,0:T(8,128)S(1)} %get-tuple-element.12), channel_id=1, source_target_pairs={{48,0},{64,18},{80,34},{96,50},{112,2},{114,66},{128,20},{130,84},... | collective-permute-start | bytes 196616 | tf_op jit(solution)/shard_map/ppermute | solution.py:66
  18.6 3.7 %collective-permute-start = (f32[1,128,128]{1,2,0:T(8,128)S(1)}, f32[1,128,128]{1,2,0:T(8,128)S(1)}, u32[]{:S(2)}, u32[]{:S(2)}) collective-permute-start(f32[1,128,128]{1,2,0:T(8,128)S(1)} %get-tuple-element.9), channel_id=1, source_target_pairs={{64,2},{80,18},{96,34},{112,50},{128,4},{130,68},{144,20},{146,84}... | collective-permute-start | bytes 196616 | tf_op jit(solution)/shard_map/ppermute | solution.py:66
  22.4 9.9 %collective-permute-start.4 = (f32[1,128,4,128]{3,1,2,0:T(8,128)S(1)}, f32[1,128,4,128]{3,1,2,0:T(8,128)S(1)}, u32[]{:S(2)}, u32[]{:S(2)}) collective-permute-start(f32[1,128,4,128]{3,1,2,0:T(8,128)S(1)} %get-tuple-element.14), channel_id=1, source_target_pairs={{0,1},{1,0},{2,3},{3,2},{4,5},{5,4},{6,7},{7,6},{8,9},{9,8},{10,11... | collective-permute-start | bytes 786440 | tf_op jit(solution)/shard_map/ppermute | solution.py:69
  32.9 1.3 copy-start.1
  36.9 27.7 %copy-start.2 = (f32[2,1]{0,1:T(1,128)S(1)}, f32[2,1]{0,1:T(1,128)}, u32[]{:S(2)}) copy-start(f32[2,1]{0,1:T(1,128)} %param.7) | copy-start | bytes 28
  36.9 28.4 %copy-start.3 = (s32[1,24]{1,0:T(1,128)S(1)}, s32[1,24]{1,0:T(1,128)}, u32[]{:S(2)}) copy-start(s32[1,24]{1,0:T(1,128)} %param.6) | copy-start | bytes 292
  36.9 79.0 %all-to-all-start = ((f32[8,2,1,128,256]{3,4,1,2,0:T(8,128)}), f32[8,2,1,128,256]{3,4,1,2,0:T(8,128)S(1)}, u32[]{:S(2)}, u32[]{:S(2)}) async-start(f32[8,2,1,128,256]{3,4,1,2,0:T(8,128)} %broadcast_in_dim.75), calls=%async_computation | async-start | bytes 4194304 | tf_op jit(solution)/shard_map/all_to_all | solution.py:11
  131.0 8.2 %copy-start = (f32[2,1,1,1,2048,512]{5,4,3,0,2,1:T(8,128)S(1)}, f32[2,1,1,1,2048,512]{5,4,3,0,2,1:T(8,128)}, u32[]{:S(2)}) copy-start(f32[2,1,1,1,2048,512]{5,4,3,0,2,1:T(8,128)} %all-gather.3.cloned.1.call-done) | copy-start | bytes 25165828
  140.4 11.2 %collective-permute-start.5 = (f32[2,1,128,256]{3,2,1,0:T(8,128)S(1)}, f32[2,1,128,256]{3,2,1,0:T(8,128)S(1)}, u32[]{:S(2)}, u32[]{:S(2)}) collective-permute-start(f32[2,1,128,256]{3,2,1,0:T(8,128)S(1)} %pad_maximum_fusion.1), channel_id=1, source_target_pairs={{0,1},{1,0},{2,3},{3,2},{4,5},{5,4},{6,7},{7,6},{8,9},{9,8},{10,11... | collective-permute-start | bytes 786440 | tf_op jit(solution)/shard_map/ppermute | solution.py:109
Sparse Core Ops, SparseCore 0:
  35.1 95.8 all-gather.2

commit v9 on v8

--- a/solution.py
+++ b/solution.py
@@ -58,16 +58,15 @@
     me_src = lax.axis_index("src")
     tiles = traces.reshape(comp_count, freq_count, TILE, per_rcv, TILE)
     assert comp_count == half_count
-    arrived = []
+    mine, theirs = [], []
     for step in range(per_rcv):
         pick = (me_src % per_rcv + step) % per_rcv
         sent = lax.dynamic_index_in_dim(tiles, pick, 3, keepdims=False)
         sent = lax.dynamic_index_in_dim(sent, my_half, 0, keepdims=False)
         got = lax.ppermute(sent, ("src", "rcv"), mirror_pairs(src_count, rcv_count, per_rcv, step))
-        arrived.append(jnp.swapaxes(got, 1, 2))
-    mine = jnp.stack(arrived, axis=2)
-    theirs = lax.ppermute(mine, "int", [(0, 1), (1, 0)])
-    arrived = jnp.stack([mine, theirs])
+        mine.append(jnp.swapaxes(got, 1, 2))
+        theirs.append(jnp.swapaxes(lax.ppermute(got, "int", [(0, 1), (1, 0)]), 1, 2))
+    arrived = jnp.stack([jnp.stack(mine, axis=2), jnp.stack(theirs, axis=2)])
     arrived = jnp.take(arrived, (jnp.arange(comp_count) + my_half) % comp_count, axis=0)
     order = (me_src % per_rcv - jnp.arange(per_rcv)) % per_rcv
     mirrored = jnp.take(arrived, order, axis=3)

time: 161 us -> 163 us (1.012)
  starting transfers between devices: 45.6 us -> 57.1 us
  waiting for transfers between devices: 76.7 us -> 67.2 us
    ppermute x1 -> x4, starting transfers between devices: 1.92 us -> 13.4 us  [per_device(): lax.ppermute(got, 'int', [(0, 1), (1, 0)])]
    ppermute x1 -> x4, waiting for transfers between devices: 7.87 us -> 1.76 us  [per_device(): lax.ppermute(got, 'int', [(0, 1), (1, 0)])]
    ppermute x4, waiting for transfers between devices: 2.22 us -> 0.2 us  [per_device(): lax.ppermute(sent, ('src', 'rcv'), mirror_pairs(src_count, rcv_count, per...]
  transfers between devices with their start and end apart: 8 -> 11, of which waited for: 5 -> 5; matrix products, arithmetic and copies ran while one was open for 6% -> 6% of each run, Pallas kernels for 0% -> 0%
where the time goes in v9:
time: 163 us
  waiting for transfers between devices  67.2 us (41%)
  starting transfers between devices  57.1 us (35%)
  matrix products  13.8 us (8%)
  between operations  13.8 us (8%)
  local copies, waits for them, and re-layouts  6.47 us (4%)
  other arithmetic  4.11 us (3%)
    all_to_all x1, waiting for transfers between devices, from_everyone(): return lax.all_to_all(copies, axis, split_axis=0, concat_axis=0, tiled=True)  50.4 us
    all_to_all x1, starting transfers between devices, from_everyone(): return lax.all_to_all(copies, axis, split_axis=0, concat_axis=0, tiled=True)  27.3 us
    dot_general x8, matrix products, complex_prod(): jnp.einsum('fik,fkj->fij', left_side, right_side, precision=lax.Precision...  13.8 us
    ppermute x4, starting transfers between devices, per_device(): lax.ppermute(got, 'int', [(0, 1), (1, 0)])  13.4 us
    all_gather x1, waiting for transfers between devices, per_device(): slab_piece = lax.all_gather(right_half, 'src', axis=2, tiled=True)  13.2 us
    ppermute x4, starting transfers between devices, per_device(): lax.ppermute(sent, ('src', 'rcv'), mirror_pairs(src_count, rcv_count, per...  11.4 us
    ppermute x1, starting transfers between devices, per_device(): got = lax.ppermute(sent, 'int', [(0, 1), (1, 0)])  4.95 us
  transfers between devices with their start and end apart: 11, of which 5 were waited for; matrix products, arithmetic and copies ran while one was open for 6% of the time, Pallas kernels for 0%

profile of v9, /device:TPU:1, one launch (start us, length us, event | category | flops | bytes accessed | tf_op | source)
XLA Modules:
  0.0 162.6 jit_solution(9487867925756790925)
XLA Ops:
  6.5 0.0 all-gather.3.cloned.1.call-start
  6.5 1.2 copy.50
  7.8 8.8 %collective-permute-start.3 = (f32[1,128,128]{1,2,0:T(8,128)S(1)}, f32[1,128,128]{1,2,0:T(8,128)S(1)}, u32[]{:S(2)}, u32[]{:S(2)}) collective-permute-start(f32[1,128,128]{1,2,0:T(8,128)S(1)} %get-tuple-element.10), channel_id=1, source_target_pairs={{16,0},{32,16},{48,32},{64,50},{80,2},{82,66},{96,18},{98,82},{112... | collective-permute-start | bytes 196616 | tf_op jit(solution)/shard_map/ppermute | solution.py:66
  16.6 1.3 collective-permute-start.2
  17.9 0.7 collective-permute-start.1
  18.6 0.7 collective-permute-start
  19.4 0.7 compare_bitcast_fusion
  20.0 0.1 broadcast_bitcast_fusion.3
  20.1 0.1 broadcast_bitcast_fusion.2
  20.2 0.0 collective-permute-done.3
  20.2 1.9 %collective-permute-start.7 = (f32[1,128,128]{1,2,0:T(8,128)S(1)}, f32[1,128,128]{1,2,0:T(8,128)S(1)}, u32[]{:S(2)}, u32[]{:S(2)}) collective-permute-start(f32[1,128,128]{1,2,0:T(8,128)S(1)} %collective-permute-done.3), channel_id=1, source_target_pairs={{0,1},{1,0},{2,3},{3,2},{4,5},{5,4},{6,7},{7,6},{8,9},{9,8},{10,11... | collective-permute-start | bytes 196616 | tf_op jit(solution)/shard_map/ppermute | solution.py:68
  22.1 0.2 collective-permute-done.2
  22.3 4.7 %collective-permute-start.6 = (f32[1,128,128]{1,2,0:T(8,128)S(1)}, f32[1,128,128]{1,2,0:T(8,128)S(1)}, u32[]{:S(2)}, u32[]{:S(2)}) collective-permute-start(f32[1,128,128]{1,2,0:T(8,128)S(1)} %collective-permute-done.2), channel_id=1, source_target_pairs={{0,1},{1,0},{2,3},{3,2},{4,5},{5,4},{6,7},{7,6},{8,9},{9,8},{10,11... | collective-permute-start | bytes 196616 | tf_op jit(solution)/shard_map/ppermute | solution.py:68
  27.0 0.0 collective-permute-done.1
  27.0 2.1 %collective-permute-start.5 = (f32[1,128,128]{1,2,0:T(8,128)S(1)}, f32[1,128,128]{1,2,0:T(8,128)S(1)}, u32[]{:S(2)}, u32[]{:S(2)}) collective-permute-start(f32[1,128,128]{1,2,0:T(8,128)S(1)} %collective-permute-done.1), channel_id=1, source_target_pairs={{0,1},{1,0},{2,3},{3,2},{4,5},{5,4},{6,7},{7,6},{8,9},{9,8},{10,11... | collective-permute-start | bytes 196616 | tf_op jit(solution)/shard_map/ppermute | solution.py:68
  29.1 0.0 collective-permute-done
  29.1 4.7 %collective-permute-start.4 = (f32[1,128,128]{1,2,0:T(8,128)S(1)}, f32[1,128,128]{1,2,0:T(8,128)S(1)}, u32[]{:S(2)}, u32[]{:S(2)}) collective-permute-start(f32[1,128,128]{1,2,0:T(8,128)S(1)} %collective-permute-done), channel_id=1, source_target_pairs={{0,1},{1,0},{2,3},{3,2},{4,5},{5,4},{6,7},{7,6},{8,9},{9,8},{10,11... | collective-permute-start | bytes 196616 | tf_op jit(solution)/shard_map/ppermute | solution.py:68
  33.9 0.0 collective-permute-done.7
  33.9 0.0 collective-permute-done.6
  33.9 0.0 collective-permute-done.5
  33.9 1.7 %collective-permute-done.4 = f32[1,128,128]{1,2,0:T(8,128)S(1)} collective-permute-done((f32[1,128,128]{1,2,0:T(8,128)S(1)}, f32[1,128,128]{1,2,0:T(8,128)S(1)}, u32[]{:S(2)}, u32[]{:S(2)}) %collective-permute-start.4) | collective-permute-done | bytes 65568 | tf_op jit(solution)/shard_map/ppermute | solution.py:68
  35.7 0.6 gather_fusion
  36.3 0.0 copy-start.1
  36.3 0.1 fusion.16
  36.4 0.6 gather_fusion.1
  37.0 0.3 copy.49
  37.4 0.2 gather.18
  37.6 0.0 copy-done.1
  37.6 0.7 dynamic-slice_select_fusion
  38.4 0.0 all-gather.3.cloned.1.call-update
  38.4 0.2 copy.42
  38.6 0.1 dynamic-slice_select_fusion.2
  38.7 1.6 broadcast_in_dim.75
  40.3 0.0 copy-start.2
  40.3 0.0 copy-start.3
  40.3 27.3 %all-to-all-start = ((f32[8,2,1,128,256]{3,4,1,2,0:T(8,128)}), f32[8,2,1,128,256]{3,4,1,2,0:T(8,128)S(1)}, u32[]{:S(2)}, u32[]{:S(2)}) async-start(f32[8,2,1,128,256]{3,4,1,2,0:T(8,128)} %broadcast_in_dim.75), calls=%async_computation | async-start | bytes 4194304 | tf_op jit(solution)/shard_map/all_to_all | solution.py:11
  67.6 0.1 copy.52
  67.8 0.1 gt.15
  67.9 0.1 broadcast_bitcast_fusion.1
  68.0 0.1 broadcast_bitcast_fusion
  68.1 0.0 copy-done.2
  68.1 0.6 fusion.35
  68.7 0.0 copy-done.3
  68.7 0.1 convert_reduce_fusion
  68.8 0.1 copy.51
  69.0 50.4 %all-to-all-done = f32[8,2,1,128,256]{3,4,1,2,0:T(8,128)S(1)} async-done(((f32[8,2,1,128,256]{3,4,1,2,0:T(8,128)}), f32[8,2,1,128,256]{3,4,1,2,0:T(8,128)S(1)}, u32[]{:S(2)}, u32[]{:S(2)}) %all-to-all-start) | async-done | bytes 2097184 | tf_op jit(solution)/shard_map/all_to_all | solution.py:11
  119.3 0.2 copy.48
  119.5 0.2 broadcast_multiply_fusion
  119.7 0.2 fusion.34
  119.9 13.2 %all-gather.3.cloned.1.call-done = f32[2,1,1,1,2048,512]{5,4,3,0,2,1:T(8,128)} async-done(((f32[2,1,1,1,64,512]{5,4,3,0,2,1:T(8,128)}), f32[2,1,1,1,2048,512]{5,4,3,0,2,1:T(8,128)}) %all-gather.3.cloned.1.call-update) | async-done | bytes 8388624 | tf_op jit(solution)/shard_map/all_gather | solution.py:97
  133.1 0.0 copy-start
  133.1 2.7 %fusion.2 = f32[128,256]{1,0:T(8,128)S(1)} fusion(f32[128,2048]{0,1:T(8,128)S(1)} %bitcast.138, f32[2,1,1,1,2048,512]{5,4,3,0,2,1:T(8,128)} %all-gather.3.cloned.1.call-done, s32[]{:T(128)S(6)} %select_n.252), kind=kOutput, calls=%fused_computation.8 | convolution fusion | flops 402653184 | bytes 3276804 | tf_op jit(solution)/shard_map/fik,fkj->fij/dot_general | solution.py:48
  135.9 2.9 %fusion.3 = f32[128,256]{1,0:T(8,128)S(1)} fusion(f32[128,2048]{0,1:T(8,128)S(1)} %bitcast.142, f32[2,1,1,1,2048,512]{5,4,3,0,2,1:T(8,128)} %all-gather.3.cloned.1.call-done, s32[]{:T(128)S(6)} %select_n.252), kind=kOutput, calls=%fused_computation.9 | convolution fusion | flops 402653184 | bytes 3276804 | tf_op jit(solution)/shard_map/fik,fkj->fij/dot_general | solution.py:48
  138.7 2.6 %fusion.11 = f32[1,1,128,256]{3,2,1,0:T(8,128)S(1)} fusion(f32[128,256]{1,0:T(8,128)S(1)} %fusion.2, f32[128,2048]{0,1:T(8,128)S(1)} %bitcast.143, f32[2,1,1,1,2048,512]{5,4,3,0,2,1:T(8,128)} %all-gather.3.cloned.1.call-done, s32[]{:T(128)S(6)} %add.223, s32[]{:T(128)S(6)} %select_n.252), kind=kOutput, calls=%fused_computation.17 | convolution fusion | flops 402685952 | bytes 3407880 | tf_op jit(solution)/shard_map/fik,fkj->fij/dot_general | solution.py:48
  141.3 0.0 copy-done
  141.3 1.1 fusion.9
  142.5 5.0 %collective-permute-start.8 = (f32[2,1,128,256]{3,2,1,0:T(8,128)S(1)}, f32[2,1,128,256]{3,2,1,0:T(8,128)S(1)}, u32[]{:S(2)}, u32[]{:S(2)}) collective-permute-start(f32[2,1,128,256]{3,2,1,0:T(8,128)S(1)} %pad_maximum_fusion), channel_id=1, source_target_pairs={{0,1},{1,0},{2,3},{3,2},{4,5},{5,4},{6,7},{7,6},{8,9},{9,8},{10,11... | collective-permute-start | bytes 786440 | tf_op jit(solution)/shard_map/ppermute | solution.py:108
  147.5 1.1 fusion
  148.6 1.1 fusion.1
  149.7 1.1 fusion.15
  150.9 1.1 fusion.13
  152.0 1.7 %collective-permute-done.8 = f32[2,1,128,256]{3,2,1,0:T(8,128)S(1)} collective-permute-done((f32[2,1,128,256]{3,2,1,0:T(8,128)S(1)}, f32[2,1,128,256]{3,2,1,0:T(8,128)S(1)}, u32[]{:S(2)}, u32[]{:S(2)}) %collective-permute-start.8) | collective-permute-done | bytes 262176 | tf_op jit(solution)/shard_map/ppermute | solution.py:108
  153.8 1.2 fusion.18
  155.0 0.7 pad_maximum_fusion.1
  (19 shorter events, 0.4 us)
Async XLA Ops:
  6.5 126.6 %all-gather.3.cloned.1.call-start = ((), (), s32[]{:S(2)}) async-start(), calls=%async_computation.1 | async-start | bytes 8650752 | tf_op jit(solution)/shard_map/all_gather | solution.py:97
  7.8 12.4 %collective-permute-start.3 = (f32[1,128,128]{1,2,0:T(8,128)S(1)}, f32[1,128,128]{1,2,0:T(8,128)S(1)}, u32[]{:S(2)}, u32[]{:S(2)}) collective-permute-start(f32[1,128,128]{1,2,0:T(8,128)S(1)} %get-tuple-element.10), channel_id=1, source_target_pairs={{16,0},{32,16},{48,32},{64,50},{80,2},{82,66},{96,18},{98,82},{112... | collective-permute-start | bytes 196616 | tf_op jit(solution)/shard_map/ppermute | solution.py:66
  16.6 5.7 %collective-permute-start.2 = (f32[1,128,128]{1,2,0:T(8,128)S(1)}, f32[1,128,128]{1,2,0:T(8,128)S(1)}, u32[]{:S(2)}, u32[]{:S(2)}) collective-permute-start(f32[1,128,128]{1,2,0:T(8,128)S(1)} %get-tuple-element.11), channel_id=1, source_target_pairs={{32,0},{48,16},{64,34},{80,50},{96,2},{98,66},{112,18},{114,82},{1... | collective-permute-start | bytes 196616 | tf_op jit(solution)/shard_map/ppermute | solution.py:66
  17.9 9.1 %collective-permute-start.1 = (f32[1,128,128]{1,2,0:T(8,128)S(1)}, f32[1,128,128]{1,2,0:T(8,128)S(1)}, u32[]{:S(2)}, u32[]{:S(2)}) collective-permute-start(f32[1,128,128]{1,2,0:T(8,128)S(1)} %get-tuple-element.12), channel_id=1, source_target_pairs={{48,0},{64,18},{80,34},{96,50},{112,2},{114,66},{128,20},{130,84},... | collective-permute-start | bytes 196616 | tf_op jit(solution)/shard_map/ppermute | solution.py:66
  18.6 10.5 %collective-permute-start = (f32[1,128,128]{1,2,0:T(8,128)S(1)}, f32[1,128,128]{1,2,0:T(8,128)S(1)}, u32[]{:S(2)}, u32[]{:S(2)}) collective-permute-start(f32[1,128,128]{1,2,0:T(8,128)S(1)} %get-tuple-element.9), channel_id=1, source_target_pairs={{64,2},{80,18},{96,34},{112,50},{128,4},{130,68},{144,20},{146,84}... | collective-permute-start | bytes 196616 | tf_op jit(solution)/shard_map/ppermute | solution.py:66
  20.2 13.7 %collective-permute-start.7 = (f32[1,128,128]{1,2,0:T(8,128)S(1)}, f32[1,128,128]{1,2,0:T(8,128)S(1)}, u32[]{:S(2)}, u32[]{:S(2)}) collective-permute-start(f32[1,128,128]{1,2,0:T(8,128)S(1)} %collective-permute-done.3), channel_id=1, source_target_pairs={{0,1},{1,0},{2,3},{3,2},{4,5},{5,4},{6,7},{7,6},{8,9},{9,8},{10,11... | collective-permute-start | bytes 196616 | tf_op jit(solution)/shard_map/ppermute | solution.py:68
  22.3 11.6 %collective-permute-start.6 = (f32[1,128,128]{1,2,0:T(8,128)S(1)}, f32[1,128,128]{1,2,0:T(8,128)S(1)}, u32[]{:S(2)}, u32[]{:S(2)}) collective-permute-start(f32[1,128,128]{1,2,0:T(8,128)S(1)} %collective-permute-done.2), channel_id=1, source_target_pairs={{0,1},{1,0},{2,3},{3,2},{4,5},{5,4},{6,7},{7,6},{8,9},{9,8},{10,11... | collective-permute-start | bytes 196616 | tf_op jit(solution)/shard_map/ppermute | solution.py:68
  27.0 6.9 %collective-permute-start.5 = (f32[1,128,128]{1,2,0:T(8,128)S(1)}, f32[1,128,128]{1,2,0:T(8,128)S(1)}, u32[]{:S(2)}, u32[]{:S(2)}) collective-permute-start(f32[1,128,128]{1,2,0:T(8,128)S(1)} %collective-permute-done.1), channel_id=1, source_target_pairs={{0,1},{1,0},{2,3},{3,2},{4,5},{5,4},{6,7},{7,6},{8,9},{9,8},{10,11... | collective-permute-start | bytes 196616 | tf_op jit(solution)/shard_map/ppermute | solution.py:68
  29.1 6.5 %collective-permute-start.4 = (f32[1,128,128]{1,2,0:T(8,128)S(1)}, f32[1,128,128]{1,2,0:T(8,128)S(1)}, u32[]{:S(2)}, u32[]{:S(2)}) collective-permute-start(f32[1,128,128]{1,2,0:T(8,128)S(1)} %collective-permute-done), channel_id=1, source_target_pairs={{0,1},{1,0},{2,3},{3,2},{4,5},{5,4},{6,7},{7,6},{8,9},{9,8},{10,11... | collective-permute-start | bytes 196616 | tf_op jit(solution)/shard_map/ppermute | solution.py:68
  36.3 1.3 copy-start.1
  40.3 27.8 %copy-start.2 = (f32[2,1]{0,1:T(1,128)S(1)}, f32[2,1]{0,1:T(1,128)}, u32[]{:S(2)}) copy-start(f32[2,1]{0,1:T(1,128)} %param.7) | copy-start | bytes 28
  40.3 28.4 %copy-start.3 = (s32[1,24]{1,0:T(1,128)S(1)}, s32[1,24]{1,0:T(1,128)}, u32[]{:S(2)}) copy-start(s32[1,24]{1,0:T(1,128)} %param.6) | copy-start | bytes 292
  40.3 79.0 %all-to-all-start = ((f32[8,2,1,128,256]{3,4,1,2,0:T(8,128)}), f32[8,2,1,128,256]{3,4,1,2,0:T(8,128)S(1)}, u32[]{:S(2)}, u32[]{:S(2)}) async-start(f32[8,2,1,128,256]{3,4,1,2,0:T(8,128)} %broadcast_in_dim.75), calls=%async_computation | async-start | bytes 4194304 | tf_op jit(solution)/shard_map/all_to_all | solution.py:11
  133.1 8.2 %copy-start = (f32[2,1,1,1,2048,512]{5,4,3,0,2,1:T(8,128)S(1)}, f32[2,1,1,1,2048,512]{5,4,3,0,2,1:T(8,128)}, u32[]{:S(2)}) copy-start(f32[2,1,1,1,2048,512]{5,4,3,0,2,1:T(8,128)} %all-gather.3.cloned.1.call-done) | copy-start | bytes 25165828
  142.5 11.2 %collective-permute-start.8 = (f32[2,1,128,256]{3,2,1,0:T(8,128)S(1)}, f32[2,1,128,256]{3,2,1,0:T(8,128)S(1)}, u32[]{:S(2)}, u32[]{:S(2)}) collective-permute-start(f32[2,1,128,256]{3,2,1,0:T(8,128)S(1)} %pad_maximum_fusion), channel_id=1, source_target_pairs={{0,1},{1,0},{2,3},{3,2},{4,5},{5,4},{6,7},{7,6},{8,9},{9,8},{10,11... | collective-permute-start | bytes 786440 | tf_op jit(solution)/shard_map/ppermute | solution.py:108
Sparse Core Ops, SparseCore 0:
  38.5 94.5 all-gather.2

commit v10 on v8

--- a/solution.py
+++ b/solution.py
@@ -95,12 +95,18 @@
     weighted = (weighted * chosen[None, None, :, None, :, None]).reshape(
         comp_count, freq_count, local_rows, block_count * half_tile
     )
-    slab_piece = lax.all_gather(right_half, "src", axis=2, tiled=True)
+    slab_piece = jnp.transpose(right_half, (1, 2, 0, 3)).reshape(
+        freq_count, row_tiles * half_tile, comp_count * local_cols
+    )
+    slab_piece = lax.all_gather(slab_piece, "src", axis=1, tiled=True)
     out_cols = local_cols // half_count
     assert half_count == 2
 
     def half_product(which):
-        cols = lax.dynamic_slice_in_dim(slab_piece, which * out_cols, out_cols, axis=3)
+        cols = [
+            lax.dynamic_slice_in_dim(slab_piece, comp * local_cols + which * out_cols, out_cols, axis=2)
+            for comp in range(comp_count)
+        ]
         real_part = complex_prod(weighted[0], cols[0]) - complex_prod(weighted[1], cols[1])
         imag_part = complex_prod(weighted[0], cols[1]) + complex_prod(weighted[1], cols[0])
         return jnp.stack([real_part, imag_part])

time: 161 us -> 161 us (level)
  no operation moved by 1% of the time
where the time goes in v10:
time: 161 us
  waiting for transfers between devices  77.5 us (48%)
  starting transfers between devices  44.9 us (28%)
  matrix products  13.8 us (9%)
  between operations  13.8 us (9%)
  local copies, waits for them, and re-layouts  7.19 us (4%)
  other arithmetic  3.54 us (2%)
    all_to_all x1, waiting for transfers between devices, from_everyone(): return lax.all_to_all(copies, axis, split_axis=0, concat_axis=0, tiled=True)  50.3 us
    all_to_all x1, starting transfers between devices, from_everyone(): return lax.all_to_all(copies, axis, split_axis=0, concat_axis=0, tiled=True)  27.3 us
    all_gather x1, waiting for transfers between devices, per_device(): slab_piece = lax.all_gather(slab_piece, 'src', axis=1, tiled=True)  14.9 us
    dot_general x8, matrix products, complex_prod(): jnp.einsum('fik,fkj->fij', left_side, right_side, precision=lax.Precision...  13.8 us
    ppermute x4, starting transfers between devices, per_device(): lax.ppermute(sent, ('src', 'rcv'), mirror_pairs(src_count, rcv_count, per...  11.4 us
    ppermute x1, waiting for transfers between devices, per_device(): theirs = lax.ppermute(mine, 'int', [(0, 1), (1, 0)])  7.87 us
    ppermute x1, starting transfers between devices, per_device(): got = lax.ppermute(sent, 'int', [(0, 1), (1, 0)])  4.27 us
  transfers between devices with their start and end apart: 8, of which 5 were waited for; matrix products, arithmetic and copies ran while one was open for 6% of the time, Pallas kernels for 0%

profile of v10, /device:TPU:1, one launch (start us, length us, event | category | flops | bytes accessed | tf_op | source)
XLA Modules:
  0.0 160.7 jit_solution(12617821132708226497)
XLA Ops:
  6.5 0.0 all-gather.2.cloned.1.call-start
  6.5 1.2 copy.66
  7.8 8.8 %collective-permute-start.3 = (f32[1,128,128]{1,2,0:T(8,128)S(1)}, f32[1,128,128]{1,2,0:T(8,128)S(1)}, u32[]{:S(2)}, u32[]{:S(2)}) collective-permute-start(f32[1,128,128]{1,2,0:T(8,128)S(1)} %get-tuple-element.10), channel_id=1, source_target_pairs={{16,0},{32,16},{48,32},{64,50},{80,2},{82,66},{96,18},{98,82},{112... | collective-permute-start | bytes 196616 | tf_op jit(solution)/shard_map/ppermute | solution.py:66
  16.6 1.3 collective-permute-start.2
  17.9 0.7 collective-permute-start.1
  18.6 0.7 collective-permute-start
  19.3 0.7 compare_bitcast_fusion
  20.0 0.1 broadcast_bitcast_fusion.3
  20.1 0.0 collective-permute-done.3
  20.1 2.2 %collective-permute-done.2 = f32[1,128,128]{1,2,0:T(8,128)S(1)} collective-permute-done((f32[1,128,128]{1,2,0:T(8,128)S(1)}, f32[1,128,128]{1,2,0:T(8,128)S(1)}, u32[]{:S(2)}, u32[]{:S(2)}) %collective-permute-start.2) | collective-permute-done | bytes 65568 | tf_op jit(solution)/shard_map/ppermute | solution.py:66
  22.3 0.0 collective-permute-done.1
  22.3 0.0 collective-permute-done
  22.4 1.9 %collective-permute-start.4 = (f32[1,128,4,128]{3,1,2,0:T(8,128)S(1)}, f32[1,128,4,128]{3,1,2,0:T(8,128)S(1)}, u32[]{:S(2)}, u32[]{:S(2)}) collective-permute-start(f32[1,128,4,128]{3,1,2,0:T(8,128)S(1)} %get-tuple-element.14), channel_id=1, source_target_pairs={{0,1},{1,0},{2,3},{3,2},{4,5},{5,4},{6,7},{7,6},{8,9},{9,8},{10,11... | collective-permute-start | bytes 786440 | tf_op jit(solution)/shard_map/ppermute | solution.py:69
  24.3 0.1 broadcast_bitcast_fusion.2
  24.4 7.9 %collective-permute-done.4 = f32[1,128,4,128]{3,1,2,0:T(8,128)S(1)} collective-permute-done((f32[1,128,4,128]{3,1,2,0:T(8,128)S(1)}, f32[1,128,4,128]{3,1,2,0:T(8,128)S(1)}, u32[]{:S(2)}, u32[]{:S(2)}) %collective-permute-start.4) | collective-permute-done | bytes 262176 | tf_op jit(solution)/shard_map/ppermute | solution.py:69
  32.3 0.6 gather_fusion
  32.9 0.0 copy-start.1
  32.9 0.1 fusion.48
  33.0 0.6 gather_fusion.1
  33.6 0.3 copy.64
  34.0 0.2 gather.18
  34.2 0.0 copy-done.1
  34.2 0.7 copy.69
  35.0 0.0 all-gather.2.cloned.1.call-update
  35.0 0.2 copy.57
  35.2 0.1 dynamic-slice_select_fusion.2
  35.3 1.6 broadcast_in_dim.75
  36.9 0.0 copy-start.2
  36.9 0.0 copy-start.3
  36.9 27.3 %all-to-all-start = ((f32[8,2,1,128,256]{3,4,1,2,0:T(8,128)}), f32[8,2,1,128,256]{3,4,1,2,0:T(8,128)S(1)}, u32[]{:S(2)}, u32[]{:S(2)}) async-start(f32[8,2,1,128,256]{3,4,1,2,0:T(8,128)} %broadcast_in_dim.75), calls=%async_computation | async-start | bytes 4194304 | tf_op jit(solution)/shard_map/all_to_all | solution.py:11
  64.2 0.1 copy.68
  64.3 0.1 gt.15
  64.4 0.1 broadcast_bitcast_fusion.1
  64.5 0.1 broadcast_bitcast_fusion
  64.6 0.0 copy-done.2
  64.6 0.6 fusion.69
  65.2 0.0 copy-done.3
  65.2 0.1 convert_reduce_fusion
  65.4 0.1 copy.67
  65.5 50.3 %all-to-all-done = f32[8,2,1,128,256]{3,4,1,2,0:T(8,128)S(1)} async-done(((f32[8,2,1,128,256]{3,4,1,2,0:T(8,128)}), f32[8,2,1,128,256]{3,4,1,2,0:T(8,128)S(1)}, u32[]{:S(2)}, u32[]{:S(2)}) %all-to-all-start) | async-done | bytes 2097184 | tf_op jit(solution)/shard_map/all_to_all | solution.py:11
  115.8 0.2 copy.63
  116.0 0.2 broadcast_multiply_fusion
  116.2 0.2 fusion.68
  116.5 14.9 %all-gather.2.cloned.1.call-done = f32[1,2048,1024]{2,1,0:T(8,128)} async-done(((f32[1,64,1024]{2,1,0:T(8,128)}), f32[1,2048,1024]{2,1,0:T(8,128)}) %all-gather.2.cloned.1.call-update) | async-done | bytes 8388624 | tf_op jit(solution)/shard_map/all_gather | solution.py:101
  131.3 0.0 copy-start
  131.3 2.7 %fusion = f32[128,256]{1,0:T(8,128)S(1)} fusion(f32[128,2048]{0,1:T(8,128)S(1)} %bitcast.135, f32[1,2048,1024]{2,1,0:T(8,128)} %all-gather.2.cloned.1.call-done, s32[]{:T(128)S(6)} %select_n.260), kind=kOutput, calls=%fused_computation.2 | convolution fusion | flops 402653184 | bytes 3276804 | tf_op jit(solution)/shard_map/fik,fkj->fij/dot_general | solution.py:48
  134.1 2.9 %fusion.2 = f32[128,256]{1,0:T(8,128)S(1)} fusion(f32[128,2048]{0,1:T(8,128)S(1)} %bitcast.139, f32[1,2048,1024]{2,1,0:T(8,128)} %all-gather.2.cloned.1.call-done, s32[]{:T(128)S(6)} %select_n.260), kind=kOutput, calls=%fused_computation.4 | convolution fusion | flops 402653184 | bytes 3276804 | tf_op jit(solution)/shard_map/fik,fkj->fij/dot_general | solution.py:48
  137.0 2.6 %fusion.45 = f32[1,1,128,256]{3,2,1,0:T(8,128)S(1)} fusion(f32[128,256]{1,0:T(8,128)S(1)} %fusion, f32[128,2048]{0,1:T(8,128)S(1)} %bitcast.140, f32[1,2048,1024]{2,1,0:T(8,128)} %all-gather.2.cloned.1.call-done, s32[]{:T(128)S(6)} %select_n.259), kind=kOutput, calls=%fused_computation.33 | convolution fusion | flops 402685952 | bytes 3407876 | tf_op jit(solution)/shard_map/fik,fkj->fij/dot_general | solution.py:48
  139.6 0.0 copy-done
  139.6 1.1 fusion.39
  140.7 4.3 %collective-permute-start.5 = (f32[2,1,128,256]{3,2,1,0:T(8,128)S(1)}, f32[2,1,128,256]{3,2,1,0:T(8,128)S(1)}, u32[]{:S(2)}, u32[]{:S(2)}) collective-permute-start(f32[2,1,128,256]{3,2,1,0:T(8,128)S(1)} %pad_maximum_fusion.1), channel_id=1, source_target_pairs={{0,1},{1,0},{2,3},{3,2},{4,5},{5,4},{6,7},{7,6},{8,9},{9,8},{10,11... | collective-permute-start | bytes 786440 | tf_op jit(solution)/shard_map/ppermute | solution.py:115
  145.0 1.1 fusion.8
  146.1 1.1 fusion.10
  147.3 1.1 fusion.33
  148.4 1.1 fusion.27
  149.5 2.2 %collective-permute-done.5 = f32[2,1,128,256]{3,2,1,0:T(8,128)S(1)} collective-permute-done((f32[2,1,128,256]{3,2,1,0:T(8,128)S(1)}, f32[2,1,128,256]{3,2,1,0:T(8,128)S(1)}, u32[]{:S(2)}, u32[]{:S(2)}) %collective-permute-start.5) | collective-permute-done | bytes 262176 | tf_op jit(solution)/shard_map/ppermute | solution.py:115
  151.8 1.4 fusion.51
  153.2 0.7 pad_maximum_fusion.2
  (19 shorter events, 0.4 us)
Async XLA Ops:
  6.5 124.8 %all-gather.2.cloned.1.call-start = ((), (), s32[]{:S(2)}) async-start(), calls=%async_computation.1 | async-start | bytes 8650752 | tf_op jit(solution)/shard_map/all_gather | solution.py:101
  7.8 12.3 %collective-permute-start.3 = (f32[1,128,128]{1,2,0:T(8,128)S(1)}, f32[1,128,128]{1,2,0:T(8,128)S(1)}, u32[]{:S(2)}, u32[]{:S(2)}) collective-permute-start(f32[1,128,128]{1,2,0:T(8,128)S(1)} %get-tuple-element.10), channel_id=1, source_target_pairs={{16,0},{32,16},{48,32},{64,50},{80,2},{82,66},{96,18},{98,82},{112... | collective-permute-start | bytes 196616 | tf_op jit(solution)/shard_map/ppermute | solution.py:66
  16.6 5.7 %collective-permute-start.2 = (f32[1,128,128]{1,2,0:T(8,128)S(1)}, f32[1,128,128]{1,2,0:T(8,128)S(1)}, u32[]{:S(2)}, u32[]{:S(2)}) collective-permute-start(f32[1,128,128]{1,2,0:T(8,128)S(1)} %get-tuple-element.11), channel_id=1, source_target_pairs={{32,0},{48,16},{64,34},{80,50},{96,2},{98,66},{112,18},{114,82},{1... | collective-permute-start | bytes 196616 | tf_op jit(solution)/shard_map/ppermute | solution.py:66
  17.9 4.4 %collective-permute-start.1 = (f32[1,128,128]{1,2,0:T(8,128)S(1)}, f32[1,128,128]{1,2,0:T(8,128)S(1)}, u32[]{:S(2)}, u32[]{:S(2)}) collective-permute-start(f32[1,128,128]{1,2,0:T(8,128)S(1)} %get-tuple-element.12), channel_id=1, source_target_pairs={{48,0},{64,18},{80,34},{96,50},{112,2},{114,66},{128,20},{130,84},... | collective-permute-start | bytes 196616 | tf_op jit(solution)/shard_map/ppermute | solution.py:66
  18.6 3.7 %collective-permute-start = (f32[1,128,128]{1,2,0:T(8,128)S(1)}, f32[1,128,128]{1,2,0:T(8,128)S(1)}, u32[]{:S(2)}, u32[]{:S(2)}) collective-permute-start(f32[1,128,128]{1,2,0:T(8,128)S(1)} %get-tuple-element.9), channel_id=1, source_target_pairs={{64,2},{80,18},{96,34},{112,50},{128,4},{130,68},{144,20},{146,84}... | collective-permute-start | bytes 196616 | tf_op jit(solution)/shard_map/ppermute | solution.py:66
  22.4 9.9 %collective-permute-start.4 = (f32[1,128,4,128]{3,1,2,0:T(8,128)S(1)}, f32[1,128,4,128]{3,1,2,0:T(8,128)S(1)}, u32[]{:S(2)}, u32[]{:S(2)}) collective-permute-start(f32[1,128,4,128]{3,1,2,0:T(8,128)S(1)} %get-tuple-element.14), channel_id=1, source_target_pairs={{0,1},{1,0},{2,3},{3,2},{4,5},{5,4},{6,7},{7,6},{8,9},{9,8},{10,11... | collective-permute-start | bytes 786440 | tf_op jit(solution)/shard_map/ppermute | solution.py:69
  32.9 1.3 copy-start.1
  36.9 27.7 %copy-start.2 = (f32[2,1]{0,1:T(1,128)S(1)}, f32[2,1]{0,1:T(1,128)}, u32[]{:S(2)}) copy-start(f32[2,1]{0,1:T(1,128)} %param.7) | copy-start | bytes 28
  36.9 28.4 %copy-start.3 = (s32[1,24]{1,0:T(1,128)S(1)}, s32[1,24]{1,0:T(1,128)}, u32[]{:S(2)}) copy-start(s32[1,24]{1,0:T(1,128)} %param.6) | copy-start | bytes 292
  36.9 79.0 %all-to-all-start = ((f32[8,2,1,128,256]{3,4,1,2,0:T(8,128)}), f32[8,2,1,128,256]{3,4,1,2,0:T(8,128)S(1)}, u32[]{:S(2)}, u32[]{:S(2)}) async-start(f32[8,2,1,128,256]{3,4,1,2,0:T(8,128)} %broadcast_in_dim.75), calls=%async_computation | async-start | bytes 4194304 | tf_op jit(solution)/shard_map/all_to_all | solution.py:11
  131.3 8.2 %copy-start = (f32[1,2048,1024]{2,1,0:T(8,128)S(1)}, f32[1,2048,1024]{2,1,0:T(8,128)}, u32[]{:S(2)}) copy-start(f32[1,2048,1024]{2,1,0:T(8,128)} %all-gather.2.cloned.1.call-done) | copy-start | bytes 25165828
  140.7 11.0 %collective-permute-start.5 = (f32[2,1,128,256]{3,2,1,0:T(8,128)S(1)}, f32[2,1,128,256]{3,2,1,0:T(8,128)S(1)}, u32[]{:S(2)}, u32[]{:S(2)}) collective-permute-start(f32[2,1,128,256]{3,2,1,0:T(8,128)S(1)} %pad_maximum_fusion.1), channel_id=1, source_target_pairs={{0,1},{1,0},{2,3},{3,2},{4,5},{5,4},{6,7},{7,6},{8,9},{9,8},{10,11... | collective-permute-start | bytes 786440 | tf_op jit(solution)/shard_map/ppermute | solution.py:115
Sparse Core Ops, SparseCore 0:
  35.1 96.1 all-gather.1

commit v11 on v10

--- a/solution.py
+++ b/solution.py
@@ -44,6 +44,26 @@
     return pairs
 
 
+def block_pairs(n_src, n_rcv, per_rcv):
+    pairs = []
+    for s in range(n_src):
+        for r in range(n_rcv):
+            if s > per_rcv * r:
+                pairs.append((s * n_rcv + r, (per_rcv * r + s % per_rcv) * n_rcv + s // per_rcv))
+    return pairs
+
+
+def trade_pairs(n_src, n_rcv, per_rcv, dist):
+    pairs = []
+    for q in range(n_src // per_rcv):
+        for u in range(per_rcv):
+            t = u ^ dist
+            for r in range(n_rcv):
+                if per_rcv * r + u > per_rcv * q + t:
+                    pairs.append(((per_rcv * q + u) * n_rcv + r, (per_rcv * q + t) * n_rcv + r))
+    return pairs
+
+
 def complex_prod(left_side, right_side):
     return jnp.einsum("fik,fkj->fij", left_side, right_side, precision=lax.Precision.HIGH)
 
@@ -58,19 +78,21 @@
     me_src = lax.axis_index("src")
     tiles = traces.reshape(comp_count, freq_count, TILE, per_rcv, TILE)
     assert comp_count == half_count
-    arrived = []
-    for step in range(per_rcv):
-        pick = (me_src % per_rcv + step) % per_rcv
-        sent = lax.dynamic_index_in_dim(tiles, pick, 3, keepdims=False)
-        sent = lax.dynamic_index_in_dim(sent, my_half, 0, keepdims=False)
-        got = lax.ppermute(sent, ("src", "rcv"), mirror_pairs(src_count, rcv_count, per_rcv, step))
-        arrived.append(jnp.swapaxes(got, 1, 2))
-    mine = jnp.stack(arrived, axis=2)
+    own = lax.dynamic_index_in_dim(tiles, my_half, 0, keepdims=False)
+    held = lax.ppermute(own, ("src", "rcv"), block_pairs(src_count, rcv_count, per_rcv))
+    slot = me_src % per_rcv
+    pieces = []
+    for dist in range(per_rcv):
+        piece = lax.dynamic_index_in_dim(held, slot ^ dist, 2, keepdims=False)
+        if dist:
+            piece = lax.ppermute(piece, ("src", "rcv"), trade_pairs(src_count, rcv_count, per_rcv, dist))
+        pieces.append(piece)
+    pieces = jnp.stack(pieces, axis=2)
+    mine = jnp.take(pieces, jnp.arange(per_rcv) ^ slot, axis=2)
+    mine = jnp.swapaxes(mine, 1, 3)
     theirs = lax.ppermute(mine, "int", [(0, 1), (1, 0)])
-    arrived = jnp.stack([mine, theirs])
-    arrived = jnp.take(arrived, (jnp.arange(comp_count) + my_half) % comp_count, axis=0)
-    order = (me_src % per_rcv - jnp.arange(per_rcv)) % per_rcv
-    mirrored = jnp.take(arrived, order, axis=3)
+    mirrored = jnp.stack([mine, theirs])
+    mirrored = jnp.take(mirrored, (jnp.arange(comp_count) + my_half) % comp_count, axis=0)
     marks = (missing[0] > 0)[None, None, None, :, None]
     filled = jnp.where(marks, mirrored, tiles).reshape(traces.shape)
     row_tiles = local_rows // TILE

time: 161 us -> 170 us (1.056)
  starting transfers between devices: 44.9 us -> 55 us
    all_to_all x1, starting transfers between devices: 27.3 us -> 36.4 us  [from_everyone(): return lax.all_to_all(copies, axis, split_axis=0, concat_axis=0, tiled=True)]
  transfers between devices with their start and end apart: 8 -> 8, of which waited for: 5 -> 5; matrix products, arithmetic and copies ran while one was open for 6% -> 5% of each run, Pallas kernels for 0% -> 0%
where the time goes in v11:
time: 170 us
  waiting for transfers between devices  76.6 us (45%)
  starting transfers between devices  55 us (32%)
  matrix products  13.8 us (8%)
  between operations  13.8 us (8%)
  local copies, waits for them, and re-layouts  7.45 us (4%)
  other arithmetic  2.95 us (2%)
    all_to_all x1, waiting for transfers between devices, from_everyone(): return lax.all_to_all(copies, axis, split_axis=0, concat_axis=0, tiled=True)  50 us
    all_to_all x1, starting transfers between devices, from_everyone(): return lax.all_to_all(copies, axis, split_axis=0, concat_axis=0, tiled=True)  36.4 us
    all_gather x1, waiting for transfers between devices, per_device(): slab_piece = lax.all_gather(slab_piece, 'src', axis=1, tiled=True)  14.3 us
    dot_general x8, matrix products, complex_prod(): jnp.einsum('fik,fkj->fij', left_side, right_side, precision=lax.Precision...  13.8 us
    ppermute x3, starting transfers between devices, per_device(): lax.ppermute(piece, ('src', 'rcv'), trade_pairs(src_count, rcv_count, per...  11.4 us
    ppermute x1, waiting for transfers between devices, per_device(): theirs = lax.ppermute(mine, 'int', [(0, 1), (1, 0)])  8.28 us
    ppermute x1, starting transfers between devices, per_device(): got = lax.ppermute(sent, 'int', [(0, 1), (1, 0)])  4.62 us
  transfers between devices with their start and end apart: 8, of which 5 were waited for; matrix products, arithmetic and copies ran while one was open for 5% of the time, Pallas kernels for 0%

profile of v11, /device:TPU:1, one launch (start us, length us, event | category | flops | bytes accessed | tf_op | source)
XLA Modules:
  0.0 169.7 jit_solution(18122271393515774777)
XLA Ops:
  6.5 0.0 copy-start.3
  6.5 0.0 all-gather.2.cloned.1.call-start
  6.5 1.2 reshape.336
  7.8 0.7 collective-permute-start
  8.6 0.0 copy-done.3
  8.6 0.0 collective-permute-done
  8.7 1.3 collective-permute-start.3
  10.0 1.3 collective-permute-start.2
  11.3 8.8 %collective-permute-start.1 = (f32[1,128,128]{2,1,0:T(8,128)S(1)}, f32[1,128,128]{2,1,0:T(8,128)S(1)}, u32[]{:S(2)}, u32[]{:S(2)}) collective-permute-start(f32[1,128,128]{2,1,0:T(8,128)S(1)} %get-tuple-element.14), channel_id=1, source_target_pairs={{2,18},{4,20},{6,22},{8,24},{10,26},{12,28},{14,30},{16,0},{18,2},... | collective-permute-start | bytes 196616 | tf_op jit(solution)/shard_map/ppermute | solution.py:88
  20.1 0.0 collective-permute-done.3
  20.1 2.1 %collective-permute-done.2 = f32[1,128,128]{2,1,0:T(8,128)S(1)} collective-permute-done((f32[1,128,128]{2,1,0:T(8,128)S(1)}, f32[1,128,128]{2,1,0:T(8,128)S(1)}, u32[]{:S(2)}, u32[]{:S(2)}) %collective-permute-start.2) | collective-permute-done | bytes 65568 | tf_op jit(solution)/shard_map/ppermute | solution.py:88
  22.2 0.0 collective-permute-done.1
  22.3 0.6 gather_fusion
  22.8 0.1 fusion.49
  23.0 1.9 %collective-permute-start.4 = (f32[1,128,4,128]{1,3,2,0:T(8,128)S(1)}, f32[1,128,4,128]{1,3,2,0:T(8,128)S(1)}, u32[]{:S(2)}, u32[]{:S(2)}) collective-permute-start(f32[1,128,4,128]{1,3,2,0:T(8,128)S(1)} %get-tuple-element.10), channel_id=1, source_target_pairs={{0,1},{1,0},{2,3},{3,2},{4,5},{5,4},{6,7},{7,6},{8,9},{9,8},{10,11... | collective-permute-start | bytes 786440 | tf_op jit(solution)/shard_map/ppermute | solution.py:93
  24.9 0.1 broadcast_bitcast_fusion.1
  25.0 8.3 %collective-permute-done.4 = f32[1,128,4,128]{1,3,2,0:T(8,128)S(1)} collective-permute-done((f32[1,128,4,128]{1,3,2,0:T(8,128)S(1)}, f32[1,128,4,128]{1,3,2,0:T(8,128)S(1)}, u32[]{:S(2)}, u32[]{:S(2)}) %collective-permute-start.4) | collective-permute-done | bytes 262176 | tf_op jit(solution)/shard_map/ppermute | solution.py:93
  33.3 0.0 copy-start.1
  33.3 0.2 copy.49
  33.5 0.6 gather_fusion.1
  34.1 0.3 copy.57
  34.5 0.2 gather.18
  34.7 0.0 copy-done.1
  34.7 0.1 fusion.48
  34.8 0.7 copy.62
  35.5 0.0 all-gather.2.cloned.1.call-update
  35.5 0.2 copy.52
  35.7 0.2 copy.50
  35.9 0.1 dynamic-slice_select_fusion.2
  36.0 1.6 broadcast_in_dim.65
  37.6 0.0 copy-start.2
  37.6 0.0 copy-start.4
  37.6 36.4 %all-to-all-start = ((f32[8,2,1,128,256]{3,4,1,2,0:T(8,128)}), f32[8,2,1,128,256]{3,4,1,2,0:T(8,128)S(1)}, u32[]{:S(2)}, u32[]{:S(2)}) async-start(f32[8,2,1,128,256]{3,4,1,2,0:T(8,128)} %broadcast_in_dim.65), calls=%async_computation | async-start | bytes 4194304 | tf_op jit(solution)/shard_map/all_to_all | solution.py:11
  74.0 0.1 copy.61
  74.2 0.1 gt.15
  74.3 0.1 broadcast_bitcast_fusion
  74.4 0.0 copy-done.2
  74.4 0.6 fusion.66
  75.0 0.0 copy-done.4
  75.0 0.1 convert_reduce_fusion
  75.1 0.1 copy.60
  75.2 0.1 select_select_fusion
  75.3 50.0 %all-to-all-done = f32[8,2,1,128,256]{3,4,1,2,0:T(8,128)S(1)} async-done(((f32[8,2,1,128,256]{3,4,1,2,0:T(8,128)}), f32[8,2,1,128,256]{3,4,1,2,0:T(8,128)S(1)}, u32[]{:S(2)}, u32[]{:S(2)}) %all-to-all-start) | async-done | bytes 2097184 | tf_op jit(solution)/shard_map/all_to_all | solution.py:11
  125.3 0.2 copy.56
  125.5 0.2 broadcast_multiply_fusion
  125.7 0.2 fusion.65
  125.9 14.3 %all-gather.2.cloned.1.call-done = f32[1,2048,1024]{2,1,0:T(8,128)} async-done(((f32[1,64,1024]{2,1,0:T(8,128)}), f32[1,2048,1024]{2,1,0:T(8,128)}) %all-gather.2.cloned.1.call-update) | async-done | bytes 8388624 | tf_op jit(solution)/shard_map/all_gather | solution.py:123
  140.2 0.0 copy-start
  140.2 2.7 %fusion = f32[128,256]{1,0:T(8,128)S(1)} fusion(f32[128,2048]{0,1:T(8,128)S(1)} %bitcast.125, f32[1,2048,1024]{2,1,0:T(8,128)} %all-gather.2.cloned.1.call-done, s32[]{:T(128)S(6)} %select_n.187), kind=kOutput, calls=%fused_computation.2 | convolution fusion | flops 402653184 | bytes 3276804 | tf_op jit(solution)/shard_map/fik,fkj->fij/dot_general | solution.py:68
  143.0 2.9 %fusion.2 = f32[128,256]{1,0:T(8,128)S(1)} fusion(f32[128,2048]{0,1:T(8,128)S(1)} %bitcast.129, f32[1,2048,1024]{2,1,0:T(8,128)} %all-gather.2.cloned.1.call-done, s32[]{:T(128)S(6)} %select_n.187), kind=kOutput, calls=%fused_computation.4 | convolution fusion | flops 402653184 | bytes 3276804 | tf_op jit(solution)/shard_map/fik,fkj->fij/dot_general | solution.py:68
  145.9 2.6 %fusion.45 = f32[1,1,128,256]{3,2,1,0:T(8,128)S(1)} fusion(f32[128,256]{1,0:T(8,128)S(1)} %fusion, f32[128,2048]{0,1:T(8,128)S(1)} %bitcast.130, f32[1,2048,1024]{2,1,0:T(8,128)} %all-gather.2.cloned.1.call-done, s32[]{:T(128)S(6)} %select_n.186), kind=kOutput, calls=%fused_computation.33 | convolution fusion | flops 402685952 | bytes 3407876 | tf_op jit(solution)/shard_map/fik,fkj->fij/dot_general | solution.py:68
  148.5 0.0 copy-done
  148.5 1.1 fusion.39
  149.6 4.6 %collective-permute-start.5 = (f32[2,1,128,256]{3,2,1,0:T(8,128)S(1)}, f32[2,1,128,256]{3,2,1,0:T(8,128)S(1)}, u32[]{:S(2)}, u32[]{:S(2)}) collective-permute-start(f32[2,1,128,256]{3,2,1,0:T(8,128)S(1)} %pad_maximum_fusion), channel_id=1, source_target_pairs={{0,1},{1,0},{2,3},{3,2},{4,5},{5,4},{6,7},{7,6},{8,9},{9,8},{10,11... | collective-permute-start | bytes 786440 | tf_op jit(solution)/shard_map/ppermute | solution.py:137
  154.3 1.1 fusion.8
  155.4 1.1 fusion.10
  156.5 1.1 fusion.33
  157.7 1.1 fusion.27
  158.8 1.9 %collective-permute-done.5 = f32[2,1,128,256]{3,2,1,0:T(8,128)S(1)} collective-permute-done((f32[2,1,128,256]{3,2,1,0:T(8,128)S(1)}, f32[2,1,128,256]{3,2,1,0:T(8,128)S(1)}, u32[]{:S(2)}, u32[]{:S(2)}) %collective-permute-start.5) | collective-permute-done | bytes 262176 | tf_op jit(solution)/shard_map/ppermute | solution.py:137
  160.7 1.4 fusion.52
  162.1 0.7 pad_maximum_fusion.1
  (18 shorter events, 0.3 us)
Async XLA Ops:
  6.5 2.1 %copy-start.3 = (s32[1,4]{1,0:T(1,128)S(1)}, s32[1,4]{1,0:T(1,128)}, u32[]{:S(2)}) copy-start(s32[1,4]{1,0:T(1,128)} %param.5) | copy-start | bytes 52
  6.5 133.7 %all-gather.2.cloned.1.call-start = ((), (), s32[]{:S(2)}) async-start(), calls=%async_computation.1 | async-start | bytes 8650752 | tf_op jit(solution)/shard_map/all_gather | solution.py:123
  7.8 0.8 collective-permute-start
  8.7 11.4 %collective-permute-start.3 = (f32[1,128,128]{2,1,0:T(8,128)S(1)}, f32[1,128,128]{2,1,0:T(8,128)S(1)}, u32[]{:S(2)}, u32[]{:S(2)}) collective-permute-start(f32[1,128,128]{2,1,0:T(8,128)S(1)} %get-tuple-element.12), channel_id=1, source_target_pairs={{2,50},{4,52},{6,54},{8,56},{10,58},{12,60},{14,62},{18,34},{20,36... | collective-permute-start | bytes 196616 | tf_op jit(solution)/shard_map/ppermute | solution.py:88
  10.0 12.3 %collective-permute-start.2 = (f32[1,128,128]{2,1,0:T(8,128)S(1)}, f32[1,128,128]{2,1,0:T(8,128)S(1)}, u32[]{:S(2)}, u32[]{:S(2)}) collective-permute-start(f32[1,128,128]{2,1,0:T(8,128)S(1)} %get-tuple-element.13), channel_id=1, source_target_pairs={{2,34},{4,36},{6,38},{8,40},{10,42},{12,44},{14,46},{18,50},{20,52... | collective-permute-start | bytes 196616 | tf_op jit(solution)/shard_map/ppermute | solution.py:88
  11.3 11.0 %collective-permute-start.1 = (f32[1,128,128]{2,1,0:T(8,128)S(1)}, f32[1,128,128]{2,1,0:T(8,128)S(1)}, u32[]{:S(2)}, u32[]{:S(2)}) collective-permute-start(f32[1,128,128]{2,1,0:T(8,128)S(1)} %get-tuple-element.14), channel_id=1, source_target_pairs={{2,18},{4,20},{6,22},{8,24},{10,26},{12,28},{14,30},{16,0},{18,2},... | collective-permute-start | bytes 196616 | tf_op jit(solution)/shard_map/ppermute | solution.py:88
  23.0 10.3 %collective-permute-start.4 = (f32[1,128,4,128]{1,3,2,0:T(8,128)S(1)}, f32[1,128,4,128]{1,3,2,0:T(8,128)S(1)}, u32[]{:S(2)}, u32[]{:S(2)}) collective-permute-start(f32[1,128,4,128]{1,3,2,0:T(8,128)S(1)} %get-tuple-element.10), channel_id=1, source_target_pairs={{0,1},{1,0},{2,3},{3,2},{4,5},{5,4},{6,7},{7,6},{8,9},{9,8},{10,11... | collective-permute-start | bytes 786440 | tf_op jit(solution)/shard_map/ppermute | solution.py:93
  33.3 1.4 copy-start.1
  37.6 36.7 %copy-start.2 = (f32[2,1]{0,1:T(1,128)S(1)}, f32[2,1]{0,1:T(1,128)}, u32[]{:S(2)}) copy-start(f32[2,1]{0,1:T(1,128)} %param.7) | copy-start | bytes 28
  37.6 37.4 %copy-start.4 = (s32[1,24]{1,0:T(1,128)S(1)}, s32[1,24]{1,0:T(1,128)}, u32[]{:S(2)}) copy-start(s32[1,24]{1,0:T(1,128)} %param.6) | copy-start | bytes 292
  37.6 87.7 %all-to-all-start = ((f32[8,2,1,128,256]{3,4,1,2,0:T(8,128)}), f32[8,2,1,128,256]{3,4,1,2,0:T(8,128)S(1)}, u32[]{:S(2)}, u32[]{:S(2)}) async-start(f32[8,2,1,128,256]{3,4,1,2,0:T(8,128)} %broadcast_in_dim.65), calls=%async_computation | async-start | bytes 4194304 | tf_op jit(solution)/shard_map/all_to_all | solution.py:11
  140.2 8.2 %copy-start = (f32[1,2048,1024]{2,1,0:T(8,128)S(1)}, f32[1,2048,1024]{2,1,0:T(8,128)}, u32[]{:S(2)}) copy-start(f32[1,2048,1024]{2,1,0:T(8,128)} %all-gather.2.cloned.1.call-done) | copy-start | bytes 25165828
  149.6 11.0 %collective-permute-start.5 = (f32[2,1,128,256]{3,2,1,0:T(8,128)S(1)}, f32[2,1,128,256]{3,2,1,0:T(8,128)S(1)}, u32[]{:S(2)}, u32[]{:S(2)}) collective-permute-start(f32[2,1,128,256]{3,2,1,0:T(8,128)S(1)} %pad_maximum_fusion), channel_id=1, source_target_pairs={{0,1},{1,0},{2,3},{3,2},{4,5},{5,4},{6,7},{7,6},{8,9},{9,8},{10,11... | collective-permute-start | bytes 786440 | tf_op jit(solution)/shard_map/ppermute | solution.py:137
Sparse Core Ops, SparseCore 0:
  35.7 104.5 all-gather.1

commit v12 on v7

v12 whole, which is shorter than its diff:
```python
import jax
import jax.numpy as jnp
from jax import lax
from jax.sharding import PartitionSpec as P

TILE = 128


def from_everyone(x, axis):
    copies = jnp.broadcast_to(x, (lax.axis_size(axis), *x.shape))
    return lax.all_to_all(copies, axis, split_axis=0, concat_axis=0, tiled=True)


def joined_along(pieces, dim):
    pieces = jnp.moveaxis(pieces, 0, dim)
    lengths = pieces.shape
    return pieces.reshape(*lengths[:dim], lengths[dim] * lengths[dim + 1], *lengths[dim + 2 :])


def collect(x, axis, dim):
    pieces = from_everyone(x, axis)
    return joined_along(pieces, dim)


def in_blocks(x, dim, count):
    before, after = (x.shape[:dim], x.shape[dim + 1 :])
    return jnp.moveaxis(x.reshape(*before, count, -1, *after), dim, 0)


def sent_and_summed(x, axis, dim):
    pieces = in_blocks(x, dim, lax.axis_size(axis))
    arrived = lax.all_to_all(pieces, axis, split_axis=0, concat_axis=0, tiled=True)
    return arrived.sum(axis=0)


def mirror_pairs(n_src, n_rcv, per_rcv, step):
    pairs = []
    for s in range(n_src):
        for r in range(n_rcv):
            t = (s % per_rcv + step) % per_rcv
            dest_s = per_rcv * r + t
            if s > dest_s:
                pairs.append((s * n_rcv + r, dest_s * n_rcv + s // per_rcv))
    return pairs


def block_pairs(n_src, n_rcv, per_rcv):
    pairs = []
    for s in range(n_src):
        for r in range(n_rcv):
            if s > per_rcv * r:
                pairs.append((s * n_rcv + r, (per_rcv * r + s % per_rcv) * n_rcv + s // per_rcv))
    return pairs


def trade_pairs(n_src, n_rcv, per_rcv, dist):
    pairs = []
    for q in range(n_src // per_rcv):
        for u in range(per_rcv):
            t = u ^ dist
            for r in range(n_rcv):
                if per_rcv * r + u > per_rcv * q + t:
                    pairs.append(((per_rcv * q + u) * n_rcv + r, (per_rcv * q + t) * n_rcv + r))
    return pairs


def complex_prod(left_side, right_side):
    return jnp.einsum("fik,fkj->fij", left_side, right_side, precision=lax.Precision.HIGH)


def per_device(traces, missing, aperture, wavelet):
    half_count = lax.axis_size("int")
    my_half = lax.axis_index("int")
    rcv_count = lax.axis_size("rcv")
    src_count = lax.axis_size("src")
    me_src = lax.axis_index("src")
    me_rcv = lax.axis_index("rcv")
    comp_count, freq_count, local_rows, local_cols = traces.shape
    assert comp_count == half_count == 2 and local_rows == TILE
    per_rcv = local_cols // TILE
    swap = [(0, 1), (1, 0)]
    tiles = traces.reshape(comp_count, freq_count, TILE, per_rcv, TILE)
    arrived = []
    for step in range(per_rcv):
        pick = (me_src % per_rcv + step) % per_rcv
        sent = lax.dynamic_index_in_dim(tiles, pick, 3, keepdims=False)
        sent = lax.dynamic_index_in_dim(sent, my_half, 0, keepdims=False)
        got = lax.ppermute(sent, ("src", "rcv"), mirror_pairs(src_count, rcv_count, per_rcv, step))
        arrived.append(jnp.swapaxes(got, 1, 2))
    arrived = jnp.stack(arrived, axis=2)
    order = (me_src % per_rcv - jnp.arange(per_rcv)) % per_rcv
    mine = jnp.take(arrived, order, axis=2)
    marks = (missing[0] > 0)[None, None, :, None]
    own_comp = lax.dynamic_index_in_dim(tiles, my_half, 0, keepdims=False)
    filled_mine = jnp.where(marks, mine, own_comp)

    local_blocks = me_rcv * per_rcv + jnp.arange(per_rcv, dtype=jnp.int32)
    chosen = (aperture[0][:, None] == local_blocks[None, :]).astype(jnp.float32).sum(axis=0)
    left = (filled_mine * chosen[None, None, :, None]).reshape(freq_count, TILE, local_cols)
    left_mine = collect(left, "rcv", 2)
    right = lax.all_gather(filled_mine.reshape(freq_count, TILE, local_cols), "src", axis=1, tiled=True)
    left_other = lax.ppermute(left_mine, "int", swap)
    sign = jnp.where(my_half == 0, 1.0, -1.0).astype(jnp.float32)
    out_cols = local_cols // half_count

    def half_product(which):
        cols = lax.dynamic_slice_in_dim(right, which * out_cols, out_cols, axis=2)
        real_part = sign * complex_prod(left_mine, cols)
        imag_part = complex_prod(left_other, cols)
        return jnp.stack([real_part, imag_part])

    sent = half_product(1 - my_half)
    got = lax.ppermute(sent, "int", swap)
    my_share = half_product(my_half) + got

    theirs = lax.ppermute(mine, "int", swap)
    other_comp = lax.dynamic_index_in_dim(tiles, 1 - my_half, 0, keepdims=False)
    filled_other = jnp.where(marks, theirs, other_comp)
    both = jnp.stack([filled_mine, filled_other])
    both = jnp.take(both, (jnp.arange(comp_count) + my_half) % comp_count, axis=0)
    both = both.reshape(comp_count, freq_count, TILE, local_cols)
    kept_data = lax.dynamic_slice_in_dim(both, my_half * out_cols, out_cols, axis=3)
    w_real = wavelet[0][:, None, None]
    w_imag = wavelet[1][:, None, None]
    out_real = kept_data[0] - (w_real * my_share[0] - w_imag * my_share[1])
    out_imag = kept_data[1] - (w_real * my_share[1] + w_imag * my_share[0])
    return jnp.stack([out_real, out_imag])


def solution(mesh):
    placed = (P(None, None, "src", "rcv"), P("src", "rcv"), P("src", None), P())
    return jax.shard_map(
        per_device,
        mesh=mesh,
        in_specs=placed,
        out_specs=P(None, None, "src", ("rcv", "int")),
        check_vma=False,
    )
```

time: 172 us -> 204 us (1.19)
  blocking collectives: 0 us -> 75.6 us
  starting transfers between devices: 63.9 us -> 20.5 us
  local copies, waits for them, and re-layouts: 8.47 us -> 4.28 us
  other arithmetic: 3.4 us -> 5.47 us
    all_to_all x0 -> x1, blocking collectives: none -> 75.6 us  [from_everyone(): return lax.all_to_all(copies, axis, split_axis=0, concat_axis=0, tiled=True)]
    ppermute x1 -> x3, waiting for transfers between devices: 1.74 us -> 65 us  [the longest x1 63.1 us: per_device(): theirs = lax.ppermute(mine, 'int', swap)]
    all_to_all x1 -> x0, waiting for transfers between devices: 48.3 us -> none  [from_everyone(): return lax.all_to_all(copies, axis, split_axis=0, concat_axis=0, tiled=True)]
    all_to_all x1 -> x0, starting transfers between devices: 47.5 us -> none  [from_everyone(): return lax.all_to_all(copies, axis, split_axis=0, concat_axis=0, tiled=True)]
    all_gather x1, waiting for transfers between devices: 14.2 us -> 0.02 us  [per_device(): lax.all_gather(filled_mine.reshape(freq_count, TILE, local_cols), 'src',...]
    ppermute x1 -> x3, starting transfers between devices: 4.95 us -> 9.1 us  [the longest x1 5.13 us: per_device(): left_other = lax.ppermute(left_mine, 'int', swap)]
    dot_general x8 -> x4, matrix products: 13.8 us -> 14.3 us  [complex_prod(): jnp.einsum('fik,fkj->fij', left_side, right_side, precision=lax.Precision...]
  transfers between devices with their start and end apart: 7 -> 8, of which waited for: 4 -> 3; matrix products, arithmetic and copies ran while one was open for 6% -> 5% of each run, Pallas kernels for 0% -> 0%
where the time goes in v12:
time: 204 us; the launch traced here: 202 us
  blocking collectives  75.6 us (37%)
  waiting for transfers between devices  68 us (33%)
  starting transfers between devices  20.5 us (10%)
  matrix products  14.3 us (7%)
  between operations  13.7 us (7%)
  other arithmetic  5.47 us (3%)
  local copies, waits for them, and re-layouts  4.28 us (2%)
    all_to_all x1, blocking collectives, from_everyone(): return lax.all_to_all(copies, axis, split_axis=0, concat_axis=0, tiled=True)  75.6 us
    ppermute x1, waiting for transfers between devices, per_device(): theirs = lax.ppermute(mine, 'int', swap)  63.1 us
    dot_general x4, matrix products, complex_prod(): jnp.einsum('fik,fkj->fij', left_side, right_side, precision=lax.Precision...  14.3 us
    ppermute x4, starting transfers between devices, per_device(): lax.ppermute(sent, ('src', 'rcv'), mirror_pairs(src_count, rcv_count, per...  11.4 us
    ppermute x1, starting transfers between devices, per_device(): left_other = lax.ppermute(left_mine, 'int', swap)  5.13 us
  transfers between devices with their start and end apart: 8, of which 3 were waited for; matrix products, arithmetic and copies ran while one was open for 5% of the time, Pallas kernels for 0%

profile of v12, /device:TPU:1, one launch (start us, length us, event | category | flops | bytes accessed | tf_op | source)
XLA Modules:
  0.0 201.9 jit_solution(4792944895903186363)
XLA Ops:
  6.5 0.0 copy-start.2
  6.5 0.0 all-gather.2.cloned.1.call-start
  6.5 1.2 copy.40
  7.8 0.7 collective-permute-start
  8.5 8.8 %collective-permute-start.3 = (f32[1,128,128]{1,2,0:T(8,128)S(1)}, f32[1,128,128]{1,2,0:T(8,128)S(1)}, u32[]{:S(2)}, u32[]{:S(2)}) collective-permute-start(f32[1,128,128]{1,2,0:T(8,128)S(1)} %get-tuple-element.10), channel_id=1, source_target_pairs={{16,0},{32,16},{48,32},{64,50},{80,2},{82,66},{96,18},{98,82},{112... | collective-permute-start | bytes 196616 | tf_op jit(solution)/shard_map/ppermute | solution.py:88
  17.3 1.3 collective-permute-start.2
  18.6 0.7 collective-permute-start.1
  19.3 0.7 compare_bitcast_fusion
  20.0 0.1 broadcast_bitcast_fusion.1
  20.1 0.0 collective-permute-done
  20.1 0.0 collective-permute-done.3
  20.1 2.9 %collective-permute-done.2 = f32[1,128,128]{1,2,0:T(8,128)S(1)} collective-permute-done((f32[1,128,128]{1,2,0:T(8,128)S(1)}, f32[1,128,128]{1,2,0:T(8,128)S(1)}, u32[]{:S(2)}, u32[]{:S(2)}) %collective-permute-start.2) | collective-permute-done | bytes 65568 | tf_op jit(solution)/shard_map/ppermute | solution.py:88
  23.0 0.0 collective-permute-done.1
  23.0 0.6 gather_fusion
  23.6 0.1 copy.52
  23.7 0.0 copy-start.1
  23.7 0.9 bitcast_select_fusion.1
  24.6 0.0 all-gather.2.cloned.1.call-update
  24.7 0.0 copy-done.2
  24.7 0.2 convert_reduce_fusion
  24.9 0.1 broadcast_bitcast_fusion
  24.9 0.3 fusion.36
  25.2 0.1 broadcast_in_dim.78
  25.4 75.6 %all_to_all.5 = f32[8,1,128,512]{2,3,1,0:T(8,128)S(1)} all-to-all(f32[8,1,128,512]{2,3,1,0:T(8,128)S(1)} %broadcast_in_dim.78), channel_id=1, replica_groups=mesh['src'=32,'rcv'=8,'int'=2] {'rcv'}, dimensions={0} | all-to-all | bytes 4194304 | tf_op jit(solution)/shard_map/all_to_all | solution.py:11
  101.0 5.1 %collective-permute-start.5 = (f32[1,128,4096]{1,2,0:T(8,128)S(1)}, f32[1,128,4096]{1,2,0:T(8,128)}, u32[]{:S(2)}, u32[]{:S(2)}) collective-permute-start(f32[1,128,4096]{1,2,0:T(8,128)S(1)} %bitcast.120), channel_id=1, source_target_pairs={{0,1},{1,0},{2,3},{3,2},{4,5},{5,4},{6,7},{7,6},{8,9},{9,8},{10,11... | collective-permute-start | bytes 6291464 | tf_op jit(solution)/shard_map/ppermute | solution.py:102
  106.1 0.0 copy-done.1
  106.2 0.6 fusion.49
  106.7 0.1 bitcast_select_fusion.2
  106.8 1.9 collective-permute-start.4
  108.8 0.1 copy.61
  108.9 0.1 copy.50
  109.1 0.1 fusion.37
  109.2 63.1 %collective-permute-done.4 = f32[1,128,4,128]{3,1,2,0:T(8,128)} collective-permute-done((f32[1,128,4,128]{3,1,2,0:T(8,128)S(1)}, f32[1,128,4,128]{3,1,2,0:T(8,128)}, u32[]{:S(2)}, u32[]{:S(2)}) %collective-permute-start.4) | collective-permute-done | bytes 262176 | tf_op jit(solution)/shard_map/ppermute | solution.py:116
  172.3 1.0 fusion.38
  173.3 0.1 maximum_bitcast_fusion
  173.3 0.6 gather_fusion.1
  173.9 0.3 copy.51
  174.3 0.2 gather.19
  174.5 0.1 dynamic-slice_select_fusion
  174.6 0.0 collective-permute-done.5
  174.6 0.0 all-gather.2.cloned.1.call-done
  174.6 0.0 copy-start
  174.6 4.8 %fusion.19 = f32[1,1,128,256]{3,2,1,0:T(8,128)S(1)} fusion(f32[1,4096,512]{1,2,0:T(8,128)} %all-gather.2.cloned.1.call-done, s32[]{:T(128)S(6)} %select_n.251, f32[1,128,4096]{1,2,0:T(8,128)} %collective-permute-done.5), kind=kOutput, calls=%fused_computation.17 | convolution fusion | flops 805306368 | bytes 6422532 | tf_op jit(solution)/shard_map/fik,fkj->fij/dot_general | solution.py:68
  179.4 4.0 %fusion.33 = f32[1,1,128,256]{3,2,1,0:T(8,128)S(1)} fusion(f32[128,4096]{0,1:T(8,128)S(1)} %bitcast.121, f32[1,4096,512]{1,2,0:T(8,128)} %all-gather.2.cloned.1.call-done, s32[]{:T(128)S(6)} %select_n.251, f32[]{:T(128)S(6)} %select_n.246), kind=kOutput, calls=%fused_computation.21 | convolution fusion | flops 805339136 | bytes 6422536 | tf_op jit(solution)/shard_map/fik,fkj->fij/dot_general | solution.py:68
  183.5 2.0 %collective-permute-start.6 = (f32[2,1,128,256]{3,2,1,0:T(8,128)S(1)}, f32[2,1,128,256]{3,2,1,0:T(8,128)S(1)}, u32[]{:S(2)}, u32[]{:S(2)}) collective-permute-start(f32[2,1,128,256]{3,2,1,0:T(8,128)S(1)} %pad_maximum_fusion), channel_id=1, source_target_pairs={{0,1},{1,0},{2,3},{3,2},{4,5},{5,4},{6,7},{7,6},{8,9},{9,8},{10,11... | collective-permute-start | bytes 786440 | tf_op jit(solution)/shard_map/ppermute | solution.py:113
  185.5 0.0 copy-done
  185.5 3.6 %fusion.14 = f32[1,1,128,256]{3,2,1,0:T(8,128)S(1)} fusion(f32[1,4096,512]{1,2,0:T(8,128)S(1)} %copy-done, s32[]{:T(128)S(6)} %select_n.245, f32[1,128,4096]{1,2,0:T(8,128)} %collective-permute-done.5), kind=kOutput, calls=%fused_computation.16 | convolution fusion | flops 805306368 | bytes 6422532 | tf_op jit(solution)/shard_map/fik,fkj->fij/dot_general | solution.py:68
  189.1 2.0 fusion.27
  191.1 2.0 collective-permute-done.6
  193.1 1.2 slice_subtract_fusion.1
  194.3 0.7 pad_maximum_fusion.1
  (12 shorter events, 0.2 us)
Async XLA Ops:
  6.5 18.2 %copy-start.2 = (s32[1,24]{1,0:T(1,128)S(1)}, s32[1,24]{1,0:T(1,128)}, u32[]{:S(2)}) copy-start(s32[1,24]{1,0:T(1,128)} %param.6) | copy-start | bytes 292
  6.5 168.1 %all-gather.2.cloned.1.call-start = ((), (), s32[]{:S(2)}) async-start(), calls=%async_computation.1 | async-start | bytes 8650752 | tf_op jit(solution)/shard_map/all_gather | solution.py:101
  7.8 12.3 %collective-permute-start = (f32[1,128,128]{1,2,0:T(8,128)S(1)}, f32[1,128,128]{1,2,0:T(8,128)S(1)}, u32[]{:S(2)}, u32[]{:S(2)}) collective-permute-start(f32[1,128,128]{1,2,0:T(8,128)S(1)} %get-tuple-element.9), channel_id=1, source_target_pairs={{64,2},{80,18},{96,34},{112,50},{128,4},{130,68},{144,20},{146,84}... | collective-permute-start | bytes 196616 | tf_op jit(solution)/shard_map/ppermute | solution.py:88
  8.5 11.6 %collective-permute-start.3 = (f32[1,128,128]{1,2,0:T(8,128)S(1)}, f32[1,128,128]{1,2,0:T(8,128)S(1)}, u32[]{:S(2)}, u32[]{:S(2)}) collective-permute-start(f32[1,128,128]{1,2,0:T(8,128)S(1)} %get-tuple-element.10), channel_id=1, source_target_pairs={{16,0},{32,16},{48,32},{64,50},{80,2},{82,66},{96,18},{98,82},{112... | collective-permute-start | bytes 196616 | tf_op jit(solution)/shard_map/ppermute | solution.py:88
  17.3 5.7 %collective-permute-start.2 = (f32[1,128,128]{1,2,0:T(8,128)S(1)}, f32[1,128,128]{1,2,0:T(8,128)S(1)}, u32[]{:S(2)}, u32[]{:S(2)}) collective-permute-start(f32[1,128,128]{1,2,0:T(8,128)S(1)} %get-tuple-element.11), channel_id=1, source_target_pairs={{32,0},{48,16},{64,34},{80,50},{96,2},{98,66},{112,18},{114,82},{1... | collective-permute-start | bytes 196616 | tf_op jit(solution)/shard_map/ppermute | solution.py:88
  18.6 4.4 %collective-permute-start.1 = (f32[1,128,128]{1,2,0:T(8,128)S(1)}, f32[1,128,128]{1,2,0:T(8,128)S(1)}, u32[]{:S(2)}, u32[]{:S(2)}) collective-permute-start(f32[1,128,128]{1,2,0:T(8,128)S(1)} %get-tuple-element.12), channel_id=1, source_target_pairs={{48,0},{64,18},{80,34},{96,50},{112,2},{114,66},{128,20},{130,84},... | collective-permute-start | bytes 196616 | tf_op jit(solution)/shard_map/ppermute | solution.py:88
  23.7 82.4 %copy-start.1 = (f32[2,1]{0,1:T(1,128)S(1)}, f32[2,1]{0,1:T(1,128)}, u32[]{:S(2)}) copy-start(f32[2,1]{0,1:T(1,128)} %param.7) | copy-start | bytes 28
  101.0 73.6 %collective-permute-start.5 = (f32[1,128,4096]{1,2,0:T(8,128)S(1)}, f32[1,128,4096]{1,2,0:T(8,128)}, u32[]{:S(2)}, u32[]{:S(2)}) collective-permute-start(f32[1,128,4096]{1,2,0:T(8,128)S(1)} %bitcast.120), channel_id=1, source_target_pairs={{0,1},{1,0},{2,3},{3,2},{4,5},{5,4},{6,7},{7,6},{8,9},{9,8},{10,11... | collective-permute-start | bytes 6291464 | tf_op jit(solution)/shard_map/ppermute | solution.py:102
  106.8 65.4 %collective-permute-start.4 = (f32[1,128,4,128]{3,1,2,0:T(8,128)S(1)}, f32[1,128,4,128]{3,1,2,0:T(8,128)}, u32[]{:S(2)}, u32[]{:S(2)}) collective-permute-start(f32[1,128,4,128]{3,1,2,0:T(8,128)S(1)} %bitcast_select_fusion.2), channel_id=1, source_target_pairs={{0,1},{1,0},{2,3},{3,2},{4,5},{5,4},{6,7},{7,6},{8,9},{9,8},{10,11... | collective-permute-start | bytes 786440 | tf_op jit(solution)/shard_map/ppermute | solution.py:116
  174.6 10.9 %copy-start = (f32[1,4096,512]{1,2,0:T(8,128)S(1)}, f32[1,4096,512]{1,2,0:T(8,128)}, u32[]{:S(2)}) copy-start(f32[1,4096,512]{1,2,0:T(8,128)} %all-gather.2.cloned.1.call-done) | copy-start | bytes 25165828
  183.5 9.6 %collective-permute-start.6 = (f32[2,1,128,256]{3,2,1,0:T(8,128)S(1)}, f32[2,1,128,256]{3,2,1,0:T(8,128)S(1)}, u32[]{:S(2)}, u32[]{:S(2)}) collective-permute-start(f32[2,1,128,256]{3,2,1,0:T(8,128)S(1)} %pad_maximum_fusion), channel_id=1, source_target_pairs={{0,1},{1,0},{2,3},{3,2},{4,5},{5,4},{6,7},{7,6},{8,9},{9,8},{10,11... | collective-permute-start | bytes 786440 | tf_op jit(solution)/shard_map/ppermute | solution.py:113
Sparse Core Ops, SparseCore 0:
  24.8 118.3 all-gather.1

commit v13 on v7

--- a/solution.py
+++ b/solution.py
@@ -57,28 +57,31 @@
     src_count = lax.axis_size("src")
     me_src = lax.axis_index("src")
     tiles = traces.reshape(comp_count, freq_count, TILE, per_rcv, TILE)
+    assert comp_count == half_count
+    half_tile = TILE // half_count
     arrived = []
     for step in range(per_rcv):
         pick = (me_src % per_rcv + step) % per_rcv
         sent = lax.dynamic_index_in_dim(tiles, pick, 3, keepdims=False)
+        sent = lax.dynamic_slice_in_dim(sent, my_half * half_tile, half_tile, axis=3)
         got = lax.ppermute(sent, ("src", "rcv"), mirror_pairs(src_count, rcv_count, per_rcv, step))
         arrived.append(jnp.swapaxes(got, 2, 3))
     arrived = jnp.stack(arrived, axis=3)
     order = (me_src % per_rcv - jnp.arange(per_rcv)) % per_rcv
-    mirrored = jnp.take(arrived, order, axis=3)
+    rows_mine = jnp.take(arrived, order, axis=3)
     marks = (missing[0] > 0)[None, None, None, :, None]
+    own_rows = lax.dynamic_slice_in_dim(tiles, my_half * half_tile, half_tile, axis=2)
+    right_half = jnp.where(marks, rows_mine, own_rows).reshape(comp_count, freq_count, half_tile, local_cols)
+    rows_other = lax.ppermute(rows_mine, "int", [(0, 1), (1, 0)])
+    mirrored = jnp.stack([rows_mine, rows_other])
+    mirrored = jnp.take(mirrored, (jnp.arange(half_count) + my_half) % half_count, axis=0)
+    mirrored = jnp.moveaxis(mirrored, 0, 2).reshape(tiles.shape)
     filled = jnp.where(marks, mirrored, tiles).reshape(traces.shape)
     row_tiles = local_rows // TILE
     col_tiles = local_cols // TILE
-    half_tile = TILE // half_count
     left_half = filled.reshape(comp_count, freq_count, local_rows, col_tiles, half_count, half_tile)
     left_half = lax.dynamic_index_in_dim(left_half, my_half, 4, keepdims=False)
     left_half = left_half.reshape(comp_count, freq_count, local_rows, col_tiles * half_tile)
-    right_half = filled.reshape(
-        comp_count, freq_count, row_tiles, half_count, half_tile, local_cols
-    )
-    right_half = lax.dynamic_index_in_dim(right_half, my_half, 3, keepdims=False)
-    right_half = right_half.reshape(comp_count, freq_count, row_tiles * half_tile, local_cols)
     gathered = collect(left_half, "rcv", 3)
     block_count = gathered.shape[3] // half_tile
     chosen = (

time: 172 us -> 154 us (0.90)
  starting transfers between devices: 63.9 us -> 44.9 us
  local copies, waits for them, and re-layouts: 8.47 us -> 17.2 us
  matrix products: 13.8 us -> 9.73 us
  waiting for transfers between devices: 68.3 us -> 64.7 us
    all_to_all x1, starting transfers between devices: 47.5 us -> 27 us  [from_everyone(): return lax.all_to_all(copies, axis, split_axis=0, concat_axis=0, tiled=True)]
    all_gather x1, waiting for transfers between devices: 14.2 us -> 1.24 us  [per_device(): slab_piece = lax.all_gather(right_half, 'src', axis=2, tiled=True)]
    ppermute x0 -> x1, waiting for transfers between devices: none -> 7.51 us  [per_device(): rows_other = lax.ppermute(rows_mine, 'int', [(0, 1), (1, 0)])]
    slice x1 -> x2, local copies, waits for them, and re-layouts: 0.24 us -> 7.64 us  [the longest x1 7.4 us: half_product(): cols[0]]
    dot_general x8, matrix products: 13.8 us -> 9.73 us  [complex_prod(): jnp.einsum('fik,fkj->fij', left_side, right_side, precision=lax.Precision...]
    ppermute x1, waiting for transfers between devices: 1.74 us -> 3.95 us  [per_device(): got = lax.ppermute(sent, 'int', [(0, 1), (1, 0)])]
    ppermute x0 -> x1, starting transfers between devices: none -> 1.92 us  [per_device(): rows_other = lax.ppermute(rows_mine, 'int', [(0, 1), (1, 0)])]
  transfers between devices with their start and end apart: 7 -> 8, of which waited for: 4 -> 5; matrix products, arithmetic and copies ran while one was open for 6% -> 7% of each run, Pallas kernels for 0% -> 0%
where the time goes in v13:
time: 154 us
  waiting for transfers between devices  64.7 us (42%)
  starting transfers between devices  44.9 us (29%)
  local copies, waits for them, and re-layouts  17.2 us (11%)
  between operations  13.8 us (9%)
  matrix products  9.73 us (6%)
  other arithmetic  3.6 us (2%)
    all_to_all x1, waiting for transfers between devices, from_everyone(): return lax.all_to_all(copies, axis, split_axis=0, concat_axis=0, tiled=True)  48.7 us
    all_to_all x1, starting transfers between devices, from_everyone(): return lax.all_to_all(copies, axis, split_axis=0, concat_axis=0, tiled=True)  27 us
    ppermute x4, starting transfers between devices, per_device(): lax.ppermute(sent, ('src', 'rcv'), mirror_pairs(src_count, rcv_count, per...  11.4 us
    dot_general x8, matrix products, complex_prod(): jnp.einsum('fik,fkj->fij', left_side, right_side, precision=lax.Precision...  9.73 us
    ppermute x1, waiting for transfers between devices, per_device(): rows_other = lax.ppermute(rows_mine, 'int', [(0, 1), (1, 0)])  7.51 us
    slice x1, local copies, waits for them, and re-layouts, half_product(): cols[0]  7.4 us
    ppermute x1, starting transfers between devices, per_device(): got = lax.ppermute(sent, 'int', [(0, 1), (1, 0)])  4.64 us
    ppermute x1, waiting for transfers between devices, per_device(): got = lax.ppermute(sent, 'int', [(0, 1), (1, 0)])  3.95 us
  transfers between devices with their start and end apart: 8, of which 5 were waited for; matrix products, arithmetic and copies ran while one was open for 7% of the time, Pallas kernels for 0%

profile of v13, /device:TPU:1, one launch (start us, length us, event | category | flops | bytes accessed | tf_op | source)
XLA Modules:
  0.0 153.9 jit_solution(11746784059281062226)
XLA Ops:
  6.5 0.0 copy-start.2
  6.5 0.0 all-gather.2.cloned.1.call-start
  6.5 1.2 copy.44
  7.8 0.7 collective-permute-start
  8.5 8.8 %collective-permute-start.3 = (f32[2,1,128,64]{2,3,0,1:T(8,128)S(1)}, f32[2,1,128,64]{2,3,0,1:T(8,128)S(1)}, u32[]{:S(2)}, u32[]{:S(2)}) collective-permute-start(f32[2,1,128,64]{2,3,0,1:T(8,128)S(1)} %get-tuple-element.16), channel_id=1, source_target_pairs={{16,0},{32,16},{48,32},{64,50},{80,2},{82,66},{96,18},{98,82},{112... | collective-permute-start | bytes 196616 | tf_op jit(solution)/shard_map/ppermute | solution.py:67
  17.3 1.3 collective-permute-start.2
  18.6 0.7 collective-permute-start.1
  19.3 0.2 constant_dynamic-slice_fusion.6
  19.5 0.0 copy-done.2
  19.5 0.2 copy.64
  19.7 0.0 collective-permute-done
  19.8 0.0 collective-permute-done.3
  19.8 3.2 %collective-permute-done.2 = f32[2,1,128,64]{2,3,0,1:T(8,128)S(1)} collective-permute-done((f32[2,1,128,64]{2,3,0,1:T(8,128)S(1)}, f32[2,1,128,64]{2,3,0,1:T(8,128)S(1)}, u32[]{:S(2)}, u32[]{:S(2)}) %collective-permute-start.2) | collective-permute-done | bytes 65568 | tf_op jit(solution)/shard_map/ppermute | solution.py:67
  23.0 0.0 collective-permute-done.1
  23.0 0.6 gather_fusion
  23.6 0.1 broadcast_select_fusion.1
  23.7 0.9 copy.59
  24.6 0.0 all-gather.2.cloned.1.call-update
  24.7 1.9 %collective-permute-start.4 = (f32[2,1,64,4,128]{4,2,0,3,1:T(8,128)S(1)}, f32[2,1,64,4,128]{4,2,0,3,1:T(8,128)S(1)}, u32[]{:S(2)}, u32[]{:S(2)}) collective-permute-start(f32[2,1,64,4,128]{4,2,0,3,1:T(8,128)S(1)} %get-tuple-element.6), channel_id=1, source_target_pairs={{0,1},{1,0},{2,3},{3,2},{4,5},{5,4},{6,7},{7,6},{8,9},{9,8},{10,11... | collective-permute-start | bytes 786440 | tf_op jit(solution)/shard_map/ppermute | solution.py:75
  26.6 0.3 copy.67
  27.0 0.1 bitcast_select_fusion.2
  27.1 7.5 %collective-permute-done.4 = f32[2,1,64,4,128]{4,2,0,3,1:T(8,128)S(1)} collective-permute-done((f32[2,1,64,4,128]{4,2,0,3,1:T(8,128)S(1)}, f32[2,1,64,4,128]{4,2,0,3,1:T(8,128)S(1)}, u32[]{:S(2)}, u32[]{:S(2)}) %collective-permute-start.4) | collective-permute-done | bytes 262176 | tf_op jit(solution)/shard_map/ppermute | solution.py:75
  34.6 0.6 gather_fusion.1
  35.2 0.1 fusion.48
  35.4 0.6 reshape.376
  36.0 0.7 broadcast_select_fusion
  36.7 0.3 copy.56
  37.0 1.6 %broadcast_in_dim.63 = f32[8,2,1,128,256]{3,4,1,2,0:T(8,128)} broadcast(f32[2,128,256]{1,2,0:T(8,128)S(1)} %bitcast.150), dimensions={1,3,4} | broadcast | bytes 2359296 | tf_op jit(solution)/shard_map/broadcast_in_dim | solution.py:10
  38.6 0.0 copy-start.1
  38.6 0.0 copy-start.3
  38.6 27.0 %all-to-all-start = ((f32[8,2,1,128,256]{3,4,1,2,0:T(8,128)}), f32[8,2,1,128,256]{3,4,1,2,0:T(8,128)S(1)}, u32[]{:S(2)}, u32[]{:S(2)}) async-start(f32[8,2,1,128,256]{3,4,1,2,0:T(8,128)} %broadcast_in_dim.63), calls=%async_computation | async-start | bytes 4194304 | tf_op jit(solution)/shard_map/all_to_all | solution.py:11
  65.6 0.1 gt.15
  65.7 0.1 broadcast_bitcast_fusion
  65.8 0.8 copy.66
  66.6 0.0 copy-start
  66.6 0.0 copy-done.1
  66.6 0.6 fusion.58
  67.3 0.0 copy-done.3
  67.3 0.1 convert_reduce_fusion
  67.4 0.3 copy.49
  67.7 0.5 reshape.374
  68.2 0.3 constant_dynamic-slice_fusion.2
  68.4 0.0 copy-done
  68.5 48.7 %all-to-all-done = f32[8,2,1,128,256]{3,4,1,2,0:T(8,128)S(1)} async-done(((f32[8,2,1,128,256]{3,4,1,2,0:T(8,128)}), f32[8,2,1,128,256]{3,4,1,2,0:T(8,128)S(1)}, u32[]{:S(2)}, u32[]{:S(2)}) %all-to-all-start) | async-done | bytes 2097184 | tf_op jit(solution)/shard_map/all_to_all | solution.py:11
  117.2 0.2 copy.57
  117.4 0.2 broadcast_multiply_fusion
  117.6 0.2 fusion.57
  117.9 1.2 all-gather.2.cloned.1.call-done
  119.1 7.4 %constant_dynamic-slice_fusion.1 = (f32[1,1,2048,256]{3,1,2,0:T(1,128)S(1)}, f32[1,1,2048,256]{3,1,2,0:T(1,128)S(1)}, f32[1,1,2048,256]{3,1,2,0:T(1,128)S(1)}, f32[1,1,2048,256]{3,1,2,0:T(1,128)S(1)}) fusion(f32[2,1,2048,512]{3,1,2,0:T(1,128)} %all-gather.2.cloned.1.call-done, s32[]{:T(128)S(6)} %select_n.228, s32[]{:T(128)S(6)} %select_n.229, s32[]{:T(128)S(6)} %add.215), kind=kLoop, calls=%fused_computation.61 | loop fusion | bytes 16777228 | tf_op jit(solution)/shard_map/slice | solution.py:102
  126.5 1.2 fusion
  127.7 1.2 fusion.2
  128.9 1.2 fusion.8
  130.2 1.2 fusion.10
  131.4 1.2 fusion.39
  132.6 1.2 fusion.45
  133.9 4.6 %collective-permute-start.5 = (f32[2,1,128,256]{3,2,1,0:T(8,128)S(1)}, f32[2,1,128,256]{3,2,1,0:T(8,128)S(1)}, u32[]{:S(2)}, u32[]{:S(2)}) collective-permute-start(f32[2,1,128,256]{3,2,1,0:T(8,128)S(1)} %pad_maximum_fusion), channel_id=1, source_target_pairs={{0,1},{1,0},{2,3},{3,2},{4,5},{5,4},{6,7},{7,6},{8,9},{9,8},{10,11... | collective-permute-start | bytes 786440 | tf_op jit(solution)/shard_map/ppermute | solution.py:107
  138.5 1.2 fusion.33
  139.7 1.2 fusion.27
  141.0 3.9 %collective-permute-done.5 = f32[2,1,128,256]{3,2,1,0:T(8,128)S(1)} collective-permute-done((f32[2,1,128,256]{3,2,1,0:T(8,128)S(1)}, f32[2,1,128,256]{3,2,1,0:T(8,128)S(1)}, u32[]{:S(2)}, u32[]{:S(2)}) %collective-permute-start.5) | collective-permute-done | bytes 262176 | tf_op jit(solution)/shard_map/ppermute | solution.py:107
  145.0 1.3 fusion.50
  146.3 0.7 pad_maximum_fusion.1
  (18 shorter events, 0.4 us)
Async XLA Ops:
  6.5 13.0 %copy-start.2 = (s32[1,4]{1,0:T(1,128)S(1)}, s32[1,4]{1,0:T(1,128)}, u32[]{:S(2)}) copy-start(s32[1,4]{1,0:T(1,128)} %param.5) | copy-start | bytes 52
  6.5 112.6 %all-gather.2.cloned.1.call-start = ((), (), s32[]{:S(2)}) async-start(), calls=%async_computation.1 | async-start | bytes 8650752 | tf_op jit(solution)/shard_map/all_gather | solution.py:96
  7.8 11.9 %collective-permute-start = (f32[2,1,128,64]{2,3,0,1:T(8,128)S(1)}, f32[2,1,128,64]{2,3,0,1:T(8,128)S(1)}, u32[]{:S(2)}, u32[]{:S(2)}) collective-permute-start(f32[2,1,128,64]{2,3,0,1:T(8,128)S(1)} %get-tuple-element.15), channel_id=1, source_target_pairs={{64,2},{80,18},{96,34},{112,50},{128,4},{130,68},{144,20},{146,84}... | collective-permute-start | bytes 196616 | tf_op jit(solution)/shard_map/ppermute | solution.py:67
  8.5 11.2 %collective-permute-start.3 = (f32[2,1,128,64]{2,3,0,1:T(8,128)S(1)}, f32[2,1,128,64]{2,3,0,1:T(8,128)S(1)}, u32[]{:S(2)}, u32[]{:S(2)}) collective-permute-start(f32[2,1,128,64]{2,3,0,1:T(8,128)S(1)} %get-tuple-element.16), channel_id=1, source_target_pairs={{16,0},{32,16},{48,32},{64,50},{80,2},{82,66},{96,18},{98,82},{112... | collective-permute-start | bytes 196616 | tf_op jit(solution)/shard_map/ppermute | solution.py:67
  17.3 5.7 %collective-permute-start.2 = (f32[2,1,128,64]{2,3,0,1:T(8,128)S(1)}, f32[2,1,128,64]{2,3,0,1:T(8,128)S(1)}, u32[]{:S(2)}, u32[]{:S(2)}) collective-permute-start(f32[2,1,128,64]{2,3,0,1:T(8,128)S(1)} %get-tuple-element.17), channel_id=1, source_target_pairs={{32,0},{48,16},{64,34},{80,50},{96,2},{98,66},{112,18},{114,82},{1... | collective-permute-start | bytes 196616 | tf_op jit(solution)/shard_map/ppermute | solution.py:67
  18.6 4.4 %collective-permute-start.1 = (f32[2,1,128,64]{2,3,0,1:T(8,128)S(1)}, f32[2,1,128,64]{2,3,0,1:T(8,128)S(1)}, u32[]{:S(2)}, u32[]{:S(2)}) collective-permute-start(f32[2,1,128,64]{2,3,0,1:T(8,128)S(1)} %get-tuple-element.18), channel_id=1, source_target_pairs={{48,0},{64,18},{80,34},{96,50},{112,2},{114,66},{128,20},{130,84},... | collective-permute-start | bytes 196616 | tf_op jit(solution)/shard_map/ppermute | solution.py:67
  24.7 9.9 %collective-permute-start.4 = (f32[2,1,64,4,128]{4,2,0,3,1:T(8,128)S(1)}, f32[2,1,64,4,128]{4,2,0,3,1:T(8,128)S(1)}, u32[]{:S(2)}, u32[]{:S(2)}) collective-permute-start(f32[2,1,64,4,128]{4,2,0,3,1:T(8,128)S(1)} %get-tuple-element.6), channel_id=1, source_target_pairs={{0,1},{1,0},{2,3},{3,2},{4,5},{5,4},{6,7},{7,6},{8,9},{9,8},{10,11... | collective-permute-start | bytes 786440 | tf_op jit(solution)/shard_map/ppermute | solution.py:75
  38.6 28.0 %copy-start.1 = (f32[2,1]{0,1:T(1,128)S(1)}, f32[2,1]{0,1:T(1,128)}, u32[]{:S(2)}) copy-start(f32[2,1]{0,1:T(1,128)} %param.7) | copy-start | bytes 28
  38.6 28.7 %copy-start.3 = (s32[1,24]{1,0:T(1,128)S(1)}, s32[1,24]{1,0:T(1,128)}, u32[]{:S(2)}) copy-start(s32[1,24]{1,0:T(1,128)} %param.6) | copy-start | bytes 292
  38.6 78.6 %all-to-all-start = ((f32[8,2,1,128,256]{3,4,1,2,0:T(8,128)}), f32[8,2,1,128,256]{3,4,1,2,0:T(8,128)S(1)}, u32[]{:S(2)}, u32[]{:S(2)}) async-start(f32[8,2,1,128,256]{3,4,1,2,0:T(8,128)} %broadcast_in_dim.63), calls=%async_computation | async-start | bytes 4194304 | tf_op jit(solution)/shard_map/all_to_all | solution.py:11
  66.6 1.8 %copy-start = (f32[2,1,128,1,256]{4,2,3,1,0:T(8,128)S(1)}, f32[2,1,128,1,256]{4,2,3,1,0:T(8,128)}, u32[]{:S(2)}) copy-start(f32[2,1,128,1,256]{4,2,3,1,0:T(8,128)} %copy.66) | copy-start | bytes 786436
  133.9 11.0 %collective-permute-start.5 = (f32[2,1,128,256]{3,2,1,0:T(8,128)S(1)}, f32[2,1,128,256]{3,2,1,0:T(8,128)S(1)}, u32[]{:S(2)}, u32[]{:S(2)}) collective-permute-start(f32[2,1,128,256]{3,2,1,0:T(8,128)S(1)} %pad_maximum_fusion), channel_id=1, source_target_pairs={{0,1},{1,0},{2,3},{3,2},{4,5},{5,4},{6,7},{7,6},{8,9},{9,8},{10,11... | collective-permute-start | bytes 786440 | tf_op jit(solution)/shard_map/ppermute | solution.py:107
Sparse Core Ops, SparseCore 0:
  24.8 94.2 all-gather.1

commit v14 on v13

--- a/solution.py
+++ b/solution.py
@@ -104,6 +104,7 @@
         return jnp.stack([real_part, imag_part])
 
     sent = half_product(1 - my_half)
+    sent, slab_piece = lax.optimization_barrier((sent, slab_piece))
     got = lax.ppermute(sent, "int", [(0, 1), (1, 0)])
     my_share = half_product(my_half) + got
     kept_data = filled.reshape(comp_count, freq_count, local_rows, half_count, out_cols)

time: 154 us -> 154 us (level)
    slice x1 -> x2, local copies, waits for them, and re-layouts: 7.4 us -> 7.79 us  [half_product(): cols[0]]
where the time goes in v14:
time: 154 us
  waiting for transfers between devices  64 us (42%)
  starting transfers between devices  45.6 us (30%)
  local copies, waits for them, and re-layouts  17.5 us (11%)
  between operations  13.8 us (9%)
  matrix products  9.12 us (6%)
  other arithmetic  3.5 us (2%)
    all_to_all x1, waiting for transfers between devices, from_everyone(): return lax.all_to_all(copies, axis, split_axis=0, concat_axis=0, tiled=True)  48.8 us
    all_to_all x1, starting transfers between devices, from_everyone(): return lax.all_to_all(copies, axis, split_axis=0, concat_axis=0, tiled=True)  27.3 us
    ppermute x4, starting transfers between devices, per_device(): lax.ppermute(sent, ('src', 'rcv'), mirror_pairs(src_count, rcv_count, per...  11.4 us
    dot_general x8, matrix products, complex_prod(): jnp.einsum('fik,fkj->fij', left_side, right_side, precision=lax.Precision...  9.12 us
    slice x2, local copies, waits for them, and re-layouts, half_product(): cols[0]  7.79 us
    ppermute x1, waiting for transfers between devices, per_device(): rows_other = lax.ppermute(rows_mine, 'int', [(0, 1), (1, 0)])  7.51 us
    ppermute x1, starting transfers between devices, per_device(): got = lax.ppermute(sent, 'int', [(0, 1), (1, 0)])  4.96 us
    ppermute x1, waiting for transfers between devices, per_device(): got = lax.ppermute(sent, 'int', [(0, 1), (1, 0)])  3.98 us
  transfers between devices with their start and end apart: 8, of which 5 were waited for; matrix products, arithmetic and copies ran while one was open for 7% of the time, Pallas kernels for 0%

profile of v14, /device:TPU:1, one launch (start us, length us, event | category | flops | bytes accessed | tf_op | source)
XLA Modules:
  0.0 153.5 jit_solution(415253577292187801)
XLA Ops:
  6.5 0.0 copy-start.2
  6.5 0.0 all-gather.2.cloned.1.call-start
  6.5 1.2 copy.44
  7.9 8.8 %collective-permute-start.3 = (f32[2,1,128,64]{2,3,0,1:T(8,128)S(1)}, f32[2,1,128,64]{2,3,0,1:T(8,128)S(1)}, u32[]{:S(2)}, u32[]{:S(2)}) collective-permute-start(f32[2,1,128,64]{2,3,0,1:T(8,128)S(1)} %get-tuple-element.20), channel_id=1, source_target_pairs={{16,0},{32,16},{48,32},{64,50},{80,2},{82,66},{96,18},{98,82},{112... | collective-permute-start | bytes 196616 | tf_op jit(solution)/shard_map/ppermute | solution.py:67
  16.7 1.3 collective-permute-start.2
  18.0 0.7 collective-permute-start.1
  18.6 0.7 collective-permute-start
  19.3 0.2 constant_dynamic-slice_fusion.6
  19.5 0.2 copy.64
  19.7 0.0 copy-done.2
  19.8 0.0 collective-permute-done.3
  19.8 2.6 %collective-permute-done.2 = f32[2,1,128,64]{2,3,0,1:T(8,128)S(1)} collective-permute-done((f32[2,1,128,64]{2,3,0,1:T(8,128)S(1)}, f32[2,1,128,64]{2,3,0,1:T(8,128)S(1)}, u32[]{:S(2)}, u32[]{:S(2)}) %collective-permute-start.2) | collective-permute-done | bytes 65568 | tf_op jit(solution)/shard_map/ppermute | solution.py:67
  22.4 0.0 collective-permute-done.1
  22.4 0.0 collective-permute-done
  22.4 0.6 gather_fusion
  23.0 0.1 broadcast_select_fusion.1
  23.1 0.9 copy.59
  23.9 0.0 all-gather.2.cloned.1.call-update
  24.0 1.9 %collective-permute-start.4 = (f32[2,1,64,4,128]{4,2,0,3,1:T(8,128)S(1)}, f32[2,1,64,4,128]{4,2,0,3,1:T(8,128)S(1)}, u32[]{:S(2)}, u32[]{:S(2)}) collective-permute-start(f32[2,1,64,4,128]{4,2,0,3,1:T(8,128)S(1)} %get-tuple-element.10), channel_id=1, source_target_pairs={{0,1},{1,0},{2,3},{3,2},{4,5},{5,4},{6,7},{7,6},{8,9},{9,8},{10,11... | collective-permute-start | bytes 786440 | tf_op jit(solution)/shard_map/ppermute | solution.py:75
  26.0 0.3 copy.67
  26.3 0.1 bitcast_select_fusion.2
  26.4 7.5 %collective-permute-done.4 = f32[2,1,64,4,128]{4,2,0,3,1:T(8,128)S(1)} collective-permute-done((f32[2,1,64,4,128]{4,2,0,3,1:T(8,128)S(1)}, f32[2,1,64,4,128]{4,2,0,3,1:T(8,128)S(1)}, u32[]{:S(2)}, u32[]{:S(2)}) %collective-permute-start.4) | collective-permute-done | bytes 262176 | tf_op jit(solution)/shard_map/ppermute | solution.py:75
  34.0 0.6 gather_fusion.1
  34.6 0.1 fusion.48
  34.7 0.6 reshape.376
  35.4 0.7 broadcast_select_fusion
  36.1 0.3 copy.56
  36.4 1.6 %broadcast_in_dim.63 = f32[8,2,1,128,256]{3,4,1,2,0:T(8,128)} broadcast(f32[2,128,256]{1,2,0:T(8,128)S(1)} %bitcast.152), dimensions={1,3,4} | broadcast | bytes 2359296 | tf_op jit(solution)/shard_map/broadcast_in_dim | solution.py:10
  38.0 0.0 copy-start.1
  38.0 0.0 copy-start.3
  38.0 27.3 %all-to-all-start = ((f32[8,2,1,128,256]{3,4,1,2,0:T(8,128)}), f32[8,2,1,128,256]{3,4,1,2,0:T(8,128)S(1)}, u32[]{:S(2)}, u32[]{:S(2)}) async-start(f32[8,2,1,128,256]{3,4,1,2,0:T(8,128)} %broadcast_in_dim.63), calls=%async_computation | async-start | bytes 4194304 | tf_op jit(solution)/shard_map/all_to_all | solution.py:11
  65.3 0.8 copy.66
  66.1 0.1 gt.15
  66.2 0.1 broadcast_bitcast_fusion
  66.3 0.0 copy-done.1
  66.3 0.6 fusion.58
  66.9 0.0 copy-done.3
  66.9 0.1 convert_reduce_fusion
  67.0 0.3 copy.49
  67.4 0.5 reshape.374
  67.8 0.3 constant_dynamic-slice_fusion.2
  68.1 0.0 copy-done
  68.2 48.8 %all-to-all-done = f32[8,2,1,128,256]{3,4,1,2,0:T(8,128)S(1)} async-done(((f32[8,2,1,128,256]{3,4,1,2,0:T(8,128)}), f32[8,2,1,128,256]{3,4,1,2,0:T(8,128)S(1)}, u32[]{:S(2)}, u32[]{:S(2)}) %all-to-all-start) | async-done | bytes 2097184 | tf_op jit(solution)/shard_map/all_to_all | solution.py:11
  116.9 0.2 copy.57
  117.1 0.2 broadcast_multiply_fusion
  117.3 0.2 fusion.57
  117.6 1.1 all-gather.2.cloned.1.call-done
  118.7 4.8 %constant_dynamic-slice_fusion.1 = (f32[1,1,2048,256]{3,1,2,0:T(1,128)S(1)}, f32[1,1,2048,256]{3,1,2,0:T(1,128)S(1)}) fusion(f32[2,1,2048,512]{3,1,2,0:T(1,128)} %all-gather.2.cloned.1.call-done, s32[]{:T(128)S(6)} %select_n.228, s32[]{:T(128)S(6)} %add.215), kind=kLoop, calls=%fused_computation.61 | loop fusion | bytes 8388616 | tf_op jit(solution)/shard_map/slice | solution.py:102
  123.5 0.0 slice-start.1
  123.5 1.1 fusion.8
  124.7 1.1 fusion.10
  125.8 1.1 fusion.33
  127.0 1.1 fusion.27
  128.1 0.0 slice-done
  128.2 0.0 slice-done.1
  128.2 3.0 %constant_dynamic-slice_fusion = (f32[1,1,2048,256]{3,1,2,0:T(1,128)S(1)}, f32[1,1,2048,256]{3,1,2,0:T(1,128)S(1)}) fusion(f32[2,1,2048,512]{3,1,2,0:T(1,128)S(1)} %bitcast.146, s32[]{:T(128)S(6)} %select_n.229, s32[]{:T(128)S(6)} %add.215), kind=kLoop, calls=%fused_computation.60 | loop fusion | bytes 8388616 | tf_op jit(solution)/shard_map/slice | solution.py:102
  131.1 1.1 fusion
  132.3 1.1 fusion.2
  133.4 5.0 %collective-permute-start.5 = (f32[2,1,128,256]{3,2,1,0:T(8,128)S(1)}, f32[2,1,128,256]{3,2,1,0:T(8,128)S(1)}, u32[]{:S(2)}, u32[]{:S(2)}) collective-permute-start(f32[2,1,128,256]{3,2,1,0:T(8,128)S(1)} %pad_maximum_fusion), channel_id=1, source_target_pairs={{0,1},{1,0},{2,3},{3,2},{4,5},{5,4},{6,7},{7,6},{8,9},{9,8},{10,11... | collective-permute-start | bytes 786440 | tf_op jit(solution)/shard_map/ppermute | solution.py:108
  138.4 1.1 fusion.45
  139.6 1.1 fusion.39
  140.7 4.0 %collective-permute-done.5 = f32[2,1,128,256]{3,2,1,0:T(8,128)S(1)} collective-permute-done((f32[2,1,128,256]{3,2,1,0:T(8,128)S(1)}, f32[2,1,128,256]{3,2,1,0:T(8,128)S(1)}, u32[]{:S(2)}, u32[]{:S(2)}) %collective-permute-start.5) | collective-permute-done | bytes 262176 | tf_op jit(solution)/shard_map/ppermute | solution.py:108
  144.7 1.2 fusion.50
  146.0 0.7 pad_maximum_fusion.1
  (21 shorter events, 0.4 us)
Async XLA Ops:
  6.5 13.2 %copy-start.2 = (s32[1,4]{1,0:T(1,128)S(1)}, s32[1,4]{1,0:T(1,128)}, u32[]{:S(2)}) copy-start(s32[1,4]{1,0:T(1,128)} %param.5) | copy-start | bytes 52
  6.5 112.1 %all-gather.2.cloned.1.call-start = ((), (), s32[]{:S(2)}) async-start(), calls=%async_computation.1 | async-start | bytes 8650752 | tf_op jit(solution)/shard_map/all_gather | solution.py:96
  7.9 11.9 %collective-permute-start.3 = (f32[2,1,128,64]{2,3,0,1:T(8,128)S(1)}, f32[2,1,128,64]{2,3,0,1:T(8,128)S(1)}, u32[]{:S(2)}, u32[]{:S(2)}) collective-permute-start(f32[2,1,128,64]{2,3,0,1:T(8,128)S(1)} %get-tuple-element.20), channel_id=1, source_target_pairs={{16,0},{32,16},{48,32},{64,50},{80,2},{82,66},{96,18},{98,82},{112... | collective-permute-start | bytes 196616 | tf_op jit(solution)/shard_map/ppermute | solution.py:67
  16.7 5.7 %collective-permute-start.2 = (f32[2,1,128,64]{2,3,0,1:T(8,128)S(1)}, f32[2,1,128,64]{2,3,0,1:T(8,128)S(1)}, u32[]{:S(2)}, u32[]{:S(2)}) collective-permute-start(f32[2,1,128,64]{2,3,0,1:T(8,128)S(1)} %get-tuple-element.21), channel_id=1, source_target_pairs={{32,0},{48,16},{64,34},{80,50},{96,2},{98,66},{112,18},{114,82},{1... | collective-permute-start | bytes 196616 | tf_op jit(solution)/shard_map/ppermute | solution.py:67
  18.0 4.4 %collective-permute-start.1 = (f32[2,1,128,64]{2,3,0,1:T(8,128)S(1)}, f32[2,1,128,64]{2,3,0,1:T(8,128)S(1)}, u32[]{:S(2)}, u32[]{:S(2)}) collective-permute-start(f32[2,1,128,64]{2,3,0,1:T(8,128)S(1)} %get-tuple-element.22), channel_id=1, source_target_pairs={{48,0},{64,18},{80,34},{96,50},{112,2},{114,66},{128,20},{130,84},... | collective-permute-start | bytes 196616 | tf_op jit(solution)/shard_map/ppermute | solution.py:67
  18.6 3.7 %collective-permute-start = (f32[2,1,128,64]{2,3,0,1:T(8,128)S(1)}, f32[2,1,128,64]{2,3,0,1:T(8,128)S(1)}, u32[]{:S(2)}, u32[]{:S(2)}) collective-permute-start(f32[2,1,128,64]{2,3,0,1:T(8,128)S(1)} %get-tuple-element.19), channel_id=1, source_target_pairs={{64,2},{80,18},{96,34},{112,50},{128,4},{130,68},{144,20},{146,84}... | collective-permute-start | bytes 196616 | tf_op jit(solution)/shard_map/ppermute | solution.py:67
  24.0 9.9 %collective-permute-start.4 = (f32[2,1,64,4,128]{4,2,0,3,1:T(8,128)S(1)}, f32[2,1,64,4,128]{4,2,0,3,1:T(8,128)S(1)}, u32[]{:S(2)}, u32[]{:S(2)}) collective-permute-start(f32[2,1,64,4,128]{4,2,0,3,1:T(8,128)S(1)} %get-tuple-element.10), channel_id=1, source_target_pairs={{0,1},{1,0},{2,3},{3,2},{4,5},{5,4},{6,7},{7,6},{8,9},{9,8},{10,11... | collective-permute-start | bytes 786440 | tf_op jit(solution)/shard_map/ppermute | solution.py:75
  38.0 28.3 %copy-start.1 = (f32[2,1]{0,1:T(1,128)S(1)}, f32[2,1]{0,1:T(1,128)}, u32[]{:S(2)}) copy-start(f32[2,1]{0,1:T(1,128)} %param.7) | copy-start | bytes 28
  38.0 29.0 %copy-start.3 = (s32[1,24]{1,0:T(1,128)S(1)}, s32[1,24]{1,0:T(1,128)}, u32[]{:S(2)}) copy-start(s32[1,24]{1,0:T(1,128)} %param.6) | copy-start | bytes 292
  38.0 79.0 %all-to-all-start = ((f32[8,2,1,128,256]{3,4,1,2,0:T(8,128)}), f32[8,2,1,128,256]{3,4,1,2,0:T(8,128)S(1)}, u32[]{:S(2)}, u32[]{:S(2)}) async-start(f32[8,2,1,128,256]{3,4,1,2,0:T(8,128)} %broadcast_in_dim.63), calls=%async_computation | async-start | bytes 4194304 | tf_op jit(solution)/shard_map/all_to_all | solution.py:11
  66.1 2.0 %copy-start = (f32[2,1,128,1,256]{4,2,3,1,0:T(8,128)S(1)}, f32[2,1,128,1,256]{4,2,3,1,0:T(8,128)}, u32[]{:S(2)}) copy-start(f32[2,1,128,1,256]{4,2,3,1,0:T(8,128)} %copy.66) | copy-start | bytes 786436
  118.7 9.5 %slice-start = ((s8[8388608]{0:T(1024)(128)(4,1)}), s8[4194304]{0:T(1024)(128)(4,1)S(1)}, s32[]{:S(2)}) async-start(s8[8388608]{0:T(1024)(128)(4,1)} %bitcast.145), calls=%async_computation.2 | async-start | bytes 8388608
  123.5 4.6 %slice-start.1 = ((s8[8388608]{0:T(1024)(128)(4,1)}), s8[4194304]{0:T(1024)(128)(4,1)S(1)}, s32[]{:S(2)}) async-start(s8[8388608]{0:T(1024)(128)(4,1)} %bitcast.145), calls=%async_computation.3 | async-start | bytes 8388608
  133.4 11.2 %collective-permute-start.5 = (f32[2,1,128,256]{3,2,1,0:T(8,128)S(1)}, f32[2,1,128,256]{3,2,1,0:T(8,128)S(1)}, u32[]{:S(2)}, u32[]{:S(2)}) collective-permute-start(f32[2,1,128,256]{3,2,1,0:T(8,128)S(1)} %pad_maximum_fusion), channel_id=1, source_target_pairs={{0,1},{1,0},{2,3},{3,2},{4,5},{5,4},{6,7},{7,6},{8,9},{9,8},{10,11... | collective-permute-start | bytes 786440 | tf_op jit(solution)/shard_map/ppermute | solution.py:108
Sparse Core Ops, SparseCore 0:
  24.1 94.5 all-gather.1

commit v15 on v13

--- a/solution.py
+++ b/solution.py
@@ -98,14 +98,19 @@
     assert half_count == 2
 
     def half_product(which):
-        cols = lax.dynamic_slice_in_dim(slab_piece, which * out_cols, out_cols, axis=3)
+        cols = slab_piece[..., which * out_cols : (which + 1) * out_cols]
         real_part = complex_prod(weighted[0], cols[0]) - complex_prod(weighted[1], cols[1])
         imag_part = complex_prod(weighted[0], cols[1]) + complex_prod(weighted[1], cols[0])
         return jnp.stack([real_part, imag_part])
 
-    sent = half_product(1 - my_half)
+    def chosen_half(first):
+        return lax.cond(
+            (my_half == 0) == first, lambda: half_product(1), lambda: half_product(0)
+        )
+
+    sent = chosen_half(True)
     got = lax.ppermute(sent, "int", [(0, 1), (1, 0)])
-    my_share = half_product(my_half) + got
+    my_share = chosen_half(False) + got
     kept_data = filled.reshape(comp_count, freq_count, local_rows, half_count, out_cols)
     kept_data = lax.dynamic_index_in_dim(kept_data, my_half, 3, keepdims=False)
     w_real = wavelet[0][:, None, None]

time: 154 us -> 179 us (1.16)
  local copies, waits for them, and re-layouts: 17.2 us -> 32.1 us
  matrix products: 9.73 us -> 19.2 us
  waiting for transfers between devices: 64.7 us -> 60.7 us
  other arithmetic: 3.6 us -> 6.53 us
    another operation x0 -> x5, local copies, waits for them, and re-layouts: none -> 19.5 us
    dot_general x8, matrix products: 9.73 us -> 19.2 us  [complex_prod(): jnp.einsum('fik,fkj->fij', left_side, right_side, precision=lax.Precision...]
    slice x2 -> x0, local copies, waits for them, and re-layouts: 7.64 us -> none  [the longest x1 7.4 us: half_product(): cols[0]]
    ppermute x1, waiting for transfers between devices: 3.95 us -> 0.01 us  [per_device(): got = lax.ppermute(sent, 'int', [(0, 1), (1, 0)])]
    all_to_all x1, waiting for transfers between devices: 48.7 us -> 50.6 us  [from_everyone(): return lax.all_to_all(copies, axis, split_axis=0, concat_axis=0, tiled=True)]
  transfers between devices with their start and end apart: 8 -> 8, of which waited for: 5 -> 3; matrix products, arithmetic and copies ran while one was open for 7% -> 17% of each run, Pallas kernels for 0% -> 0%
where the time goes in v15:
time: 179 us; the launch traced here: 178 us
  waiting for transfers between devices  60.7 us (34%)
  starting transfers between devices  45.5 us (25%)
  local copies, waits for them, and re-layouts  32.1 us (18%)
  matrix products  19.2 us (11%)
  between operations  13.7 us (8%)
  other arithmetic  6.53 us (4%)
    all_to_all x1, waiting for transfers between devices, from_everyone(): return lax.all_to_all(copies, axis, split_axis=0, concat_axis=0, tiled=True)  50.6 us
    all_to_all x1, starting transfers between devices, from_everyone(): return lax.all_to_all(copies, axis, split_axis=0, concat_axis=0, tiled=True)  27.3 us
    dot_general x8, matrix products, complex_prod(): jnp.einsum('fik,fkj->fij', left_side, right_side, precision=lax.Precision...  19.2 us
    another operation x4, local copies, waits for them, and re-layouts  18.8 us
    ppermute x4, starting transfers between devices, per_device(): lax.ppermute(sent, ('src', 'rcv'), mirror_pairs(src_count, rcv_count, per...  11.4 us
    ppermute x1, waiting for transfers between devices, per_device(): rows_other = lax.ppermute(rows_mine, 'int', [(0, 1), (1, 0)])  7.51 us
    ppermute x1, starting transfers between devices, per_device(): got = lax.ppermute(sent, 'int', [(0, 1), (1, 0)])  4.9 us
  transfers between devices with their start and end apart: 8, of which 3 were waited for; matrix products, arithmetic and copies ran while one was open for 17% of the time, Pallas kernels for 0%

profile of v15, /device:TPU:1, one launch (start us, length us, event | category | flops | bytes accessed | tf_op | source)
XLA Modules:
  0.0 178.3 jit_solution(2290513296979514783)
XLA Ops:
  6.5 1.2 copy.91
  7.9 8.8 %collective-permute-start.3 = (f32[2,1,128,64]{2,3,0,1:T(8,128)S(1)}, f32[2,1,128,64]{2,3,0,1:T(8,128)S(1)}, u32[]{:S(2)}, u32[]{:S(2)}) collective-permute-start(f32[2,1,128,64]{2,3,0,1:T(8,128)S(1)} %get-tuple-element.73), channel_id=1, source_target_pairs={{16,0},{32,16},{48,32},{64,50},{80,2},{82,66},{96,18},{98,82},{112... | collective-permute-start | bytes 196616 | tf_op jit(solution)/shard_map/ppermute | solution.py:67
  16.7 1.3 collective-permute-start.2
  18.0 0.7 collective-permute-start.1
  18.6 0.7 collective-permute-start
  19.3 0.2 constant_dynamic-slice_fusion.1
  19.6 0.2 copy.122
  19.8 0.0 collective-permute-done.3
  19.8 2.6 %collective-permute-done.2 = f32[2,1,128,64]{2,3,0,1:T(8,128)S(1)} collective-permute-done((f32[2,1,128,64]{2,3,0,1:T(8,128)S(1)}, f32[2,1,128,64]{2,3,0,1:T(8,128)S(1)}, u32[]{:S(2)}, u32[]{:S(2)}) %collective-permute-start.2) | collective-permute-done | bytes 65568 | tf_op jit(solution)/shard_map/ppermute | solution.py:67
  22.4 0.0 collective-permute-done.1
  22.4 0.0 collective-permute-done
  22.4 0.6 gather_fusion
  23.0 0.1 broadcast_select_fusion.2
  23.1 0.9 copy.107
  23.9 0.0 all-gather.2.cloned.1.call-update
  24.0 1.9 %collective-permute-start.4 = (f32[2,1,64,4,128]{4,2,0,3,1:T(8,128)S(1)}, f32[2,1,64,4,128]{4,2,0,3,1:T(8,128)S(1)}, u32[]{:S(2)}, u32[]{:S(2)}) collective-permute-start(f32[2,1,64,4,128]{4,2,0,3,1:T(8,128)S(1)} %get-tuple-element.69), channel_id=1, source_target_pairs={{0,1},{1,0},{2,3},{3,2},{4,5},{5,4},{6,7},{7,6},{8,9},{9,8},{10,11... | collective-permute-start | bytes 786440 | tf_op jit(solution)/shard_map/ppermute | solution.py:75
  26.0 0.3 copy.124
  26.3 0.1 bitcast_select_fusion.2
  26.4 7.5 %collective-permute-done.4 = f32[2,1,64,4,128]{4,2,0,3,1:T(8,128)S(1)} collective-permute-done((f32[2,1,64,4,128]{4,2,0,3,1:T(8,128)S(1)}, f32[2,1,64,4,128]{4,2,0,3,1:T(8,128)S(1)}, u32[]{:S(2)}, u32[]{:S(2)}) %collective-permute-start.4) | collective-permute-done | bytes 262176 | tf_op jit(solution)/shard_map/ppermute | solution.py:75
  34.0 0.6 gather_fusion.1
  34.6 0.1 fusion.32
  34.7 0.6 reshape.442
  35.4 0.7 broadcast_select_fusion
  36.1 0.3 copy.103
  36.4 0.1 copy.104
  36.5 1.6 broadcast_in_dim.63
  38.1 27.3 %all-to-all-start = ((f32[8,2,1,128,256]{4,3,1,2,0:T(8,128)}), f32[8,2,1,128,256]{4,3,1,2,0:T(8,128)S(1)}, u32[]{:S(2)}, u32[]{:S(2)}) async-start(f32[8,2,1,128,256]{4,3,1,2,0:T(8,128)} %broadcast_in_dim.63), calls=%async_computation | async-start | bytes 4194304 | tf_op jit(solution)/shard_map/all_to_all | solution.py:11
  65.4 0.1 gt.15
  65.5 0.1 broadcast_bitcast_fusion
  65.6 0.1 convert_reduce_fusion
  65.7 0.1 mul.75
  65.7 0.1 mul.76
  65.8 0.7 fusion.41
  66.5 50.6 %all-to-all-done = f32[8,2,1,128,256]{4,3,1,2,0:T(8,128)S(1)} async-done(((f32[8,2,1,128,256]{4,3,1,2,0:T(8,128)}), f32[8,2,1,128,256]{4,3,1,2,0:T(8,128)S(1)}, u32[]{:S(2)}, u32[]{:S(2)}) %all-to-all-start) | async-done | bytes 2097184 | tf_op jit(solution)/shard_map/all_to_all | solution.py:11
  117.1 1.9 %copy.105 = f32[8,2,1,128,256]{3,4,0,1,2:T(8,128)} copy(f32[8,2,1,128,256]{4,3,1,2,0:T(8,128)S(1)} %all-to-all-done) | data formatting | bytes 4194304 | tf_op jit(solution)/shard_map/all_to_all | solution.py:11
  119.0 1.9 %bitcast_multiply_fusion = f32[2,1,128,2048]{2,3,0,1:T(8,128)S(1)} fusion(f32[8,2,1,128,256]{3,4,0,1,2:T(8,128)} %copy.105, f32[2048]{0:T(1024)S(1)} %mul.76), kind=kLoop, calls=%fused_computation.54 | loop fusion | flops 524288 | bytes 4202496 | tf_op jit(solution)/shard_map/mul | solution.py:93
  120.9 0.0 all-gather.2.cloned.1.call-done
  120.9 19.3 %conditional.3 = (f32[2,1,128,256]{3,2,1,0:T(8,128)S(1)}) conditional(s32[]{:T(128)} %convert_element_type.19, (f32[2,1,128,2048]{2,3,0,1:T(8,128)S(1)}, f32[2,1,2048,512]{3,1,2,0:T(1,128)}) %tuple.18, (f32[2,1,128,2048]{2,3,0,1:T(8,128)S(1)}, f32[2,1,2048,512]{3,1,2,0:T(1,128)}) %tuple.18), branch_computations={%region_3.4_spmd, %region_4.5_spmd} | conditional | flops 1610743808 | bytes 43253796 | solution.py:107
  121.1 7.6 %copy.115 = f32[2,1,2048,512]{3,2,1,0:T(8,128)} copy(f32[2,1,2048,512]{3,1,2,0:T(1,128)} %get-tuple-element.66) | data formatting | bytes 16777216 | tf_op jit(solution)/shard_map
  128.7 1.8 %copy.114 = f32[2,1,128,2048]{3,2,1,0:T(8,128)} copy(f32[2,1,128,2048]{2,3,0,1:T(8,128)S(1)} %get-tuple-element.65) | data formatting | bytes 4194304 | tf_op jit(solution)/shard_map
  130.5 2.7 %fusion.24 = f32[128,256]{1,0:T(8,128)S(1)} fusion(f32[2,1,2048,512]{3,2,1,0:T(8,128)} %copy.115, f32[2,1,128,2048]{3,2,1,0:T(8,128)} %copy.114), kind=kOutput, calls=%fused_computation.43 | convolution fusion | flops 402653184 | bytes 3276800 | tf_op jit(solution)/shard_map/cond/branch_1_fun/fik,fkj->fij/dot_general | solution.py:48
  133.3 2.3 %fusion.31 = f32[1,1,128,256]{3,2,1,0:T(8,128)S(1)} fusion(f32[128,256]{1,0:T(8,128)S(1)} %fusion.24, f32[2,1,2048,512]{3,2,1,0:T(8,128)} %copy.115, f32[2,1,128,2048]{3,2,1,0:T(8,128)S(1)} %copy-done.1), kind=kOutput, calls=%fused_computation.50 | convolution fusion | flops 402685952 | bytes 3407872 | tf_op jit(solution)/shard_map/cond/branch_1_fun/fik,fkj->fij/dot_general | solution.py:48
  135.6 2.3 %fusion.25 = f32[128,256]{1,0:T(8,128)S(1)} fusion(f32[2,1,2048,512]{3,2,1,0:T(8,128)} %copy.115, f32[2,1,128,2048]{3,2,1,0:T(8,128)S(1)} %copy-done.1), kind=kOutput, calls=%fused_computation.44 | convolution fusion | flops 402653184 | bytes 3276800 | tf_op jit(solution)/shard_map/cond/branch_1_fun/fik,fkj->fij/dot_general | solution.py:48
  137.9 2.3 %fusion.29 = f32[1,1,128,256]{3,2,1,0:T(8,128)S(1)} fusion(f32[128,256]{1,0:T(8,128)S(1)} %fusion.25, f32[2,1,2048,512]{3,2,1,0:T(8,128)} %copy.115, f32[2,1,128,2048]{3,2,1,0:T(8,128)S(1)} %copy-done.1), kind=kOutput, calls=%fused_computation.48 | convolution fusion | flops 402685952 | bytes 3407872 | tf_op jit(solution)/shard_map/cond/branch_1_fun/fik,fkj->fij/dot_general | solution.py:48
  140.2 0.9 copy.116
  141.1 4.9 %collective-permute-start.5 = (f32[2,1,128,256]{3,0,2,1:T(2,128)}, f32[2,1,128,256]{3,0,2,1:T(2,128)}, u32[]{:S(2)}, u32[]{:S(2)}) collective-permute-start(f32[2,1,128,256]{3,0,2,1:T(2,128)} %copy.116), channel_id=1, source_target_pairs={{0,1},{1,0},{2,3},{3,2},{4,5},{5,4},{6,7},{7,6},{8,9},{9,8},{10,11... | collective-permute-start | bytes 786440 | tf_op jit(solution)/shard_map/ppermute | solution.py:112
  146.0 0.8 copy.123
  146.9 0.3 copy.96
  147.2 0.5 reshape.440
  147.7 0.1 copy-done.4
  147.8 0.3 broadcast_select_fusion.1
  148.2 19.5 %conditional.2 = (f32[2,1,128,256]{3,0,2,1:T(2,128)S(1)}) conditional(s32[]{:T(128)} %convert_element_type.17, (f32[2,1,128,2048]{2,3,0,1:T(8,128)S(1)}, f32[2,1,2048,512]{3,1,2,0:T(1,128)}) %tuple.18, (f32[2,1,128,2048]{2,3,0,1:T(8,128)S(1)}, f32[2,1,2048,512]{3,1,2,0:T(1,128)}) %tuple.18), branch_computations={%region_1.2_spmd, %region_2.3_spmd} | conditional | flops 1610743808 | bytes 43778084 | solution.py:107
  148.2 7.6 %copy.109 = f32[2,1,2048,512]{3,2,1,0:T(8,128)} copy(f32[2,1,2048,512]{3,1,2,0:T(1,128)} %get-tuple-element.60) | data formatting | bytes 16777216 | tf_op jit(solution)/shard_map
  155.8 1.8 %copy.108 = f32[2,1,128,2048]{3,2,1,0:T(8,128)} copy(f32[2,1,128,2048]{2,3,0,1:T(8,128)S(1)} %get-tuple-element.59) | data formatting | bytes 4194304 | tf_op jit(solution)/shard_map
  157.6 2.7 %fusion = f32[128,256]{1,0:T(8,128)S(1)} fusion(f32[2,1,2048,512]{3,2,1,0:T(8,128)} %copy.109, f32[2,1,128,2048]{3,2,1,0:T(8,128)} %copy.108), kind=kOutput, calls=%fused_computation.4 | convolution fusion | flops 402653184 | bytes 3276800 | tf_op jit(solution)/shard_map/cond/branch_0_fun/fik,fkj->fij/dot_general | solution.py:48
  160.3 2.3 %fusion.7 = f32[1,1,128,256]{3,2,1,0:T(8,128)S(1)} fusion(f32[128,256]{1,0:T(8,128)S(1)} %fusion, f32[2,1,2048,512]{3,2,1,0:T(8,128)} %copy.109, f32[2,1,128,2048]{3,2,1,0:T(8,128)S(1)} %copy-done.2), kind=kOutput, calls=%fused_computation.11 | convolution fusion | flops 402685952 | bytes 3407872 | tf_op jit(solution)/shard_map/cond/branch_0_fun/fik,fkj->fij/dot_general | solution.py:48
  162.6 2.3 %fusion.1 = f32[128,256]{1,0:T(8,128)S(1)} fusion(f32[2,1,2048,512]{3,2,1,0:T(8,128)} %copy.109, f32[2,1,128,2048]{3,2,1,0:T(8,128)S(1)} %copy-done.2), kind=kOutput, calls=%fused_computation.5 | convolution fusion | flops 402653184 | bytes 3276800 | tf_op jit(solution)/shard_map/cond/branch_0_fun/fik,fkj->fij/dot_general | solution.py:48
  164.9 2.3 %fusion.5 = f32[1,1,128,256]{3,2,1,0:T(8,128)S(1)} fusion(f32[128,256]{1,0:T(8,128)S(1)} %fusion.1, f32[2,1,2048,512]{3,2,1,0:T(8,128)} %copy.109, f32[2,1,128,2048]{3,2,1,0:T(8,128)S(1)} %copy-done.2), kind=kOutput, calls=%fused_computation.9 | convolution fusion | flops 402685952 | bytes 3407872 | tf_op jit(solution)/shard_map/cond/branch_0_fun/fik,fkj->fij/dot_general | solution.py:48
  167.2 0.2 copy.119
  167.7 0.0 collective-permute-done.5
  167.7 1.1 add.209
  168.8 1.6 fusion.34
  170.4 0.2 pad_maximum_fusion.4
  170.7 0.7 copy.118
  (29 shorter events, 0.4 us)
Async XLA Ops:
  6.5 13.0 %copy-start.6 = (s32[1,4]{1,0:T(1,128)S(1)}, s32[1,4]{1,0:T(1,128)}, u32[]{:S(2)}) copy-start(s32[1,4]{1,0:T(1,128)} %param.9) | copy-start | bytes 52
  6.5 114.4 %all-gather.2.cloned.1.call-start = ((), (), s32[]{:S(2)}) async-start(), calls=%async_computation.1 | async-start | bytes 8650752 | tf_op jit(solution)/shard_map/all_gather | solution.py:96
  7.9 11.9 %collective-permute-start.3 = (f32[2,1,128,64]{2,3,0,1:T(8,128)S(1)}, f32[2,1,128,64]{2,3,0,1:T(8,128)S(1)}, u32[]{:S(2)}, u32[]{:S(2)}) collective-permute-start(f32[2,1,128,64]{2,3,0,1:T(8,128)S(1)} %get-tuple-element.73), channel_id=1, source_target_pairs={{16,0},{32,16},{48,32},{64,50},{80,2},{82,66},{96,18},{98,82},{112... | collective-permute-start | bytes 196616 | tf_op jit(solution)/shard_map/ppermute | solution.py:67
  16.7 5.7 %collective-permute-start.2 = (f32[2,1,128,64]{2,3,0,1:T(8,128)S(1)}, f32[2,1,128,64]{2,3,0,1:T(8,128)S(1)}, u32[]{:S(2)}, u32[]{:S(2)}) collective-permute-start(f32[2,1,128,64]{2,3,0,1:T(8,128)S(1)} %get-tuple-element.74), channel_id=1, source_target_pairs={{32,0},{48,16},{64,34},{80,50},{96,2},{98,66},{112,18},{114,82},{1... | collective-permute-start | bytes 196616 | tf_op jit(solution)/shard_map/ppermute | solution.py:67
  18.0 4.4 %collective-permute-start.1 = (f32[2,1,128,64]{2,3,0,1:T(8,128)S(1)}, f32[2,1,128,64]{2,3,0,1:T(8,128)S(1)}, u32[]{:S(2)}, u32[]{:S(2)}) collective-permute-start(f32[2,1,128,64]{2,3,0,1:T(8,128)S(1)} %get-tuple-element.75), channel_id=1, source_target_pairs={{48,0},{64,18},{80,34},{96,50},{112,2},{114,66},{128,20},{130,84},... | collective-permute-start | bytes 196616 | tf_op jit(solution)/shard_map/ppermute | solution.py:67
  18.6 3.7 %collective-permute-start = (f32[2,1,128,64]{2,3,0,1:T(8,128)S(1)}, f32[2,1,128,64]{2,3,0,1:T(8,128)S(1)}, u32[]{:S(2)}, u32[]{:S(2)}) collective-permute-start(f32[2,1,128,64]{2,3,0,1:T(8,128)S(1)} %get-tuple-element.72), channel_id=1, source_target_pairs={{64,2},{80,18},{96,34},{112,50},{128,4},{130,68},{144,20},{146,84}... | collective-permute-start | bytes 196616 | tf_op jit(solution)/shard_map/ppermute | solution.py:67
  24.0 9.9 %collective-permute-start.4 = (f32[2,1,64,4,128]{4,2,0,3,1:T(8,128)S(1)}, f32[2,1,64,4,128]{4,2,0,3,1:T(8,128)S(1)}, u32[]{:S(2)}, u32[]{:S(2)}) collective-permute-start(f32[2,1,64,4,128]{4,2,0,3,1:T(8,128)S(1)} %get-tuple-element.69), channel_id=1, source_target_pairs={{0,1},{1,0},{2,3},{3,2},{4,5},{5,4},{6,7},{7,6},{8,9},{9,8},{10,11... | collective-permute-start | bytes 786440 | tf_op jit(solution)/shard_map/ppermute | solution.py:75
  38.1 27.5 %copy-start.7 = (s32[1,24]{1,0:T(1,128)S(1)}, s32[1,24]{1,0:T(1,128)}, u32[]{:S(2)}) copy-start(s32[1,24]{1,0:T(1,128)} %param.10) | copy-start | bytes 292
  38.1 27.7 %copy-start.5 = (f32[2,1]{0,1:T(1,128)S(1)}, f32[2,1]{0,1:T(1,128)}, u32[]{:S(2)}) copy-start(f32[2,1]{0,1:T(1,128)} %param.11) | copy-start | bytes 28
  38.1 79.0 %all-to-all-start = ((f32[8,2,1,128,256]{4,3,1,2,0:T(8,128)}), f32[8,2,1,128,256]{4,3,1,2,0:T(8,128)S(1)}, u32[]{:S(2)}, u32[]{:S(2)}) async-start(f32[8,2,1,128,256]{4,3,1,2,0:T(8,128)} %broadcast_in_dim.63), calls=%async_computation | async-start | bytes 4194304 | tf_op jit(solution)/shard_map/all_to_all | solution.py:11
  130.5 2.7 %copy-start.1 = (f32[2,1,128,2048]{3,2,1,0:T(8,128)S(1)}, f32[2,1,128,2048]{3,2,1,0:T(8,128)}, u32[]{:S(2)}) copy-start(f32[2,1,128,2048]{3,2,1,0:T(8,128)} %copy.114) | copy-start | bytes 6291460 | tf_op jit(solution)/shard_map/cond
  141.1 26.6 %collective-permute-start.5 = (f32[2,1,128,256]{3,0,2,1:T(2,128)}, f32[2,1,128,256]{3,0,2,1:T(2,128)}, u32[]{:S(2)}, u32[]{:S(2)}) collective-permute-start(f32[2,1,128,256]{3,0,2,1:T(2,128)} %copy.116), channel_id=1, source_target_pairs={{0,1},{1,0},{2,3},{3,2},{4,5},{5,4},{6,7},{7,6},{8,9},{9,8},{10,11... | collective-permute-start | bytes 786440 | tf_op jit(solution)/shard_map/ppermute | solution.py:112
  146.9 0.9 copy-start.4
  157.6 2.7 %copy-start.2 = (f32[2,1,128,2048]{3,2,1,0:T(8,128)S(1)}, f32[2,1,128,2048]{3,2,1,0:T(8,128)}, u32[]{:S(2)}) copy-start(f32[2,1,128,2048]{3,2,1,0:T(8,128)} %copy.108) | copy-start | bytes 6291460 | tf_op jit(solution)/shard_map/cond
Sparse Core Ops, SparseCore 0:
  24.1 94.9 all-gather.1

commit v16 on v13

--- a/solution.py
+++ b/solution.py
@@ -97,15 +97,12 @@
     out_cols = local_cols // half_count
     assert half_count == 2
 
-    def half_product(which):
-        cols = lax.dynamic_slice_in_dim(slab_piece, which * out_cols, out_cols, axis=3)
-        real_part = complex_prod(weighted[0], cols[0]) - complex_prod(weighted[1], cols[1])
-        imag_part = complex_prod(weighted[0], cols[1]) + complex_prod(weighted[1], cols[0])
-        return jnp.stack([real_part, imag_part])
-
-    sent = half_product(1 - my_half)
+    real_part = complex_prod(weighted[0], slab_piece[0]) - complex_prod(weighted[1], slab_piece[1])
+    imag_part = complex_prod(weighted[0], slab_piece[1]) + complex_prod(weighted[1], slab_piece[0])
+    partial_sum = jnp.stack([real_part, imag_part])
+    sent = lax.dynamic_slice_in_dim(partial_sum, (1 - my_half) * out_cols, out_cols, axis=3)
     got = lax.ppermute(sent, "int", [(0, 1), (1, 0)])
-    my_share = half_product(my_half) + got
+    my_share = lax.dynamic_slice_in_dim(partial_sum, my_half * out_cols, out_cols, axis=3) + got
     kept_data = filled.reshape(comp_count, freq_count, local_rows, half_count, out_cols)
     kept_data = lax.dynamic_index_in_dim(kept_data, my_half, 3, keepdims=False)
     w_real = wavelet[0][:, None, None]

time: 154 us -> 152 us (0.987)
  matrix products: 9.73 us -> 5.67 us
  waiting for transfers between devices: 64.7 us -> 66.6 us
    dot_general x8 -> x4, matrix products: 9.73 us -> 5.67 us  [complex_prod(): jnp.einsum('fik,fkj->fij', left_side, right_side, precision=lax.Precision...]
    ppermute x1, waiting for transfers between devices: 3.95 us -> 5.93 us  [per_device(): got = lax.ppermute(sent, 'int', [(0, 1), (1, 0)])]
  transfers between devices with their start and end apart: 8 -> 8, of which waited for: 5 -> 5; matrix products, arithmetic and copies ran while one was open for 7% -> 6% of each run, Pallas kernels for 0% -> 0%
where the time goes in v16:
time: 152 us
  waiting for transfers between devices  66.6 us (44%)
  starting transfers between devices  45.1 us (30%)
  local copies, waits for them, and re-layouts  16.8 us (11%)
  between operations  13.7 us (9%)
  matrix products  5.67 us (4%)
  other arithmetic  4.14 us (3%)
    all_to_all x1, waiting for transfers between devices, from_everyone(): return lax.all_to_all(copies, axis, split_axis=0, concat_axis=0, tiled=True)  49.1 us
    all_to_all x1, starting transfers between devices, from_everyone(): return lax.all_to_all(copies, axis, split_axis=0, concat_axis=0, tiled=True)  26.8 us
    ppermute x4, starting transfers between devices, per_device(): lax.ppermute(sent, ('src', 'rcv'), mirror_pairs(src_count, rcv_count, per...  11.4 us
    ppermute x1, waiting for transfers between devices, per_device(): rows_other = lax.ppermute(rows_mine, 'int', [(0, 1), (1, 0)])  7.51 us
    slice x1, local copies, waits for them, and re-layouts, per_device(): slab_piece[0]  7.1 us
    ppermute x1, waiting for transfers between devices, per_device(): got = lax.ppermute(sent, 'int', [(0, 1), (1, 0)])  5.93 us
    dot_general x4, matrix products, complex_prod(): jnp.einsum('fik,fkj->fij', left_side, right_side, precision=lax.Precision...  5.67 us
    ppermute x1, starting transfers between devices, per_device(): got = lax.ppermute(sent, 'int', [(0, 1), (1, 0)])  4.95 us
  transfers between devices with their start and end apart: 8, of which 5 were waited for; matrix products, arithmetic and copies ran while one was open for 6% of the time, Pallas kernels for 0%

profile of v16, /device:TPU:1, one launch (start us, length us, event | category | flops | bytes accessed | tf_op | source)
XLA Modules:
  0.0 152.0 jit_solution(879086896378312124)
XLA Ops:
  6.5 0.0 all-gather.2.cloned.1.call-start
  6.5 1.2 copy.44
  7.8 0.7 collective-permute-start
  8.5 8.8 %collective-permute-start.3 = (f32[2,1,128,64]{2,3,0,1:T(8,128)S(1)}, f32[2,1,128,64]{2,3,0,1:T(8,128)S(1)}, u32[]{:S(2)}, u32[]{:S(2)}) collective-permute-start(f32[2,1,128,64]{2,3,0,1:T(8,128)S(1)} %get-tuple-element.14), channel_id=1, source_target_pairs={{16,0},{32,16},{48,32},{64,50},{80,2},{82,66},{96,18},{98,82},{112... | collective-permute-start | bytes 196616 | tf_op jit(solution)/shard_map/ppermute | solution.py:67
  17.3 1.3 collective-permute-start.2
  18.6 0.7 collective-permute-start.1
  19.3 0.2 constant_dynamic-slice_fusion.2
  19.5 0.7 compare_reduce_fusion
  20.2 0.2 copy.62
  20.4 0.0 collective-permute-done
  20.4 0.0 collective-permute-done.3
  20.4 2.6 %collective-permute-done.2 = f32[2,1,128,64]{2,3,0,1:T(8,128)S(1)} collective-permute-done((f32[2,1,128,64]{2,3,0,1:T(8,128)S(1)}, f32[2,1,128,64]{2,3,0,1:T(8,128)S(1)}, u32[]{:S(2)}, u32[]{:S(2)}) %collective-permute-start.2) | collective-permute-done | bytes 65568 | tf_op jit(solution)/shard_map/ppermute | solution.py:67
  23.0 0.0 collective-permute-done.1
  23.0 0.6 gather_fusion
  23.6 0.1 broadcast_select_fusion.1
  23.7 0.9 copy.59
  24.6 0.0 all-gather.2.cloned.1.call-update
  24.7 1.9 %collective-permute-start.4 = (f32[2,1,64,4,128]{4,2,0,3,1:T(8,128)S(1)}, f32[2,1,64,4,128]{4,2,0,3,1:T(8,128)S(1)}, u32[]{:S(2)}, u32[]{:S(2)}) collective-permute-start(f32[2,1,64,4,128]{4,2,0,3,1:T(8,128)S(1)} %get-tuple-element.6), channel_id=1, source_target_pairs={{0,1},{1,0},{2,3},{3,2},{4,5},{5,4},{6,7},{7,6},{8,9},{9,8},{10,11... | collective-permute-start | bytes 786440 | tf_op jit(solution)/shard_map/ppermute | solution.py:75
  26.6 0.3 copy.65
  27.0 0.1 bitcast_select_fusion.2
  27.1 7.5 %collective-permute-done.4 = f32[2,1,64,4,128]{4,2,0,3,1:T(8,128)S(1)} collective-permute-done((f32[2,1,64,4,128]{4,2,0,3,1:T(8,128)S(1)}, f32[2,1,64,4,128]{4,2,0,3,1:T(8,128)S(1)}, u32[]{:S(2)}, u32[]{:S(2)}) %collective-permute-start.4) | collective-permute-done | bytes 262176 | tf_op jit(solution)/shard_map/ppermute | solution.py:75
  34.6 0.6 gather_fusion.1
  35.2 0.1 fusion.24
  35.4 0.6 reshape.348
  36.0 0.7 broadcast_select_fusion
  36.7 0.0 copy-start.1
  36.7 0.0 copy-start.2
  36.7 0.3 copy.56
  37.0 1.6 %broadcast_in_dim.63 = f32[8,2,1,128,256]{3,4,1,2,0:T(8,128)} broadcast(f32[2,128,256]{1,2,0:T(8,128)S(1)} %bitcast.120), dimensions={1,3,4} | broadcast | bytes 2359296 | tf_op jit(solution)/shard_map/broadcast_in_dim | solution.py:10
  38.6 26.8 %all-to-all-start = ((f32[8,2,1,128,256]{3,4,1,2,0:T(8,128)}), f32[8,2,1,128,256]{3,4,1,2,0:T(8,128)S(1)}, u32[]{:S(2)}, u32[]{:S(2)}) async-start(f32[8,2,1,128,256]{3,4,1,2,0:T(8,128)} %broadcast_in_dim.63), calls=%async_computation | async-start | bytes 4194304 | tf_op jit(solution)/shard_map/all_to_all | solution.py:11
  65.4 0.1 gt.15
  65.5 0.1 broadcast_bitcast_fusion
  65.6 0.8 copy.64
  66.5 0.0 copy-done.1
  66.5 0.6 fusion.38
  67.1 0.0 copy-done.2
  67.1 0.1 convert_reduce_fusion
  67.2 0.3 copy.49
  67.5 0.5 reshape.346
  68.0 49.1 %all-to-all-done = f32[8,2,1,128,256]{3,4,1,2,0:T(8,128)S(1)} async-done(((f32[8,2,1,128,256]{3,4,1,2,0:T(8,128)}), f32[8,2,1,128,256]{3,4,1,2,0:T(8,128)S(1)}, u32[]{:S(2)}, u32[]{:S(2)}) %all-to-all-start) | async-done | bytes 2097184 | tf_op jit(solution)/shard_map/all_to_all | solution.py:11
  117.1 0.2 copy.57
  117.3 0.2 broadcast_multiply_fusion
  117.5 0.2 fusion.37
  117.7 1.4 all-gather.2.cloned.1.call-done
  119.1 7.1 %fusion.36 = (f32[1,1,2048,512]{3,1,2,0:T(1,128)S(1)}, f32[1,1,2048,512]{3,1,2,0:T(1,128)S(1)}) fusion(f32[2,1,2048,512]{3,1,2,0:T(1,128)} %all-gather.2.cloned.1.call-done), kind=kLoop, calls=%fused_computation.81 | loop fusion | bytes 16777216 | tf_op jit(solution)/shard_map/slice | solution.py:100
  126.2 1.4 fusion.2
  127.6 1.4 fusion
  129.1 1.4 fusion.15
  130.5 0.0 copy-start
  130.5 1.4 fusion.21
  132.0 4.9 %collective-permute-start.5 = (f32[2,1,128,256]{3,2,1,0:T(8,128)S(1)}, f32[2,1,128,256]{3,2,1,0:T(8,128)S(1)}, u32[]{:S(2)}, u32[]{:S(2)}) collective-permute-start(f32[2,1,128,256]{3,2,1,0:T(8,128)S(1)} %fusion.25), channel_id=1, source_target_pairs={{0,1},{1,0},{2,3},{3,2},{4,5},{5,4},{6,7},{7,6},{8,9},{9,8},{10,11... | collective-permute-start | bytes 786440 | tf_op jit(solution)/shard_map/ppermute | solution.py:104
  136.9 0.3 constant_dynamic-slice_fusion
  137.2 0.0 copy-done
  137.2 5.9 %collective-permute-done.5 = f32[2,1,128,256]{3,2,1,0:T(8,128)S(1)} collective-permute-done((f32[2,1,128,256]{3,2,1,0:T(8,128)S(1)}, f32[2,1,128,256]{3,2,1,0:T(8,128)S(1)}, u32[]{:S(2)}, u32[]{:S(2)}) %collective-permute-start.5) | collective-permute-done | bytes 262176 | tf_op jit(solution)/shard_map/ppermute | solution.py:104
  143.2 1.2 fusion.29
  144.4 0.7 pad_maximum_fusion
  (17 shorter events, 0.4 us)
Async XLA Ops:
  6.5 112.6 %all-gather.2.cloned.1.call-start = ((), (), s32[]{:S(2)}) async-start(), calls=%async_computation.1 | async-start | bytes 8650752 | tf_op jit(solution)/shard_map/all_gather | solution.py:96
  7.8 12.6 %collective-permute-start = (f32[2,1,128,64]{2,3,0,1:T(8,128)S(1)}, f32[2,1,128,64]{2,3,0,1:T(8,128)S(1)}, u32[]{:S(2)}, u32[]{:S(2)}) collective-permute-start(f32[2,1,128,64]{2,3,0,1:T(8,128)S(1)} %get-tuple-element.13), channel_id=1, source_target_pairs={{64,2},{80,18},{96,34},{112,50},{128,4},{130,68},{144,20},{146,84}... | collective-permute-start | bytes 196616 | tf_op jit(solution)/shard_map/ppermute | solution.py:67
  8.5 11.9 %collective-permute-start.3 = (f32[2,1,128,64]{2,3,0,1:T(8,128)S(1)}, f32[2,1,128,64]{2,3,0,1:T(8,128)S(1)}, u32[]{:S(2)}, u32[]{:S(2)}) collective-permute-start(f32[2,1,128,64]{2,3,0,1:T(8,128)S(1)} %get-tuple-element.14), channel_id=1, source_target_pairs={{16,0},{32,16},{48,32},{64,50},{80,2},{82,66},{96,18},{98,82},{112... | collective-permute-start | bytes 196616 | tf_op jit(solution)/shard_map/ppermute | solution.py:67
  17.3 5.7 %collective-permute-start.2 = (f32[2,1,128,64]{2,3,0,1:T(8,128)S(1)}, f32[2,1,128,64]{2,3,0,1:T(8,128)S(1)}, u32[]{:S(2)}, u32[]{:S(2)}) collective-permute-start(f32[2,1,128,64]{2,3,0,1:T(8,128)S(1)} %get-tuple-element.15), channel_id=1, source_target_pairs={{32,0},{48,16},{64,34},{80,50},{96,2},{98,66},{112,18},{114,82},{1... | collective-permute-start | bytes 196616 | tf_op jit(solution)/shard_map/ppermute | solution.py:67
  18.6 4.4 %collective-permute-start.1 = (f32[2,1,128,64]{2,3,0,1:T(8,128)S(1)}, f32[2,1,128,64]{2,3,0,1:T(8,128)S(1)}, u32[]{:S(2)}, u32[]{:S(2)}) collective-permute-start(f32[2,1,128,64]{2,3,0,1:T(8,128)S(1)} %get-tuple-element.16), channel_id=1, source_target_pairs={{48,0},{64,18},{80,34},{96,50},{112,2},{114,66},{128,20},{130,84},... | collective-permute-start | bytes 196616 | tf_op jit(solution)/shard_map/ppermute | solution.py:67
  24.7 9.9 %collective-permute-start.4 = (f32[2,1,64,4,128]{4,2,0,3,1:T(8,128)S(1)}, f32[2,1,64,4,128]{4,2,0,3,1:T(8,128)S(1)}, u32[]{:S(2)}, u32[]{:S(2)}) collective-permute-start(f32[2,1,64,4,128]{4,2,0,3,1:T(8,128)S(1)} %get-tuple-element.6), channel_id=1, source_target_pairs={{0,1},{1,0},{2,3},{3,2},{4,5},{5,4},{6,7},{7,6},{8,9},{9,8},{10,11... | collective-permute-start | bytes 786440 | tf_op jit(solution)/shard_map/ppermute | solution.py:75
  36.7 29.8 %copy-start.1 = (f32[2,1]{0,1:T(1,128)S(1)}, f32[2,1]{0,1:T(1,128)}, u32[]{:S(2)}) copy-start(f32[2,1]{0,1:T(1,128)} %param.7) | copy-start | bytes 28
  36.7 30.4 %copy-start.2 = (s32[1,24]{1,0:T(1,128)S(1)}, s32[1,24]{1,0:T(1,128)}, u32[]{:S(2)}) copy-start(s32[1,24]{1,0:T(1,128)} %param.6) | copy-start | bytes 292
  38.6 78.5 %all-to-all-start = ((f32[8,2,1,128,256]{3,4,1,2,0:T(8,128)}), f32[8,2,1,128,256]{3,4,1,2,0:T(8,128)S(1)}, u32[]{:S(2)}, u32[]{:S(2)}) async-start(f32[8,2,1,128,256]{3,4,1,2,0:T(8,128)} %broadcast_in_dim.63), calls=%async_computation | async-start | bytes 4194304 | tf_op jit(solution)/shard_map/all_to_all | solution.py:11
  130.5 6.7 %copy-start = (f32[2,1,128,1,256]{4,2,3,1,0:T(8,128)S(1)}, f32[2,1,128,1,256]{4,2,3,1,0:T(8,128)}, u32[]{:S(2)}) copy-start(f32[2,1,128,1,256]{4,2,3,1,0:T(8,128)} %copy.64) | copy-start | bytes 786436
  132.0 11.2 %collective-permute-start.5 = (f32[2,1,128,256]{3,2,1,0:T(8,128)S(1)}, f32[2,1,128,256]{3,2,1,0:T(8,128)S(1)}, u32[]{:S(2)}, u32[]{:S(2)}) collective-permute-start(f32[2,1,128,256]{3,2,1,0:T(8,128)S(1)} %fusion.25), channel_id=1, source_target_pairs={{0,1},{1,0},{2,3},{3,2},{4,5},{5,4},{6,7},{7,6},{8,9},{9,8},{10,11... | collective-permute-start | bytes 786440 | tf_op jit(solution)/shard_map/ppermute | solution.py:104
Sparse Core Ops, SparseCore 0:
  24.7 94.3 all-gather.1

commit v17 on v16

--- a/solution.py
+++ b/solution.py
@@ -93,7 +93,9 @@
     weighted = (weighted * chosen[None, None, :, None, :, None]).reshape(
         comp_count, freq_count, local_rows, block_count * half_tile
     )
-    slab_piece = lax.all_gather(right_half, "src", axis=2, tiled=True)
+    slab_piece = right_half.reshape(comp_count * freq_count, half_tile, local_cols)
+    slab_piece = lax.all_gather(slab_piece, "src", axis=1, tiled=True)
+    slab_piece = slab_piece.reshape(comp_count, freq_count, -1, local_cols)
     out_cols = local_cols // half_count
     assert half_count == 2
 

time: 152 us -> 150 us (0.987)
  local copies, waits for them, and re-layouts: 16.8 us -> 9.8 us
  matrix products: 5.67 us -> 10.2 us
    slice x2 -> x1, local copies, waits for them, and re-layouts: 7.34 us -> 0.24 us  [per_device(): weighted[1]]
    dot_general x4, matrix products: 5.67 us -> 10.2 us  [complex_prod(): jnp.einsum('fik,fkj->fij', left_side, right_side, precision=lax.Precision...]
where the time goes in v17:
time: 150 us; the launch traced here: 149 us
  waiting for transfers between devices  66.6 us (44%)
  starting transfers between devices  44.8 us (30%)
  between operations  13.8 us (9%)
  matrix products  10.2 us (7%)
  local copies, waits for them, and re-layouts  9.8 us (7%)
  other arithmetic  4.13 us (3%)
    all_to_all x1, waiting for transfers between devices, from_everyone(): return lax.all_to_all(copies, axis, split_axis=0, concat_axis=0, tiled=True)  49.1 us
    all_to_all x1, starting transfers between devices, from_everyone(): return lax.all_to_all(copies, axis, split_axis=0, concat_axis=0, tiled=True)  27.2 us
    ppermute x4, starting transfers between devices, per_device(): lax.ppermute(sent, ('src', 'rcv'), mirror_pairs(src_count, rcv_count, per...  11.4 us
    dot_general x4, matrix products, complex_prod(): jnp.einsum('fik,fkj->fij', left_side, right_side, precision=lax.Precision...  10.2 us
    ppermute x1, waiting for transfers between devices, per_device(): rows_other = lax.ppermute(rows_mine, 'int', [(0, 1), (1, 0)])  7.51 us
    ppermute x1, waiting for transfers between devices, per_device(): got = lax.ppermute(sent, 'int', [(0, 1), (1, 0)])  6.44 us
    ppermute x1, starting transfers between devices, per_device(): got = lax.ppermute(sent, 'int', [(0, 1), (1, 0)])  4.27 us
  transfers between devices with their start and end apart: 8, of which 5 were waited for; matrix products, arithmetic and copies ran while one was open for 6% of the time, Pallas kernels for 0%

profile of v17, /device:TPU:1, one launch (start us, length us, event | category | flops | bytes accessed | tf_op | source)
XLA Modules:
  0.0 149.3 jit_solution(17721223387900036025)
XLA Ops:
  6.5 0.0 all-gather.2.cloned.1.call-start
  6.5 1.2 copy.44
  7.9 8.8 %collective-permute-start.3 = (f32[2,1,128,64]{2,3,0,1:T(8,128)S(1)}, f32[2,1,128,64]{2,3,0,1:T(8,128)S(1)}, u32[]{:S(2)}, u32[]{:S(2)}) collective-permute-start(f32[2,1,128,64]{2,3,0,1:T(8,128)S(1)} %get-tuple-element.12), channel_id=1, source_target_pairs={{16,0},{32,16},{48,32},{64,50},{80,2},{82,66},{96,18},{98,82},{112... | collective-permute-start | bytes 196616 | tf_op jit(solution)/shard_map/ppermute | solution.py:67
  16.7 1.3 collective-permute-start.2
  18.0 0.7 collective-permute-start.1
  18.6 0.7 collective-permute-start
  19.3 0.2 constant_dynamic-slice_fusion.2
  19.5 0.2 copy.60
  19.7 0.7 compare_reduce_fusion
  20.4 0.0 collective-permute-done.3
  20.4 1.9 %collective-permute-done.2 = f32[2,1,128,64]{2,3,0,1:T(8,128)S(1)} collective-permute-done((f32[2,1,128,64]{2,3,0,1:T(8,128)S(1)}, f32[2,1,128,64]{2,3,0,1:T(8,128)S(1)}, u32[]{:S(2)}, u32[]{:S(2)}) %collective-permute-start.2) | collective-permute-done | bytes 65568 | tf_op jit(solution)/shard_map/ppermute | solution.py:67
  22.3 0.0 collective-permute-done.1
  22.3 0.0 collective-permute-done
  22.4 0.6 gather_fusion
  22.9 0.1 broadcast_select_fusion.1
  23.1 0.2 copy.59
  23.2 0.8 reshape_reshape.9
  24.1 0.0 all-gather.2.cloned.1.call-update
  24.2 1.9 %collective-permute-start.4 = (f32[2,1,64,4,128]{4,2,0,3,1:T(8,128)S(1)}, f32[2,1,64,4,128]{4,2,0,3,1:T(8,128)S(1)}, u32[]{:S(2)}, u32[]{:S(2)}) collective-permute-start(f32[2,1,64,4,128]{4,2,0,3,1:T(8,128)S(1)} %get-tuple-element.6), channel_id=1, source_target_pairs={{0,1},{1,0},{2,3},{3,2},{4,5},{5,4},{6,7},{7,6},{8,9},{9,8},{10,11... | collective-permute-start | bytes 786440 | tf_op jit(solution)/shard_map/ppermute | solution.py:75
  26.1 0.3 copy.63
  26.4 0.1 bitcast_select_fusion.2
  26.5 7.5 %collective-permute-done.4 = f32[2,1,64,4,128]{4,2,0,3,1:T(8,128)S(1)} collective-permute-done((f32[2,1,64,4,128]{4,2,0,3,1:T(8,128)S(1)}, f32[2,1,64,4,128]{4,2,0,3,1:T(8,128)S(1)}, u32[]{:S(2)}, u32[]{:S(2)}) %collective-permute-start.4) | collective-permute-done | bytes 262176 | tf_op jit(solution)/shard_map/ppermute | solution.py:75
  34.1 0.6 gather_fusion.1
  34.7 0.1 fusion.8
  34.9 0.6 reshape.346
  35.5 0.7 broadcast_select_fusion
  36.2 0.0 copy-start.2
  36.2 0.0 copy-start.3
  36.2 0.3 copy.56
  36.5 1.6 %broadcast_in_dim.63 = f32[8,2,1,128,256]{3,4,1,2,0:T(8,128)} broadcast(f32[2,128,256]{1,2,0:T(8,128)S(1)} %bitcast.119), dimensions={1,3,4} | broadcast | bytes 2359296 | tf_op jit(solution)/shard_map/broadcast_in_dim | solution.py:10
  38.1 27.2 %all-to-all-start = ((f32[8,2,1,128,256]{3,4,1,2,0:T(8,128)}), f32[8,2,1,128,256]{3,4,1,2,0:T(8,128)S(1)}, u32[]{:S(2)}, u32[]{:S(2)}) async-start(f32[8,2,1,128,256]{3,4,1,2,0:T(8,128)} %broadcast_in_dim.63), calls=%async_computation | async-start | bytes 4194304 | tf_op jit(solution)/shard_map/all_to_all | solution.py:11
  65.3 0.8 copy.62
  66.1 0.1 gt.15
  66.2 0.1 broadcast_bitcast_fusion
  66.3 0.0 copy-done.2
  66.3 0.6 fusion.21
  66.9 0.0 copy-done.3
  66.9 0.1 convert_reduce_fusion
  67.0 0.3 copy.49
  67.3 0.5 reshape.344
  67.8 49.1 %all-to-all-done = f32[8,2,1,128,256]{3,4,1,2,0:T(8,128)S(1)} async-done(((f32[8,2,1,128,256]{3,4,1,2,0:T(8,128)}), f32[8,2,1,128,256]{3,4,1,2,0:T(8,128)S(1)}, u32[]{:S(2)}, u32[]{:S(2)}) %all-to-all-start) | async-done | bytes 2097184 | tf_op jit(solution)/shard_map/all_to_all | solution.py:11
  116.9 0.2 copy.57
  117.1 0.2 broadcast_multiply_fusion
  117.3 0.2 fusion.20
  117.5 1.6 %all-gather.2.cloned.1.call-done = f32[2,2048,512]{2,1,0:T(8,128)} async-done(((f32[2,64,512]{2,1,0:T(8,128)}), f32[2,2048,512]{2,1,0:T(8,128)}) %all-gather.2.cloned.1.call-update) | async-done | bytes 8388624 | tf_op jit(solution)/shard_map/all_gather | solution.py:97
  119.1 0.0 copy-start
  119.1 3.6 %fusion.1 = f32[128,512]{1,0:T(8,128)S(1)} fusion(f32[128,2048]{0,1:T(8,128)S(1)} %bitcast.110, f32[2,2048,512]{2,1,0:T(8,128)} %all-gather.2.cloned.1.call-done), kind=kOutput, calls=%fused_computation.5 | convolution fusion | flops 805306368 | bytes 5505024 | tf_op jit(solution)/shard_map/fik,fkj->fij/dot_general | solution.py:48
  122.8 3.5 %fusion = f32[128,512]{1,0:T(8,128)S(1)} fusion(f32[128,2048]{0,1:T(8,128)S(1)} %bitcast.112, f32[2,2048,512]{2,1,0:T(8,128)} %all-gather.2.cloned.1.call-done), kind=kOutput, calls=%fused_computation.4 | convolution fusion | flops 805306368 | bytes 5505024 | tf_op jit(solution)/shard_map/fik,fkj->fij/dot_general | solution.py:48
  126.3 0.0 copy-done
  126.3 1.5 %fusion.5 = f32[1,1,128,512]{3,2,1,0:T(8,128)S(1)} fusion(f32[128,512]{1,0:T(8,128)S(1)} %fusion.1, f32[128,2048]{0,1:T(8,128)S(1)} %bitcast.113, f32[2,2048,512]{2,1,0:T(8,128)S(1)} %copy-done), kind=kOutput, calls=%fused_computation.9 | convolution fusion | flops 805371904 | bytes 5767168 | tf_op jit(solution)/shard_map/fik,fkj->fij/dot_general | solution.py:48
  127.8 0.0 copy-start.1
  127.9 1.5 %fusion.7 = f32[1,1,128,512]{3,2,1,0:T(8,128)S(1)} fusion(f32[128,512]{1,0:T(8,128)S(1)} %fusion, f32[128,2048]{0,1:T(8,128)S(1)} %bitcast.111, f32[2,2048,512]{2,1,0:T(8,128)S(1)} %copy-done), kind=kOutput, calls=%fused_computation.11 | convolution fusion | flops 805371904 | bytes 5767168 | tf_op jit(solution)/shard_map/fik,fkj->fij/dot_general | solution.py:48
  129.4 4.3 %collective-permute-start.5 = (f32[2,1,128,256]{3,2,1,0:T(8,128)S(1)}, f32[2,1,128,256]{3,2,1,0:T(8,128)S(1)}, u32[]{:S(2)}, u32[]{:S(2)}) collective-permute-start(f32[2,1,128,256]{3,2,1,0:T(8,128)S(1)} %fusion.9), channel_id=1, source_target_pairs={{0,1},{1,0},{2,3},{3,2},{4,5},{5,4},{6,7},{7,6},{8,9},{9,8},{10,11... | collective-permute-start | bytes 786440 | tf_op jit(solution)/shard_map/ppermute | solution.py:106
  133.7 0.3 constant_dynamic-slice_fusion
  134.0 0.0 copy-done.1
  134.1 6.4 %collective-permute-done.5 = f32[2,1,128,256]{3,2,1,0:T(8,128)S(1)} collective-permute-done((f32[2,1,128,256]{3,2,1,0:T(8,128)S(1)}, f32[2,1,128,256]{3,2,1,0:T(8,128)S(1)}, u32[]{:S(2)}, u32[]{:S(2)}) %collective-permute-start.5) | collective-permute-done | bytes 262176 | tf_op jit(solution)/shard_map/ppermute | solution.py:106
  140.5 1.2 fusion.13
  141.7 0.7 pad_maximum_fusion
  (17 shorter events, 0.4 us)
Async XLA Ops:
  6.5 112.6 %all-gather.2.cloned.1.call-start = ((), (), s32[]{:S(2)}) async-start(), calls=%async_computation.1 | async-start | bytes 8650752 | tf_op jit(solution)/shard_map/all_gather | solution.py:97
  7.9 12.6 %collective-permute-start.3 = (f32[2,1,128,64]{2,3,0,1:T(8,128)S(1)}, f32[2,1,128,64]{2,3,0,1:T(8,128)S(1)}, u32[]{:S(2)}, u32[]{:S(2)}) collective-permute-start(f32[2,1,128,64]{2,3,0,1:T(8,128)S(1)} %get-tuple-element.12), channel_id=1, source_target_pairs={{16,0},{32,16},{48,32},{64,50},{80,2},{82,66},{96,18},{98,82},{112... | collective-permute-start | bytes 196616 | tf_op jit(solution)/shard_map/ppermute | solution.py:67
  16.7 5.7 %collective-permute-start.2 = (f32[2,1,128,64]{2,3,0,1:T(8,128)S(1)}, f32[2,1,128,64]{2,3,0,1:T(8,128)S(1)}, u32[]{:S(2)}, u32[]{:S(2)}) collective-permute-start(f32[2,1,128,64]{2,3,0,1:T(8,128)S(1)} %get-tuple-element.13), channel_id=1, source_target_pairs={{32,0},{48,16},{64,34},{80,50},{96,2},{98,66},{112,18},{114,82},{1... | collective-permute-start | bytes 196616 | tf_op jit(solution)/shard_map/ppermute | solution.py:67
  18.0 4.4 %collective-permute-start.1 = (f32[2,1,128,64]{2,3,0,1:T(8,128)S(1)}, f32[2,1,128,64]{2,3,0,1:T(8,128)S(1)}, u32[]{:S(2)}, u32[]{:S(2)}) collective-permute-start(f32[2,1,128,64]{2,3,0,1:T(8,128)S(1)} %get-tuple-element.14), channel_id=1, source_target_pairs={{48,0},{64,18},{80,34},{96,50},{112,2},{114,66},{128,20},{130,84},... | collective-permute-start | bytes 196616 | tf_op jit(solution)/shard_map/ppermute | solution.py:67
  18.6 3.7 %collective-permute-start = (f32[2,1,128,64]{2,3,0,1:T(8,128)S(1)}, f32[2,1,128,64]{2,3,0,1:T(8,128)S(1)}, u32[]{:S(2)}, u32[]{:S(2)}) collective-permute-start(f32[2,1,128,64]{2,3,0,1:T(8,128)S(1)} %get-tuple-element.11), channel_id=1, source_target_pairs={{64,2},{80,18},{96,34},{112,50},{128,4},{130,68},{144,20},{146,84}... | collective-permute-start | bytes 196616 | tf_op jit(solution)/shard_map/ppermute | solution.py:67
  24.2 9.9 %collective-permute-start.4 = (f32[2,1,64,4,128]{4,2,0,3,1:T(8,128)S(1)}, f32[2,1,64,4,128]{4,2,0,3,1:T(8,128)S(1)}, u32[]{:S(2)}, u32[]{:S(2)}) collective-permute-start(f32[2,1,64,4,128]{4,2,0,3,1:T(8,128)S(1)} %get-tuple-element.6), channel_id=1, source_target_pairs={{0,1},{1,0},{2,3},{3,2},{4,5},{5,4},{6,7},{7,6},{8,9},{9,8},{10,11... | collective-permute-start | bytes 786440 | tf_op jit(solution)/shard_map/ppermute | solution.py:75
  36.2 30.1 %copy-start.2 = (f32[2,1]{0,1:T(1,128)S(1)}, f32[2,1]{0,1:T(1,128)}, u32[]{:S(2)}) copy-start(f32[2,1]{0,1:T(1,128)} %param.7) | copy-start | bytes 28
  36.2 30.7 %copy-start.3 = (s32[1,24]{1,0:T(1,128)S(1)}, s32[1,24]{1,0:T(1,128)}, u32[]{:S(2)}) copy-start(s32[1,24]{1,0:T(1,128)} %param.6) | copy-start | bytes 292
  38.1 78.8 %all-to-all-start = ((f32[8,2,1,128,256]{3,4,1,2,0:T(8,128)}), f32[8,2,1,128,256]{3,4,1,2,0:T(8,128)S(1)}, u32[]{:S(2)}, u32[]{:S(2)}) async-start(f32[8,2,1,128,256]{3,4,1,2,0:T(8,128)} %broadcast_in_dim.63), calls=%async_computation | async-start | bytes 4194304 | tf_op jit(solution)/shard_map/all_to_all | solution.py:11
  119.1 7.1 %copy-start = (f32[2,2048,512]{2,1,0:T(8,128)S(1)}, f32[2,2048,512]{2,1,0:T(8,128)}, u32[]{:S(2)}) copy-start(f32[2,2048,512]{2,1,0:T(8,128)} %all-gather.2.cloned.1.call-done) | copy-start | bytes 25165828
  127.8 6.2 %copy-start.1 = (f32[2,1,128,1,256]{4,2,3,1,0:T(8,128)S(1)}, f32[2,1,128,1,256]{4,2,3,1,0:T(8,128)}, u32[]{:S(2)}) copy-start(f32[2,1,128,1,256]{4,2,3,1,0:T(8,128)} %copy.62) | copy-start | bytes 786436
  129.4 11.0 %collective-permute-start.5 = (f32[2,1,128,256]{3,2,1,0:T(8,128)S(1)}, f32[2,1,128,256]{3,2,1,0:T(8,128)S(1)}, u32[]{:S(2)}, u32[]{:S(2)}) collective-permute-start(f32[2,1,128,256]{3,2,1,0:T(8,128)S(1)} %fusion.9), channel_id=1, source_target_pairs={{0,1},{1,0},{2,3},{3,2},{4,5},{5,4},{6,7},{7,6},{8,9},{9,8},{10,11... | collective-permute-start | bytes 786440 | tf_op jit(solution)/shard_map/ppermute | solution.py:106
Sparse Core Ops, SparseCore 0:
  24.2 94.8 all-gather.1

commit v18 on v13

--- a/solution.py
+++ b/solution.py
@@ -93,7 +93,9 @@
     weighted = (weighted * chosen[None, None, :, None, :, None]).reshape(
         comp_count, freq_count, local_rows, block_count * half_tile
     )
-    slab_piece = lax.all_gather(right_half, "src", axis=2, tiled=True)
+    slab_piece = right_half.reshape(comp_count * freq_count, half_tile, local_cols)
+    slab_piece = lax.all_gather(slab_piece, "src", axis=1, tiled=True)
+    slab_piece = slab_piece.reshape(comp_count, freq_count, -1, local_cols)
     out_cols = local_cols // half_count
     assert half_count == 2
 

time: 154 us -> 149 us (0.968)
  local copies, waits for them, and re-layouts: 17.2 us -> 9.88 us
  matrix products: 9.73 us -> 13.8 us
  waiting for transfers between devices: 64.7 us -> 62 us
    slice x2 -> x1, local copies, waits for them, and re-layouts: 7.64 us -> 0.24 us  [half_product(): weighted[0]]
    dot_general x8, matrix products: 9.73 us -> 13.8 us  [complex_prod(): jnp.einsum('fik,fkj->fij', left_side, right_side, precision=lax.Precision...]
    ppermute x1, waiting for transfers between devices: 3.95 us -> 1.66 us  [per_device(): got = lax.ppermute(sent, 'int', [(0, 1), (1, 0)])]
  transfers between devices with their start and end apart: 8 -> 8, of which waited for: 5 -> 5; matrix products, arithmetic and copies ran while one was open for 7% -> 9% of each run, Pallas kernels for 0% -> 0%
where the time goes in v18:
time: 149 us
  waiting for transfers between devices  62 us (42%)
  starting transfers between devices  45.5 us (31%)
  matrix products  13.8 us (9%)
  between operations  13.8 us (9%)
  local copies, waits for them, and re-layouts  9.88 us (7%)
  other arithmetic  3.6 us (2%)
    all_to_all x1, waiting for transfers between devices, from_everyone(): return lax.all_to_all(copies, axis, split_axis=0, concat_axis=0, tiled=True)  48.7 us
    all_to_all x1, starting transfers between devices, from_everyone(): return lax.all_to_all(copies, axis, split_axis=0, concat_axis=0, tiled=True)  27.3 us
    dot_general x8, matrix products, complex_prod(): jnp.einsum('fik,fkj->fij', left_side, right_side, precision=lax.Precision...  13.8 us
    ppermute x4, starting transfers between devices, per_device(): lax.ppermute(sent, ('src', 'rcv'), mirror_pairs(src_count, rcv_count, per...  11.4 us
    ppermute x1, waiting for transfers between devices, per_device(): rows_other = lax.ppermute(rows_mine, 'int', [(0, 1), (1, 0)])  7.51 us
    ppermute x1, starting transfers between devices, per_device(): got = lax.ppermute(sent, 'int', [(0, 1), (1, 0)])  4.84 us
  transfers between devices with their start and end apart: 8, of which 5 were waited for; matrix products, arithmetic and copies ran while one was open for 9% of the time, Pallas kernels for 0%

profile of v18, /device:TPU:1, one launch (start us, length us, event | category | flops | bytes accessed | tf_op | source)
XLA Modules:
  0.0 148.6 jit_solution(7214257652002369837)
XLA Ops:
  6.5 0.0 copy-start.3
  6.5 0.0 all-gather.2.cloned.1.call-start
  6.5 1.2 copy.44
  7.9 8.8 %collective-permute-start.3 = (f32[2,1,128,64]{2,3,0,1:T(8,128)S(1)}, f32[2,1,128,64]{2,3,0,1:T(8,128)S(1)}, u32[]{:S(2)}, u32[]{:S(2)}) collective-permute-start(f32[2,1,128,64]{2,3,0,1:T(8,128)S(1)} %get-tuple-element.12), channel_id=1, source_target_pairs={{16,0},{32,16},{48,32},{64,50},{80,2},{82,66},{96,18},{98,82},{112... | collective-permute-start | bytes 196616 | tf_op jit(solution)/shard_map/ppermute | solution.py:67
  16.7 1.3 collective-permute-start.2
  18.0 0.7 collective-permute-start.1
  18.6 0.7 collective-permute-start
  19.3 0.2 constant_dynamic-slice_fusion.2
  19.5 0.2 copy.60
  19.7 0.0 copy-done.3
  19.8 0.0 collective-permute-done.3
  19.8 2.6 %collective-permute-done.2 = f32[2,1,128,64]{2,3,0,1:T(8,128)S(1)} collective-permute-done((f32[2,1,128,64]{2,3,0,1:T(8,128)S(1)}, f32[2,1,128,64]{2,3,0,1:T(8,128)S(1)}, u32[]{:S(2)}, u32[]{:S(2)}) %collective-permute-start.2) | collective-permute-done | bytes 65568 | tf_op jit(solution)/shard_map/ppermute | solution.py:67
  22.4 0.0 collective-permute-done.1
  22.4 0.0 collective-permute-done
  22.4 0.6 gather_fusion
  23.0 0.1 broadcast_select_fusion.1
  23.1 0.2 copy.59
  23.3 0.8 reshape_reshape.9
  24.1 0.0 all-gather.2.cloned.1.call-update
  24.2 1.9 %collective-permute-start.4 = (f32[2,1,64,4,128]{4,2,0,3,1:T(8,128)S(1)}, f32[2,1,64,4,128]{4,2,0,3,1:T(8,128)S(1)}, u32[]{:S(2)}, u32[]{:S(2)}) collective-permute-start(f32[2,1,64,4,128]{4,2,0,3,1:T(8,128)S(1)} %get-tuple-element.6), channel_id=1, source_target_pairs={{0,1},{1,0},{2,3},{3,2},{4,5},{5,4},{6,7},{7,6},{8,9},{9,8},{10,11... | collective-permute-start | bytes 786440 | tf_op jit(solution)/shard_map/ppermute | solution.py:75
  26.1 0.3 copy.63
  26.5 0.1 bitcast_select_fusion.2
  26.6 7.5 %collective-permute-done.4 = f32[2,1,64,4,128]{4,2,0,3,1:T(8,128)S(1)} collective-permute-done((f32[2,1,64,4,128]{4,2,0,3,1:T(8,128)S(1)}, f32[2,1,64,4,128]{4,2,0,3,1:T(8,128)S(1)}, u32[]{:S(2)}, u32[]{:S(2)}) %collective-permute-start.4) | collective-permute-done | bytes 262176 | tf_op jit(solution)/shard_map/ppermute | solution.py:75
  34.1 0.6 gather_fusion.1
  34.7 0.1 fusion.16
  34.9 0.6 reshape.376
  35.5 0.7 broadcast_select_fusion
  36.2 0.3 copy.56
  36.5 1.6 %broadcast_in_dim.63 = f32[8,2,1,128,256]{3,4,1,2,0:T(8,128)} broadcast(f32[2,128,256]{1,2,0:T(8,128)S(1)} %bitcast.147), dimensions={1,3,4} | broadcast | bytes 2359296 | tf_op jit(solution)/shard_map/broadcast_in_dim | solution.py:10
  38.1 0.0 copy-start.2
  38.1 0.0 copy-start.4
  38.1 27.3 %all-to-all-start = ((f32[8,2,1,128,256]{3,4,1,2,0:T(8,128)}), f32[8,2,1,128,256]{3,4,1,2,0:T(8,128)S(1)}, u32[]{:S(2)}, u32[]{:S(2)}) async-start(f32[8,2,1,128,256]{3,4,1,2,0:T(8,128)} %broadcast_in_dim.63), calls=%async_computation | async-start | bytes 4194304 | tf_op jit(solution)/shard_map/all_to_all | solution.py:11
  65.4 0.8 copy.62
  66.3 0.0 copy-start.1
  66.3 0.1 gt.15
  66.3 0.1 broadcast_bitcast_fusion
  66.4 0.0 copy-done.2
  66.4 0.6 fusion.34
  67.1 0.0 copy-done.4
  67.1 0.1 convert_reduce_fusion
  67.2 0.3 copy.49
  67.5 0.5 reshape.374
  68.0 0.3 constant_dynamic-slice_fusion
  68.3 0.0 copy-done.1
  68.3 48.7 %all-to-all-done = f32[8,2,1,128,256]{3,4,1,2,0:T(8,128)S(1)} async-done(((f32[8,2,1,128,256]{3,4,1,2,0:T(8,128)}), f32[8,2,1,128,256]{3,4,1,2,0:T(8,128)S(1)}, u32[]{:S(2)}, u32[]{:S(2)}) %all-to-all-start) | async-done | bytes 2097184 | tf_op jit(solution)/shard_map/all_to_all | solution.py:11
  117.1 0.2 copy.57
  117.2 0.2 broadcast_multiply_fusion
  117.4 0.2 fusion.33
  117.7 1.5 %all-gather.2.cloned.1.call-done = f32[2,2048,512]{2,1,0:T(8,128)} async-done(((f32[2,64,512]{2,1,0:T(8,128)}), f32[2,2048,512]{2,1,0:T(8,128)}) %all-gather.2.cloned.1.call-update) | async-done | bytes 8388624 | tf_op jit(solution)/shard_map/all_gather | solution.py:97
  119.2 0.0 copy-start
  119.2 2.7 %fusion.2 = f32[128,256]{1,0:T(8,128)S(1)} fusion(f32[128,2048]{0,1:T(8,128)S(1)} %bitcast.134, f32[2,2048,512]{2,1,0:T(8,128)} %all-gather.2.cloned.1.call-done, s32[]{:T(128)S(6)} %select_n.229), kind=kOutput, calls=%fused_computation.8 | convolution fusion | flops 402653184 | bytes 3276804 | tf_op jit(solution)/shard_map/fik,fkj->fij/dot_general | solution.py:48
  121.9 2.9 %fusion.3 = f32[128,256]{1,0:T(8,128)S(1)} fusion(f32[128,2048]{0,1:T(8,128)S(1)} %bitcast.138, f32[2,2048,512]{2,1,0:T(8,128)} %all-gather.2.cloned.1.call-done, s32[]{:T(128)S(6)} %select_n.229), kind=kOutput, calls=%fused_computation.9 | convolution fusion | flops 402653184 | bytes 3276804 | tf_op jit(solution)/shard_map/fik,fkj->fij/dot_general | solution.py:48
  124.8 2.6 %fusion.11 = f32[1,1,128,256]{3,2,1,0:T(8,128)S(1)} fusion(f32[128,256]{1,0:T(8,128)S(1)} %fusion.2, f32[128,2048]{0,1:T(8,128)S(1)} %bitcast.139, f32[2,2048,512]{2,1,0:T(8,128)} %all-gather.2.cloned.1.call-done, s32[]{:T(128)S(6)} %add.215, s32[]{:T(128)S(6)} %select_n.229), kind=kOutput, calls=%fused_computation.17 | convolution fusion | flops 402685952 | bytes 3407880 | tf_op jit(solution)/shard_map/fik,fkj->fij/dot_general | solution.py:48
  127.4 0.0 copy-done
  127.4 1.1 fusion.9
  128.6 4.8 %collective-permute-start.5 = (f32[2,1,128,256]{3,2,1,0:T(8,128)S(1)}, f32[2,1,128,256]{3,2,1,0:T(8,128)S(1)}, u32[]{:S(2)}, u32[]{:S(2)}) collective-permute-start(f32[2,1,128,256]{3,2,1,0:T(8,128)S(1)} %pad_maximum_fusion), channel_id=1, source_target_pairs={{0,1},{1,0},{2,3},{3,2},{4,5},{5,4},{6,7},{7,6},{8,9},{9,8},{10,11... | collective-permute-start | bytes 786440 | tf_op jit(solution)/shard_map/ppermute | solution.py:109
  133.4 1.1 fusion
  134.5 1.1 fusion.1
  135.7 1.1 fusion.15
  136.8 1.1 fusion.13
  138.0 1.7 %collective-permute-done.5 = f32[2,1,128,256]{3,2,1,0:T(8,128)S(1)} collective-permute-done((f32[2,1,128,256]{3,2,1,0:T(8,128)S(1)}, f32[2,1,128,256]{3,2,1,0:T(8,128)S(1)}, u32[]{:S(2)}, u32[]{:S(2)}) %collective-permute-start.5) | collective-permute-done | bytes 262176 | tf_op jit(solution)/shard_map/ppermute | solution.py:109
  139.7 1.3 fusion.18
  141.0 0.7 pad_maximum_fusion.1
  (18 shorter events, 0.4 us)
Async XLA Ops:
  6.5 13.2 %copy-start.3 = (s32[1,4]{1,0:T(1,128)S(1)}, s32[1,4]{1,0:T(1,128)}, u32[]{:S(2)}) copy-start(s32[1,4]{1,0:T(1,128)} %param.5) | copy-start | bytes 52
  6.5 112.6 %all-gather.2.cloned.1.call-start = ((), (), s32[]{:S(2)}) async-start(), calls=%async_computation.1 | async-start | bytes 8650752 | tf_op jit(solution)/shard_map/all_gather | solution.py:97
  7.9 11.9 %collective-permute-start.3 = (f32[2,1,128,64]{2,3,0,1:T(8,128)S(1)}, f32[2,1,128,64]{2,3,0,1:T(8,128)S(1)}, u32[]{:S(2)}, u32[]{:S(2)}) collective-permute-start(f32[2,1,128,64]{2,3,0,1:T(8,128)S(1)} %get-tuple-element.12), channel_id=1, source_target_pairs={{16,0},{32,16},{48,32},{64,50},{80,2},{82,66},{96,18},{98,82},{112... | collective-permute-start | bytes 196616 | tf_op jit(solution)/shard_map/ppermute | solution.py:67
  16.7 5.7 %collective-permute-start.2 = (f32[2,1,128,64]{2,3,0,1:T(8,128)S(1)}, f32[2,1,128,64]{2,3,0,1:T(8,128)S(1)}, u32[]{:S(2)}, u32[]{:S(2)}) collective-permute-start(f32[2,1,128,64]{2,3,0,1:T(8,128)S(1)} %get-tuple-element.13), channel_id=1, source_target_pairs={{32,0},{48,16},{64,34},{80,50},{96,2},{98,66},{112,18},{114,82},{1... | collective-permute-start | bytes 196616 | tf_op jit(solution)/shard_map/ppermute | solution.py:67
  18.0 4.4 %collective-permute-start.1 = (f32[2,1,128,64]{2,3,0,1:T(8,128)S(1)}, f32[2,1,128,64]{2,3,0,1:T(8,128)S(1)}, u32[]{:S(2)}, u32[]{:S(2)}) collective-permute-start(f32[2,1,128,64]{2,3,0,1:T(8,128)S(1)} %get-tuple-element.14), channel_id=1, source_target_pairs={{48,0},{64,18},{80,34},{96,50},{112,2},{114,66},{128,20},{130,84},... | collective-permute-start | bytes 196616 | tf_op jit(solution)/shard_map/ppermute | solution.py:67
  18.6 3.7 %collective-permute-start = (f32[2,1,128,64]{2,3,0,1:T(8,128)S(1)}, f32[2,1,128,64]{2,3,0,1:T(8,128)S(1)}, u32[]{:S(2)}, u32[]{:S(2)}) collective-permute-start(f32[2,1,128,64]{2,3,0,1:T(8,128)S(1)} %get-tuple-element.11), channel_id=1, source_target_pairs={{64,2},{80,18},{96,34},{112,50},{128,4},{130,68},{144,20},{146,84}... | collective-permute-start | bytes 196616 | tf_op jit(solution)/shard_map/ppermute | solution.py:67
  24.2 9.9 %collective-permute-start.4 = (f32[2,1,64,4,128]{4,2,0,3,1:T(8,128)S(1)}, f32[2,1,64,4,128]{4,2,0,3,1:T(8,128)S(1)}, u32[]{:S(2)}, u32[]{:S(2)}) collective-permute-start(f32[2,1,64,4,128]{4,2,0,3,1:T(8,128)S(1)} %get-tuple-element.6), channel_id=1, source_target_pairs={{0,1},{1,0},{2,3},{3,2},{4,5},{5,4},{6,7},{7,6},{8,9},{9,8},{10,11... | collective-permute-start | bytes 786440 | tf_op jit(solution)/shard_map/ppermute | solution.py:75
  38.1 28.3 %copy-start.2 = (f32[2,1]{0,1:T(1,128)S(1)}, f32[2,1]{0,1:T(1,128)}, u32[]{:S(2)}) copy-start(f32[2,1]{0,1:T(1,128)} %param.7) | copy-start | bytes 28
  38.1 29.0 %copy-start.4 = (s32[1,24]{1,0:T(1,128)S(1)}, s32[1,24]{1,0:T(1,128)}, u32[]{:S(2)}) copy-start(s32[1,24]{1,0:T(1,128)} %param.6) | copy-start | bytes 292
  38.1 79.0 %all-to-all-start = ((f32[8,2,1,128,256]{3,4,1,2,0:T(8,128)}), f32[8,2,1,128,256]{3,4,1,2,0:T(8,128)S(1)}, u32[]{:S(2)}, u32[]{:S(2)}) async-start(f32[8,2,1,128,256]{3,4,1,2,0:T(8,128)} %broadcast_in_dim.63), calls=%async_computation | async-start | bytes 4194304 | tf_op jit(solution)/shard_map/all_to_all | solution.py:11
  66.3 2.0 %copy-start.1 = (f32[2,1,128,1,256]{4,2,3,1,0:T(8,128)S(1)}, f32[2,1,128,1,256]{4,2,3,1,0:T(8,128)}, u32[]{:S(2)}) copy-start(f32[2,1,128,1,256]{4,2,3,1,0:T(8,128)} %copy.62) | copy-start | bytes 786436
  119.2 8.2 %copy-start = (f32[2,2048,512]{2,1,0:T(8,128)S(1)}, f32[2,2048,512]{2,1,0:T(8,128)}, u32[]{:S(2)}) copy-start(f32[2,2048,512]{2,1,0:T(8,128)} %all-gather.2.cloned.1.call-done) | copy-start | bytes 25165828
  128.6 11.0 %collective-permute-start.5 = (f32[2,1,128,256]{3,2,1,0:T(8,128)S(1)}, f32[2,1,128,256]{3,2,1,0:T(8,128)S(1)}, u32[]{:S(2)}, u32[]{:S(2)}) collective-permute-start(f32[2,1,128,256]{3,2,1,0:T(8,128)S(1)} %pad_maximum_fusion), channel_id=1, source_target_pairs={{0,1},{1,0},{2,3},{3,2},{4,5},{5,4},{6,7},{7,6},{8,9},{9,8},{10,11... | collective-permute-start | bytes 786440 | tf_op jit(solution)/shard_map/ppermute | solution.py:109
Sparse Core Ops, SparseCore 0:
  24.2 94.8 all-gather.1
